TPU v7x, 128 devices: a whole 4x4x4 slice. The times are simulated.
128 devices in a mesh: ep: 32 (over x, y, core), tp: 4 (over z).
Axes of the slice: x: 4, y: 4, z: 4, core: 2. Of those that a mesh axis runs over, the one named last changes fastest.
Arguments:
- query: bfloat16 [3, 1024, 8192], P(None, 'ep', 'tp'), may hold values from -110 to 110
- step_key_value: bfloat16 [3, 2, 1024, 512], P(None, None, 'ep', 'tp'), may hold values from -5 to 5
- key_value_cache: bfloat16 [2, 1024, 128, 512], P(None, 'ep', None, 'tp'), may hold values from -5 to 5
- lengths: int32 [1024], P('ep'), may hold values from 2 to 128, as said below
- hidden_in: bfloat16 [3, 1024, 4096], P(None, ('ep', 'tp')), may hold values from -3 to 3
- norm_gain: float32 [4096], replicated, may hold values from 0.5 to 1.5
- w_out: bfloat16 [8192, 4096], P('tp', 'ep'), may hold values from -0.1875 to 0.1875
- routes: int32 [3, 1024, 8], P(None, ('ep', 'tp')), may hold values from 0 to 127, all different within a row; in each aligned block of 8 rows (0 to 7, 8 to 15, ..., all dimensions but the last counted through in order) at most 2 rows name the same one
- gate_scores: float32 [3, 1024, 8], P(None, ('ep', 'tp')), may hold values from 0.1 to 1
- expert_gate: bfloat16 [128, 4096, 768], P(('ep', 'tp')), may hold values from -0.09375 to 0.09375
- expert_up: bfloat16 [128, 4096, 768], P(('ep', 'tp')), may hold values from -0.09375 to 0.09375
- expert_down: bfloat16 [128, 768, 4096], P(('ep', 'tp')), may hold values from -0.21875 to 0.21875
Outputs:
- layer_out: bfloat16 [3, 1024, 4096], P(None, ('ep', 'tp'))
Inputs may be any that keep to these rules, and one draw needn't show every extreme that they name: `lengths`: every row has at least two filled cache positions, and some row fills all 128. `routes`: A row names 8 different experts. Within one step, the 8 rows of one device (aligned blocks of rows) name any one expert at most 2 times.
All inputs are finite; a program needn't handle non-finite values.
Results may differ from a plain program's by a relative error of at most 0.007.
Values may be sent and summed in bfloat16 or wider, within the bound.
No kernel may reach another device: no remote copies, remote signals or barrier semaphores. Data moves between devices by JAX's collectives and lax.ppermute only.
A program may use at most 128 MiB of HBM per device.

v0:
```python
import jax
import jax.numpy as jnp
from jax import lax
from jax.sharding import PartitionSpec as P

HEAD_SIZE = 128
TOPK = 8
SLOTS = 256
DECODE_STEPS = 3


masked_score = -1e30
norm_eps = 1e-06


def per_device(
    query,
    step_key_value,
    key_value_cache,
    lengths,
    hidden_in,
    norm_gain,
    w_out,
    routes,
    gate_scores,
    expert_gate,
    expert_up,
    expert_down,
):
    ep_count = lax.axis_size("ep")
    tp_count = lax.axis_size("tp")
    steps = query.shape[0]
    row_dev = query.shape[1]
    row_own = hidden_in.shape[1]
    width = hidden_in.shape[2]
    heads_dev = query.shape[2] // HEAD_SIZE
    cache_len = key_value_cache.shape[2]
    expert_count = ep_count * tp_count * expert_gate.shape[0]
    capacity = SLOTS // expert_count
    score_scale = HEAD_SIZE ** (-0.5)
    stored_keys = key_value_cache[0]
    stored_values = key_value_cache[1]
    usable = jnp.arange(cache_len, dtype=jnp.int32)[None, :] < lengths[:, None]

    query_rows = query.reshape(steps, row_dev, heads_dev, HEAD_SIZE)
    incoming_keys = step_key_value[:, 0]
    incoming_values = step_key_value[:, 1]
    cache_scores = (
        jnp.einsum("srhd,rjd->srhj", query_rows, stored_keys, preferred_element_type=jnp.float32)
        * score_scale
    )
    cache_scores = jnp.where(usable[None, :, None, :], cache_scores, masked_score)
    fresh_scores = (
        jnp.einsum("srhd,jrd->srhj", query_rows, incoming_keys, preferred_element_type=jnp.float32)
        * score_scale
    )
    fresh_ok = (
        jnp.arange(steps, dtype=jnp.int32)[None, :] <= jnp.arange(steps, dtype=jnp.int32)[:, None]
    )
    fresh_scores = jnp.where(fresh_ok[:, None, None, :], fresh_scores, masked_score)
    scores = jnp.concatenate([cache_scores, fresh_scores], axis=-1)
    top = jnp.max(scores, axis=-1, keepdims=True)
    raised = jnp.exp(scores - top)
    probs = (raised / jnp.sum(raised, axis=-1, keepdims=True)).astype(jnp.bfloat16)
    attended = jnp.einsum(
        "srhj,rjd->srhd", probs[..., :cache_len], stored_values, preferred_element_type=jnp.float32
    )
    attended = attended + jnp.einsum(
        "srhj,jrd->srhd", probs[..., cache_len:], incoming_values, preferred_element_type=jnp.float32
    )
    attended = attended.astype(jnp.bfloat16).reshape(steps, row_dev, heads_dev * HEAD_SIZE)

    gathered = lax.all_gather(attended, "ep", axis=1, tiled=True)
    partial_sums = jnp.einsum(
        "srk,kc->src", gathered, w_out, preferred_element_type=jnp.float32
    )
    grouped = partial_sums.reshape(steps, ep_count * tp_count, row_own, -1)
    arrived_sums = lax.all_to_all(
        grouped, ("ep", "tp"), split_axis=1, concat_axis=1, tiled=True
    )
    arrived_sums = arrived_sums.reshape(steps, ep_count, tp_count, row_own, -1)
    summed = jnp.sum(arrived_sums, axis=2)
    projected = summed.astype(jnp.bfloat16)
    row_major = jnp.transpose(projected, (0, 2, 1, 3)).reshape(steps, row_own, width)

    residual = hidden_in.astype(jnp.float32) + row_major.astype(jnp.float32)
    mean_square = jnp.mean(residual * residual, axis=-1, keepdims=True)
    normed = (residual * lax.rsqrt(mean_square + norm_eps) * norm_gain).astype(jnp.bfloat16)
    weights = gate_scores / jnp.sum(gate_scores, axis=-1, keepdims=True)

    slots_per = steps * capacity
    expert_ids = routes.reshape(steps, -1)
    assigned = expert_ids.shape[1]
    matches = (
        expert_ids[:, :, None] == jnp.arange(expert_count, dtype=jnp.int32)[None, None, :]
    ).astype(jnp.int32)
    earlier = jnp.cumsum(matches, axis=1) - matches
    slot_rank = jnp.sum(earlier * matches, axis=2)
    step_ids = jnp.arange(steps, dtype=jnp.int32)[:, None]
    slot_index = (expert_ids * slots_per + step_ids * capacity + slot_rank).reshape(-1)
    slot_onehot = (
        slot_index[:, None] == jnp.arange(expert_count * slots_per, dtype=jnp.int32)[None, :]
    ).astype(jnp.bfloat16)
    row_ids = (step_ids * row_own + jnp.arange(assigned, dtype=jnp.int32)[None, :] // TOPK).reshape(-1)
    row_onehot = (
        row_ids[:, None] == jnp.arange(steps * row_own, dtype=jnp.int32)[None, :]
    ).astype(jnp.bfloat16)
    selector = jnp.einsum(
        "as,ar->sr", slot_onehot, row_onehot, preferred_element_type=jnp.float32
    ).astype(jnp.bfloat16)
    outgoing = jnp.dot(
        selector, normed.reshape(steps * row_own, width), preferred_element_type=jnp.float32
    ).astype(jnp.bfloat16)
    outgoing = outgoing.reshape(expert_count, slots_per, width)
    arrived = lax.all_to_all(outgoing, ("ep", "tp"), split_axis=0, concat_axis=0, tiled=True)
    flat_rows = arrived.reshape(-1, width)
    gate_act = jnp.dot(flat_rows, expert_gate[0], preferred_element_type=jnp.float32)
    up_act = jnp.dot(flat_rows, expert_up[0], preferred_element_type=jnp.float32)
    hidden = (jax.nn.silu(gate_act) * up_act).astype(jnp.bfloat16)
    expert_out = jnp.dot(hidden, expert_down[0], preferred_element_type=jnp.float32).astype(
        jnp.bfloat16
    )
    returned = lax.all_to_all(
        expert_out.reshape(arrived.shape), ("ep", "tp"), split_axis=0, concat_axis=0, tiled=True
    )
    returned = returned.reshape(expert_count * slots_per, width)
    selected = returned[slot_index].astype(jnp.float32) * weights.reshape(-1)[:, None]
    expert_mix = jnp.sum(selected.reshape(steps, row_own, TOPK, width), axis=2)
    return (residual + expert_mix).astype(jnp.bfloat16)


def solution(mesh):
    placed = (
        P(None, "ep", "tp"),
        P(None, None, "ep", "tp"),
        P(None, "ep", None, "tp"),
        P("ep"),
        P(None, ("ep", "tp"), None),
        P(),
        P("tp", "ep"),
        P(None, ("ep", "tp"), None),
        P(None, ("ep", "tp"), None),
        P(("ep", "tp"), None, None),
        P(("ep", "tp"), None, None),
        P(("ep", "tp"), None, None),
    )
    return jax.shard_map(
        per_device,
        mesh=mesh,
        in_specs=placed,
        out_specs=P(None, ("ep", "tp"), None),
        check_vma=False,
    )
```

profile of v0, /device:TPU:1, one launch (start us, length us, event | category | flops | bytes accessed | tf_op | source)
XLA Modules:
  0.0 419.5 jit_solution(10592854585237027797)
XLA Ops:
  6.5 0.8 iota_compare_fusion.7
  7.3 0.8 fusion.37
  8.1 1.1 copy.92
  9.2 0.8 fusion.22
  9.9 0.1 copy.76
  10.1 0.1 fusion.36
  10.2 0.1 copy.78
  10.3 0.4 copy.77
  10.7 2.1 fusion.38
  12.9 0.6 fusion.13
  13.5 0.5 divide_convert_fusion
  14.0 0.4 copy-done.4
  14.4 0.4 fusion.14
  14.9 0.2 fusion.12
  15.1 0.9 reshape.207
  16.1 66.5 %all-gather.2.cloned.1.call-done = bf16[3,1024,2048]{2,1,0:T(8,128)(2,1)} async-done(((bf16[3,32,2048]{2,1,0:T(8,128)(2,1)}), bf16[3,1024,2048]{2,1,0:T(8,128)(2,1)}) %all-gather.2.cloned.1.call-update) | async-done | bytes 12582928 | tf_op jit(solution)/shard_map/all_gather | solution.py:73
  82.6 6.4 %convolution_bitcast_fusion = f32[3,128,8,128]{3,2,1,0:T(8,128)S(1)} fusion(bf16[3,1024,2048]{2,1,0:T(8,128)(2,1)} %all-gather.2.cloned.1.call-done, bf16[2048,128]{1,0:T(8,128)(2,1)S(1)} %copy-done), kind=kOutput, calls=%fused_computation.15 | convolution fusion | flops 1610612736 | bytes 14680064 | tf_op jit(solution)/shard_map/srk,kc->src/dot_general | solution.py:74
  89.0 1.3 copy.82
  90.3 7.5 %all-to-all-start = ((f32[3,128,8,128]{3,2,0,1:T(8,128)}), f32[3,128,8,128]{3,2,0,1:T(8,128)S(1)}, u32[]{:S(2)}, u32[]{:S(2)}) async-start(f32[3,128,8,128]{3,2,0,1:T(8,128)} %copy.82), calls=%async_computation | async-start | bytes 3145728 | tf_op jit(solution)/shard_map/all_to_all | solution.py:78
  97.8 0.1 add.113
  98.0 0.1 add.107
  98.1 0.1 eq.20
  98.1 0.1 mul.102
  98.2 0.1 fusion.31
  98.3 0.1 reduce_window_sum.11
  98.5 0.2 select_reduce_fusion
  98.7 0.1 reduce_sum.61
  98.8 24.1 %all-to-all-done = f32[3,128,8,128]{3,2,0,1:T(8,128)S(1)} async-done(((f32[3,128,8,128]{3,2,0,1:T(8,128)}), f32[3,128,8,128]{3,2,0,1:T(8,128)S(1)}, u32[]{:S(2)}, u32[]{:S(2)}) %all-to-all-start) | async-done | bytes 1572896 | tf_op jit(solution)/shard_map/all_to_all | solution.py:78
  122.9 0.1 bitcast_reduce_fusion
  123.0 0.2 multiply_reduce_fusion
  123.1 4.2 %convolution_convert_fusion = bf16[768,4096]{1,0:T(8,128)(2,1)} fusion(s32[192]{0:T(256)S(1)} %add_add_fusion, f32[4096]{0:T(1024)S(1)} %copy-done.6, f32[3,8]{1,0:T(4,128)S(1)} %add_rsqrt_fusion, bf16[3,8,4096]{2,1,0:T(8,128)(2,1)S(1)} %copy-done.3, s32[192]{0:T(256)S(1)} %add.113, bf16[3,32,8,128]{3,2,0,1:T(8,128)(2,1)S(1)} %bitcast_reduce_fusion), kind=kOutput, calls=%fused_computation.1 | convolution fusion | flops 161978880 | bytes 6702688 | tf_op jit(solution)/shard_map/dot_general | solution.py:111
  127.4 10.1 %reshape.211 = bf16[128,6,4096]{2,1,0:T(8,128)(2,1)} reshape(bf16[768,4096]{1,0:T(8,128)(2,1)} %convolution_convert_fusion) | data formatting | bytes 12582912 | tf_op jit(solution)/shard_map/reshape | solution.py:114
  137.5 103.2 %all_to_all.15 = bf16[128,6,4096]{2,1,0:T(8,128)(2,1)} all-to-all(bf16[128,6,4096]{2,1,0:T(8,128)(2,1)} %reshape.211), channel_id=1, replica_groups=mesh['ep'=32,'tp'=4] {'ep','tp'}, dimensions={0} | all-to-all | bytes 12582912 | tf_op jit(solution)/shard_map/all_to_all | solution.py:115
  240.7 10.3 %reshape.212 = bf16[768,4096]{1,0:T(8,128)(2,1)} reshape(bf16[128,6,4096]{2,1,0:T(8,128)(2,1)} %all_to_all.15) | data formatting | bytes 12582912 | tf_op jit(solution)/shard_map/reshape | solution.py:116
  251.0 9.1 %fusion.3 = f32[768,768]{1,0:T(8,128)S(1)} fusion(bf16[768,4096]{1,0:T(8,128)(2,1)} %reshape.212, bf16[1,4096,768]{2,1,0:T(8,128)(2,1)} %param.21), kind=kOutput, calls=%fused_computation.6 | convolution fusion | flops 4831838208 | bytes 14942208 | tf_op jit(solution)/shard_map/dot_general | solution.py:117
  260.1 8.0 %multiply_convert_fusion = bf16[768,768]{1,0:T(8,128)(2,1)S(1)} fusion(f32[768,768]{1,0:T(8,128)S(1)} %fusion.3, bf16[768,4096]{1,0:T(8,128)(2,1)S(1)} %copy-done.2, bf16[1,4096,768]{2,1,0:T(8,128)(2,1)} %param.22), kind=kOutput, calls=%fused_computation.10 | convolution fusion | flops 4835377152 | bytes 16121856 | tf_op jit(solution)/shard_map/dot_general | solution.py:118
  268.1 9.8 %convolution_convert_fusion.1 = bf16[768,4096]{1,0:T(8,128)(2,1)} fusion(bf16[768,768]{1,0:T(8,128)(2,1)S(1)} %multiply_convert_fusion, bf16[1,768,4096]{2,1,0:T(8,128)(2,1)} %param.23), kind=kOutput, calls=%fused_computation.2 | convolution fusion | flops 4834983936 | bytes 13762560 | tf_op jit(solution)/shard_map/dot_general | solution.py:120
  277.9 10.1 %reshape.213 = bf16[128,6,4096]{2,1,0:T(8,128)(2,1)} reshape(bf16[768,4096]{1,0:T(8,128)(2,1)} %convolution_convert_fusion.1) | data formatting | bytes 12582912 | tf_op jit(solution)/shard_map/reshape | solution.py:124
  288.1 5.2 %all-to-all-start.2 = ((bf16[128,6,4096]{2,1,0:T(8,128)(2,1)}), bf16[128,6,4096]{2,1,0:T(8,128)(2,1)}, u32[]{:S(2)}, u32[]{:S(2)}) async-start(bf16[128,6,4096]{2,1,0:T(8,128)(2,1)} %reshape.213), calls=%async_computation.2 | async-start | bytes 16777216 | tf_op jit(solution)/shard_map/all_to_all | solution.py:123
  293.3 0.1 add.116
  293.4 0.1 mul.113
  293.4 0.1 reduce_sum.63
  293.6 0.3 fusion.35
  293.8 100.0 %all-to-all-done.2 = bf16[128,6,4096]{2,1,0:T(8,128)(2,1)} async-done(((bf16[128,6,4096]{2,1,0:T(8,128)(2,1)}), bf16[128,6,4096]{2,1,0:T(8,128)(2,1)}, u32[]{:S(2)}, u32[]{:S(2)}) %all-to-all-start.2) | async-done | bytes 6291488 | tf_op jit(solution)/shard_map/all_to_all | solution.py:123
  393.8 10.2 %reshape.214 = bf16[768,4096]{1,0:T(8,128)(2,1)} reshape(bf16[128,6,4096]{2,1,0:T(8,128)(2,1)} %all-to-all-done.2) | data formatting | bytes 12582912 | tf_op jit(solution)/shard_map/reshape | solution.py:126
  404.0 6.7 %gather_fusion = bf16[192,4096]{1,0:T(8,128)(2,1)S(1)} fusion(bf16[768,4096]{1,0:T(8,128)(2,1)} %reshape.214, s32[1024]{0:T(1024)S(1)} %pad_clamp_fusion), kind=kCustom, calls=%fused_computation | custom fusion | bytes 3146496 | tf_op jit(solution)/shard_map/gather | solution.py:127
  410.7 1.2 fusion.5
  411.9 0.8 add_convert_fusion
  (30 shorter events, 0.3 us)
Async XLA Ops:
  6.5 76.0 %copy-start = (bf16[2048,128]{1,0:T(8,128)(2,1)S(1)}, bf16[2048,128]{1,0:T(8,128)(2,1)}, u32[]{:S(2)}) copy-start(bf16[2048,128]{1,0:T(8,128)(2,1)} %param.18) | copy-start | bytes 1572868
  6.5 76.0 %all-gather.2.cloned.1.call-start = ((), (), s32[]{:S(2)}) async-start(), calls=%async_computation.3 | async-start | bytes 12976128 | tf_op jit(solution)/shard_map/all_gather | solution.py:73
  12.8 1.6 copy-start.4
  90.3 7.8 %copy-start.5 = (s32[3,8,8]{2,1,0:T(8,128)S(1)}, s32[3,8,8]{2,1,0:T(8,128)}, u32[]{:S(2)}) copy-start(s32[3,8,8]{2,1,0:T(8,128)} %param.19) | copy-start | bytes 2308
  90.3 32.7 %copy-start.3 = (bf16[3,8,4096]{2,1,0:T(8,128)(2,1)S(1)}, bf16[3,8,4096]{2,1,0:T(8,128)(2,1)}, u32[]{:S(2)}) copy-start(bf16[3,8,4096]{2,1,0:T(8,128)(2,1)} %param.16) | copy-start | bytes 589828
  90.3 32.9 %copy-start.6 = (f32[4096]{0:T(1024)S(1)}, f32[4096]{0:T(1024)}, u32[]{:S(2)}) copy-start(f32[4096]{0:T(1024)} %param.17) | copy-start | bytes 49156
  90.3 32.6 %all-to-all-start = ((f32[3,128,8,128]{3,2,0,1:T(8,128)}), f32[3,128,8,128]{3,2,0,1:T(8,128)S(1)}, u32[]{:S(2)}, u32[]{:S(2)}) async-start(f32[3,128,8,128]{3,2,0,1:T(8,128)} %copy.82), calls=%async_computation | async-start | bytes 3145728 | tf_op jit(solution)/shard_map/all_to_all | solution.py:78
  251.0 9.1 %copy-start.2 = (bf16[768,4096]{1,0:T(8,128)(2,1)S(1)}, bf16[768,4096]{1,0:T(8,128)(2,1)}, u32[]{:S(2)}) copy-start(bf16[768,4096]{1,0:T(8,128)(2,1)} %reshape.212) | copy-start | bytes 18874372
  288.1 5.5 %copy-start.7 = (f32[3,8,8]{2,1,0:T(8,128)S(1)}, f32[3,8,8]{2,1,0:T(8,128)}, u32[]{:S(2)}) copy-start(f32[3,8,8]{2,1,0:T(8,128)} %param.20) | copy-start | bytes 2308
  288.1 105.7 %all-to-all-start.2 = ((bf16[128,6,4096]{2,1,0:T(8,128)(2,1)}), bf16[128,6,4096]{2,1,0:T(8,128)(2,1)}, u32[]{:S(2)}, u32[]{:S(2)}) async-start(bf16[128,6,4096]{2,1,0:T(8,128)(2,1)} %reshape.213), calls=%async_computation.2 | async-start | bytes 16777216 | tf_op jit(solution)/shard_map/all_to_all | solution.py:123
  404.0 8.7 %copy-start.1 = (bf16[2048,128]{1,0:T(8,128)(2,1)S(1)}, bf16[2048,128]{1,0:T(8,128)(2,1)}, u32[]{:S(2)}) copy-start(bf16[2048,128]{1,0:T(8,128)(2,1)} %param.18) | copy-start | bytes 1572868
Sparse Core Ops, SparseCore 0:
  16.2 66.2 all-gather.1
where the time goes:
time: 428 us; the launch traced here: 420 us
  waiting for transfers between devices  191 us (45%)
  blocking collectives  103 us (24%)
  local copies, waits for them, and re-layouts  53.3 us (12%)
  matrix products  41.2 us (10%)
  between operations  13.6 us (3%)
  starting transfers between devices  12.7 us (3%)
  other arithmetic  5.08 us (1%)
    all_to_all x1, blocking collectives, per_device(): lax.all_to_all(outgoing, ('ep', 'tp'), split_axis=0, concat_axis=0, tiled...  103 us
    all_to_all x1, waiting for transfers between devices, per_device(): lax.all_to_all(expert_out.reshape(arrived.shape), ('ep', 'tp'), split_axi...  100 us
    all_gather x1, waiting for transfers between devices, per_device(): gathered = lax.all_gather(attended, 'ep', axis=1, tiled=True)  66.5 us
    all_to_all x1, waiting for transfers between devices, per_device(): lax.all_to_all(grouped, ('ep', 'tp'), split_axis=1, concat_axis=1, tiled=...  24.1 us
    reshape x1, local copies, waits for them, and re-layouts, per_device(): flat_rows = arrived.reshape(-1, width)  10.3 us
    reshape x1, local copies, waits for them, and re-layouts, per_device(): returned = returned.reshape(expert_count * slots_per, width)  10.2 us
    reshape x1, local copies, waits for them, and re-layouts, per_device(): outgoing = outgoing.reshape(expert_count, slots_per, width)  10.1 us
    reshape x1, local copies, waits for them, and re-layouts, per_device(): expert_out.reshape(arrived.shape)  10.1 us
  transfers between devices with their start and end apart: 3, of which 3 were waited for; matrix products, arithmetic and copies ran while one was open for 0% of the time, Pallas kernels for 0%

commit v1 on v0

--- a/solution.py
+++ b/solution.py
@@ -111,7 +111,8 @@
     outgoing = jnp.dot(
         selector, normed.reshape(steps * row_own, width), preferred_element_type=jnp.float32
     ).astype(jnp.bfloat16)
-    outgoing = outgoing.reshape(expert_count, slots_per, width)
+    wire_shape = (expert_count, slots_per * width // 128, 128)
+    outgoing = outgoing.reshape(wire_shape)
     arrived = lax.all_to_all(outgoing, ("ep", "tp"), split_axis=0, concat_axis=0, tiled=True)
     flat_rows = arrived.reshape(-1, width)
     gate_act = jnp.dot(flat_rows, expert_gate[0], preferred_element_type=jnp.float32)
@@ -121,7 +122,7 @@
         jnp.bfloat16
     )
     returned = lax.all_to_all(
-        expert_out.reshape(arrived.shape), ("ep", "tp"), split_axis=0, concat_axis=0, tiled=True
+        expert_out.reshape(wire_shape), ("ep", "tp"), split_axis=0, concat_axis=0, tiled=True
     )
     returned = returned.reshape(expert_count * slots_per, width)
     selected = returned[slot_index].astype(jnp.float32) * weights.reshape(-1)[:, None]

time: 428 us -> 379 us (0.89)
  waiting for transfers between devices: 191 us -> 166 us
  blocking collectives: 103 us -> 80.7 us
    all_to_all x1, waiting for transfers between devices: 100 us -> 75.9 us  [per_device(): lax.all_to_all(expert_out.reshape(wire_shape), ('ep', 'tp'), split_axis=0...]
    all_to_all x1, blocking collectives: 103 us -> 80.7 us  [per_device(): lax.all_to_all(outgoing, ('ep', 'tp'), split_axis=0, concat_axis=0, tiled...]
where the time goes in v1:
time: 379 us; the launch traced here: 374 us
  waiting for transfers between devices  166 us (44%)
  blocking collectives  80.7 us (21%)
  local copies, waits for them, and re-layouts  54.2 us (14%)
  matrix products  41.3 us (11%)
  between operations  13.6 us (4%)
  starting transfers between devices  12.6 us (3%)
  other arithmetic  5.02 us (1%)
    all_to_all x1, blocking collectives, per_device(): lax.all_to_all(outgoing, ('ep', 'tp'), split_axis=0, concat_axis=0, tiled...  80.7 us
    all_to_all x1, waiting for transfers between devices, per_device(): lax.all_to_all(expert_out.reshape(wire_shape), ('ep', 'tp'), split_axis=0...  75.9 us
    all_gather x1, waiting for transfers between devices, per_device(): gathered = lax.all_gather(attended, 'ep', axis=1, tiled=True)  66.5 us
    all_to_all x1, waiting for transfers between devices, per_device(): lax.all_to_all(grouped, ('ep', 'tp'), split_axis=1, concat_axis=1, tiled=...  24.1 us
    reshape x1, local copies, waits for them, and re-layouts, per_device(): expert_out.reshape(wire_shape)  10.5 us
    reshape x1, local copies, waits for them, and re-layouts, per_device(): outgoing = outgoing.reshape(wire_shape)  10.4 us
    reshape x1, local copies, waits for them, and re-layouts, per_device(): returned = returned.reshape(expert_count * slots_per, width)  10.3 us
    reshape x1, local copies, waits for them, and re-layouts, per_device(): flat_rows = arrived.reshape(-1, width)  10.3 us
  transfers between devices with their start and end apart: 3, of which 3 were waited for; matrix products, arithmetic and copies ran while one was open for 0% of the time, Pallas kernels for 0%

profile of v1, /device:TPU:1, one launch (start us, length us, event | category | flops | bytes accessed | tf_op | source)
XLA Modules:
  0.0 373.8 jit_solution(6783589383899165512)
XLA Ops:
  6.5 1.1 copy.92
  7.7 0.8 fusion.37
  8.4 0.8 fusion.22
  9.2 0.1 copy.76
  9.3 0.1 fusion.36
  9.4 0.1 copy.78
  9.5 0.7 iota_compare_fusion.7
  10.3 0.4 copy.77
  10.7 2.1 fusion.38
  12.9 0.6 fusion.13
  13.5 0.5 divide_convert_fusion
  14.0 0.4 copy-done.4
  14.5 0.4 fusion.14
  14.9 0.2 fusion.12
  15.1 0.9 reshape.207
  16.1 66.5 %all-gather.2.cloned.1.call-done = bf16[3,1024,2048]{2,1,0:T(8,128)(2,1)} async-done(((bf16[3,32,2048]{2,1,0:T(8,128)(2,1)}), bf16[3,1024,2048]{2,1,0:T(8,128)(2,1)}) %all-gather.2.cloned.1.call-update) | async-done | bytes 12582928 | tf_op jit(solution)/shard_map/all_gather | solution.py:73
  82.6 6.4 %convolution_bitcast_fusion = f32[3,128,8,128]{3,2,1,0:T(8,128)S(1)} fusion(bf16[3,1024,2048]{2,1,0:T(8,128)(2,1)} %all-gather.2.cloned.1.call-done, bf16[2048,128]{1,0:T(8,128)(2,1)S(1)} %copy-done), kind=kOutput, calls=%fused_computation.15 | convolution fusion | flops 1610612736 | bytes 14680064 | tf_op jit(solution)/shard_map/srk,kc->src/dot_general | solution.py:74
  89.0 1.3 copy.82
  90.3 7.5 %all-to-all-start = ((f32[3,128,8,128]{3,2,0,1:T(8,128)}), f32[3,128,8,128]{3,2,0,1:T(8,128)S(1)}, u32[]{:S(2)}, u32[]{:S(2)}) async-start(f32[3,128,8,128]{3,2,0,1:T(8,128)} %copy.82), calls=%async_computation | async-start | bytes 3145728 | tf_op jit(solution)/shard_map/all_to_all | solution.py:78
  97.7 0.1 eq.20
  97.8 0.1 fusion.31
  97.9 0.1 reduce_window_sum.11
  98.0 0.2 select_reduce_fusion
  98.3 0.1 reduce_sum.61
  98.4 0.1 mul.102
  98.5 0.1 add.107
  98.7 0.1 add.113
  98.8 24.1 %all-to-all-done = f32[3,128,8,128]{3,2,0,1:T(8,128)S(1)} async-done(((f32[3,128,8,128]{3,2,0,1:T(8,128)}), f32[3,128,8,128]{3,2,0,1:T(8,128)S(1)}, u32[]{:S(2)}, u32[]{:S(2)}) %all-to-all-start) | async-done | bytes 1572896 | tf_op jit(solution)/shard_map/all_to_all | solution.py:78
  122.9 0.1 bitcast_reduce_fusion
  123.0 0.2 multiply_reduce_fusion
  123.2 4.4 %convolution_convert_fusion = bf16[768,4096]{1,0:T(8,128)(2,1)} fusion(s32[192]{0:T(256)S(1)} %add_add_fusion, f32[4096]{0:T(1024)S(1)} %copy-done.6, f32[3,8]{1,0:T(4,128)S(1)} %add_rsqrt_fusion, bf16[3,8,4096]{2,1,0:T(8,128)(2,1)S(1)} %copy-done.3, s32[192]{0:T(256)S(1)} %add.113, bf16[3,32,8,128]{3,2,0,1:T(8,128)(2,1)S(1)} %bitcast_reduce_fusion), kind=kOutput, calls=%fused_computation.1 | convolution fusion | flops 161978880 | bytes 6702688 | tf_op jit(solution)/shard_map/dot_general | solution.py:111
  127.5 10.4 %reshape.211 = bf16[128,192,128]{2,1,0:T(8,128)(2,1)} reshape(bf16[768,4096]{1,0:T(8,128)(2,1)} %convolution_convert_fusion) | data formatting | bytes 12582912 | tf_op jit(solution)/shard_map/reshape | solution.py:115
  138.0 80.7 %all_to_all.15 = bf16[128,192,128]{2,1,0:T(8,128)(2,1)} all-to-all(bf16[128,192,128]{2,1,0:T(8,128)(2,1)} %reshape.211), channel_id=1, replica_groups=mesh['ep'=32,'tp'=4] {'ep','tp'}, dimensions={0} | all-to-all | bytes 12582912 | tf_op jit(solution)/shard_map/all_to_all | solution.py:116
  218.6 10.3 %reshape.212 = bf16[768,4096]{1,0:T(8,128)(2,1)} reshape(bf16[128,192,128]{2,1,0:T(8,128)(2,1)} %all_to_all.15) | data formatting | bytes 12582912 | tf_op jit(solution)/shard_map/reshape | solution.py:117
  228.9 9.1 %fusion.3 = f32[768,768]{1,0:T(8,128)S(1)} fusion(bf16[768,4096]{1,0:T(8,128)(2,1)} %reshape.212, bf16[1,4096,768]{2,1,0:T(8,128)(2,1)} %param.21), kind=kOutput, calls=%fused_computation.6 | convolution fusion | flops 4831838208 | bytes 14942208 | tf_op jit(solution)/shard_map/dot_general | solution.py:118
  238.0 8.0 %multiply_convert_fusion = bf16[768,768]{1,0:T(8,128)(2,1)S(1)} fusion(f32[768,768]{1,0:T(8,128)S(1)} %fusion.3, bf16[768,4096]{1,0:T(8,128)(2,1)S(1)} %copy-done.2, bf16[1,4096,768]{2,1,0:T(8,128)(2,1)} %param.22), kind=kOutput, calls=%fused_computation.10 | convolution fusion | flops 4835377152 | bytes 16121856 | tf_op jit(solution)/shard_map/dot_general | solution.py:119
  246.1 9.8 %convolution_convert_fusion.1 = bf16[768,4096]{1,0:T(8,128)(2,1)} fusion(bf16[768,768]{1,0:T(8,128)(2,1)S(1)} %multiply_convert_fusion, bf16[1,768,4096]{2,1,0:T(8,128)(2,1)} %param.23), kind=kOutput, calls=%fused_computation.2 | convolution fusion | flops 4834983936 | bytes 13762560 | tf_op jit(solution)/shard_map/dot_general | solution.py:121
  255.9 10.5 %reshape.213 = bf16[128,192,128]{2,1,0:T(8,128)(2,1)} reshape(bf16[768,4096]{1,0:T(8,128)(2,1)} %convolution_convert_fusion.1) | data formatting | bytes 12582912 | tf_op jit(solution)/shard_map/reshape | solution.py:125
  266.4 5.1 %all-to-all-start.2 = ((bf16[128,192,128]{2,1,0:T(8,128)(2,1)}), bf16[128,192,128]{2,1,0:T(8,128)(2,1)}, u32[]{:S(2)}, u32[]{:S(2)}) async-start(bf16[128,192,128]{2,1,0:T(8,128)(2,1)} %reshape.213), calls=%async_computation.2 | async-start | bytes 12582912 | tf_op jit(solution)/shard_map/all_to_all | solution.py:124
  271.5 0.1 reduce_sum.63
  271.6 0.1 mul.113
  271.6 0.1 add.116
  271.7 0.3 fusion.35
  272.0 75.9 %all-to-all-done.2 = bf16[128,192,128]{2,1,0:T(8,128)(2,1)} async-done(((bf16[128,192,128]{2,1,0:T(8,128)(2,1)}), bf16[128,192,128]{2,1,0:T(8,128)(2,1)}, u32[]{:S(2)}, u32[]{:S(2)}) %all-to-all-start.2) | async-done | bytes 6291488 | tf_op jit(solution)/shard_map/all_to_all | solution.py:124
  347.9 10.3 %reshape.214 = bf16[768,4096]{1,0:T(8,128)(2,1)} reshape(bf16[128,192,128]{2,1,0:T(8,128)(2,1)} %all-to-all-done.2) | data formatting | bytes 12582912 | tf_op jit(solution)/shard_map/reshape | solution.py:127
  358.3 6.7 %gather_fusion = bf16[192,4096]{1,0:T(8,128)(2,1)S(1)} fusion(bf16[768,4096]{1,0:T(8,128)(2,1)} %reshape.214, s32[1024]{0:T(1024)S(1)} %pad_clamp_fusion), kind=kCustom, calls=%fused_computation | custom fusion | bytes 3146496 | tf_op jit(solution)/shard_map/gather | solution.py:128
  365.0 1.2 fusion.5
  366.2 0.8 add_convert_fusion
  (30 shorter events, 0.3 us)
Async XLA Ops:
  6.5 76.0 %copy-start = (bf16[2048,128]{1,0:T(8,128)(2,1)S(1)}, bf16[2048,128]{1,0:T(8,128)(2,1)}, u32[]{:S(2)}) copy-start(bf16[2048,128]{1,0:T(8,128)(2,1)} %param.18) | copy-start | bytes 1572868
  6.5 76.0 %all-gather.2.cloned.1.call-start = ((), (), s32[]{:S(2)}) async-start(), calls=%async_computation.3 | async-start | bytes 12976128 | tf_op jit(solution)/shard_map/all_gather | solution.py:73
  12.9 1.6 copy-start.4
  90.3 7.5 %copy-start.5 = (s32[3,8,8]{2,1,0:T(8,128)S(1)}, s32[3,8,8]{2,1,0:T(8,128)}, u32[]{:S(2)}) copy-start(s32[3,8,8]{2,1,0:T(8,128)} %param.19) | copy-start | bytes 2308
  90.3 32.7 %copy-start.3 = (bf16[3,8,4096]{2,1,0:T(8,128)(2,1)S(1)}, bf16[3,8,4096]{2,1,0:T(8,128)(2,1)}, u32[]{:S(2)}) copy-start(bf16[3,8,4096]{2,1,0:T(8,128)(2,1)} %param.16) | copy-start | bytes 589828
  90.3 32.9 %copy-start.6 = (f32[4096]{0:T(1024)S(1)}, f32[4096]{0:T(1024)}, u32[]{:S(2)}) copy-start(f32[4096]{0:T(1024)} %param.17) | copy-start | bytes 49156
  90.3 32.6 %all-to-all-start = ((f32[3,128,8,128]{3,2,0,1:T(8,128)}), f32[3,128,8,128]{3,2,0,1:T(8,128)S(1)}, u32[]{:S(2)}, u32[]{:S(2)}) async-start(f32[3,128,8,128]{3,2,0,1:T(8,128)} %copy.82), calls=%async_computation | async-start | bytes 3145728 | tf_op jit(solution)/shard_map/all_to_all | solution.py:78
  228.9 9.1 %copy-start.2 = (bf16[768,4096]{1,0:T(8,128)(2,1)S(1)}, bf16[768,4096]{1,0:T(8,128)(2,1)}, u32[]{:S(2)}) copy-start(bf16[768,4096]{1,0:T(8,128)(2,1)} %reshape.212) | copy-start | bytes 18874372
  266.4 5.4 %copy-start.7 = (f32[3,8,8]{2,1,0:T(8,128)S(1)}, f32[3,8,8]{2,1,0:T(8,128)}, u32[]{:S(2)}) copy-start(f32[3,8,8]{2,1,0:T(8,128)} %param.20) | copy-start | bytes 2308
  266.4 81.6 %all-to-all-start.2 = ((bf16[128,192,128]{2,1,0:T(8,128)(2,1)}), bf16[128,192,128]{2,1,0:T(8,128)(2,1)}, u32[]{:S(2)}, u32[]{:S(2)}) async-start(bf16[128,192,128]{2,1,0:T(8,128)(2,1)} %reshape.213), calls=%async_computation.2 | async-start | bytes 12582912 | tf_op jit(solution)/shard_map/all_to_all | solution.py:124
  358.3 8.7 %copy-start.1 = (bf16[2048,128]{1,0:T(8,128)(2,1)S(1)}, bf16[2048,128]{1,0:T(8,128)(2,1)}, u32[]{:S(2)}) copy-start(bf16[2048,128]{1,0:T(8,128)(2,1)} %param.18) | copy-start | bytes 1572868
Sparse Core Ops, SparseCore 0:
  16.2 66.2 all-gather.1

commit v2 on v1

--- a/solution.py
+++ b/solution.py
@@ -1,7 +1,7 @@
 import jax
 import jax.numpy as jnp
 from jax import lax
-from jax.sharding import PartitionSpec as P
+from jax.sharding import Mesh, PartitionSpec as P
 
 HEAD_SIZE = 128
 TOPK = 8
@@ -27,7 +27,9 @@
     expert_up,
     expert_down,
 ):
-    ep_count = lax.axis_size("ep")
+    chip_count = lax.axis_size("eh")
+    core_count = lax.axis_size("ec")
+    ep_count = chip_count * core_count
     tp_count = lax.axis_size("tp")
     steps = query.shape[0]
     row_dev = query.shape[1]
@@ -70,15 +72,16 @@
     )
     attended = attended.astype(jnp.bfloat16).reshape(steps, row_dev, heads_dev * HEAD_SIZE)
 
-    gathered = lax.all_gather(attended, "ep", axis=1, tiled=True)
+    w_pair = lax.all_gather(w_out, "ec", axis=1, tiled=True)
+    gathered = lax.all_gather(attended, "eh", axis=1, tiled=True)
     partial_sums = jnp.einsum(
-        "srk,kc->src", gathered, w_out, preferred_element_type=jnp.float32
+        "srk,kc->src", gathered, w_pair, preferred_element_type=jnp.float32
     )
-    grouped = partial_sums.reshape(steps, ep_count * tp_count, row_own, -1)
+    grouped = partial_sums.reshape(steps, chip_count * tp_count, row_own, -1)
     arrived_sums = lax.all_to_all(
-        grouped, ("ep", "tp"), split_axis=1, concat_axis=1, tiled=True
+        grouped, ("eh", "tp"), split_axis=1, concat_axis=1, tiled=True
     )
-    arrived_sums = arrived_sums.reshape(steps, ep_count, tp_count, row_own, -1)
+    arrived_sums = arrived_sums.reshape(steps, chip_count, tp_count, row_own, -1)
     summed = jnp.sum(arrived_sums, axis=2)
     projected = summed.astype(jnp.bfloat16)
     row_major = jnp.transpose(projected, (0, 2, 1, 3)).reshape(steps, row_own, width)
@@ -113,7 +116,7 @@
     ).astype(jnp.bfloat16)
     wire_shape = (expert_count, slots_per * width // 128, 128)
     outgoing = outgoing.reshape(wire_shape)
-    arrived = lax.all_to_all(outgoing, ("ep", "tp"), split_axis=0, concat_axis=0, tiled=True)
+    arrived = lax.all_to_all(outgoing, ("eh", "ec", "tp"), split_axis=0, concat_axis=0, tiled=True)
     flat_rows = arrived.reshape(-1, width)
     gate_act = jnp.dot(flat_rows, expert_gate[0], preferred_element_type=jnp.float32)
     up_act = jnp.dot(flat_rows, expert_up[0], preferred_element_type=jnp.float32)
@@ -122,7 +125,7 @@
         jnp.bfloat16
     )
     returned = lax.all_to_all(
-        expert_out.reshape(wire_shape), ("ep", "tp"), split_axis=0, concat_axis=0, tiled=True
+        expert_out.reshape(wire_shape), ("eh", "ec", "tp"), split_axis=0, concat_axis=0, tiled=True
     )
     returned = returned.reshape(expert_count * slots_per, width)
     selected = returned[slot_index].astype(jnp.float32) * weights.reshape(-1)[:, None]
@@ -131,24 +134,29 @@
 
 
 def solution(mesh):
+    chips = mesh.devices.shape[0] // 2
+    split_mesh = Mesh(
+        mesh.devices.reshape(chips, 2, mesh.devices.shape[1]), ("eh", "ec", "tp")
+    )
+    ep = ("eh", "ec")
     placed = (
-        P(None, "ep", "tp"),
-        P(None, None, "ep", "tp"),
-        P(None, "ep", None, "tp"),
-        P("ep"),
-        P(None, ("ep", "tp"), None),
+        P(None, ep, "tp"),
+        P(None, None, ep, "tp"),
+        P(None, ep, None, "tp"),
+        P(ep),
+        P(None, (*ep, "tp"), None),
         P(),
-        P("tp", "ep"),
-        P(None, ("ep", "tp"), None),
-        P(None, ("ep", "tp"), None),
-        P(("ep", "tp"), None, None),
-        P(("ep", "tp"), None, None),
-        P(("ep", "tp"), None, None),
+        P("tp", ep),
+        P(None, (*ep, "tp"), None),
+        P(None, (*ep, "tp"), None),
+        P((*ep, "tp"), None, None),
+        P((*ep, "tp"), None, None),
+        P((*ep, "tp"), None, None),
     )
     return jax.shard_map(
         per_device,
-        mesh=mesh,
+        mesh=split_mesh,
         in_specs=placed,
-        out_specs=P(None, ("ep", "tp"), None),
+        out_specs=P(None, (*ep, "tp"), None),
         check_vma=False,
     )

time: 379 us -> 384 us (1.013)
  waiting for transfers between devices: 166 us -> 170 us
    all_gather x1 -> x2, waiting for transfers between devices: 66.5 us -> 73.1 us  [the longest x1 64.1 us: per_device(): gathered = lax.all_gather(attended, 'eh', axis=1, tiled=True)]
  transfers between devices with their start and end apart: 3 -> 4, of which waited for: 3 -> 4; matrix products, arithmetic and copies ran while one was open for 0% -> 2% of each run, Pallas kernels for 0% -> 0%
where the time goes in v2:
time: 384 us; the launch traced here: 379 us
  waiting for transfers between devices  170 us (44%)
  blocking collectives  83.8 us (22%)
  local copies, waits for them, and re-layouts  53.6 us (14%)
  matrix products  38.6 us (10%)
  starting transfers between devices  13.7 us (4%)
  between operations  13.6 us (4%)
  other arithmetic  5.02 us (1%)
    all_to_all x1, blocking collectives, per_device(): lax.all_to_all(outgoing, ('eh', 'ec', 'tp'), split_axis=0, concat_axis=0,...  83.8 us
    all_to_all x1, waiting for transfers between devices, per_device(): lax.all_to_all(expert_out.reshape(wire_shape), ('eh', 'ec', 'tp'), split_...  75.9 us
    all_gather x1, waiting for transfers between devices, per_device(): gathered = lax.all_gather(attended, 'eh', axis=1, tiled=True)  64.1 us
    all_to_all x1, waiting for transfers between devices, per_device(): lax.all_to_all(grouped, ('eh', 'tp'), split_axis=1, concat_axis=1, tiled=...  20.6 us
    reshape x1, local copies, waits for them, and re-layouts, per_device(): expert_out.reshape(wire_shape)  10.5 us
    reshape x1, local copies, waits for them, and re-layouts, per_device(): outgoing = outgoing.reshape(wire_shape)  10.4 us
    reshape x1, local copies, waits for them, and re-layouts, per_device(): returned = returned.reshape(expert_count * slots_per, width)  10.3 us
    reshape x1, local copies, waits for them, and re-layouts, per_device(): flat_rows = arrived.reshape(-1, width)  10.3 us
  transfers between devices with their start and end apart: 4, of which 4 were waited for; matrix products, arithmetic and copies ran while one was open for 2% of the time, Pallas kernels for 0%

profile of v2, /device:TPU:1, one launch (start us, length us, event | category | flops | bytes accessed | tf_op | source)
XLA Modules:
  0.0 378.8 jit_solution(2882542828912851705)
XLA Ops:
  6.5 0.7 all-gather.5.cloned.1.call-update
  7.3 0.7 iota_compare_fusion.7
  8.0 0.8 fusion.37
  8.8 1.1 copy.92
  9.9 0.8 fusion.22
  10.7 0.1 copy.76
  10.8 0.1 fusion.36
  10.9 0.1 copy.78
  11.0 0.4 copy.77
  11.4 0.9 fusion.38
  12.4 0.6 fusion.13
  13.0 0.5 divide_convert_fusion
  13.5 0.4 fusion.14
  13.9 0.2 fusion.12
  14.2 0.9 reshape.207
  15.1 9.0 %all-gather.5.cloned.1.call-done = bf16[2048,256]{1,0:T(8,128)(2,1)} async-done(((bf16[2048,128]{1,0:T(8,128)(2,1)}), bf16[2048,256]{1,0:T(8,128)(2,1)}) %all-gather.5.cloned.1.call-update) | async-done | bytes 1048592 | tf_op jit(solution)/shard_map/all_gather | solution.py:75
  24.1 64.1 %all-gather.3.cloned.1.call-done = bf16[3,512,2048]{2,1,0:T(8,128)(2,1)} async-done(((bf16[3,32,2048]{2,1,0:T(8,128)(2,1)}), bf16[3,512,2048]{2,1,0:T(8,128)(2,1)}) %all-gather.3.cloned.1.call-update) | async-done | bytes 6291472 | tf_op jit(solution)/shard_map/all_gather | solution.py:76
  88.3 4.9 %convolution_bitcast_fusion = f32[3,64,8,256]{3,2,1,0:T(8,128)S(1)} fusion(bf16[3,512,2048]{2,1,0:T(8,128)(2,1)} %all-gather.3.cloned.1.call-done, bf16[2048,256]{1,0:T(8,128)(2,1)} %all-gather.5.cloned.1.call-done), kind=kOutput, calls=%fused_computation.15 | convolution fusion | flops 1610612736 | bytes 8912896 | tf_op jit(solution)/shard_map/srk,kc->src/dot_general | solution.py:77
  93.2 1.3 copy.82
  94.4 8.6 %all-to-all-start = ((f32[3,64,8,256]{3,2,0,1:T(8,128)}), f32[3,64,8,256]{3,2,0,1:T(8,128)S(1)}, u32[]{:S(2)}, u32[]{:S(2)}) async-start(f32[3,64,8,256]{3,2,0,1:T(8,128)} %copy.82), calls=%async_computation | async-start | bytes 3145728 | tf_op jit(solution)/shard_map/all_to_all | solution.py:81
  103.2 0.1 add.113
  103.3 0.1 add.107
  103.5 0.1 mul.102
  103.6 0.1 fusion.31
  103.7 0.1 reduce_window_sum.11
  103.8 0.2 select_reduce_fusion
  104.0 0.1 reduce_sum.61
  104.1 20.6 %all-to-all-done = f32[3,64,8,256]{3,2,0,1:T(8,128)S(1)} async-done(((f32[3,64,8,256]{3,2,0,1:T(8,128)}), f32[3,64,8,256]{3,2,0,1:T(8,128)S(1)}, u32[]{:S(2)}, u32[]{:S(2)}) %all-to-all-start) | async-done | bytes 1572896 | tf_op jit(solution)/shard_map/all_to_all | solution.py:81
  124.7 0.1 bitcast_reduce_fusion
  124.9 0.1 multiply_reduce_fusion
  125.1 4.3 %convolution_convert_fusion = bf16[768,4096]{1,0:T(8,128)(2,1)} fusion(s32[192]{0:T(256)S(1)} %add_add_fusion, f32[4096]{0:T(1024)S(1)} %copy-done.4, f32[3,8]{1,0:T(4,128)S(1)} %add_rsqrt_fusion, f32[3,8,4096]{2,1,0:T(8,128)S(1)} %bitcast.86, bf16[3,8,4096]{2,1,0:T(8,128)(2,1)S(1)} %copy-done.1, s32[192]{0:T(256)S(1)} %add.113), kind=kOutput, calls=%fused_computation.1 | convolution fusion | flops 161880576 | bytes 6899296 | tf_op jit(solution)/shard_map/dot_general | solution.py:114
  129.4 10.4 %reshape.211 = bf16[128,192,128]{2,1,0:T(8,128)(2,1)} reshape(bf16[768,4096]{1,0:T(8,128)(2,1)} %convolution_convert_fusion) | data formatting | bytes 12582912 | tf_op jit(solution)/shard_map/reshape | solution.py:118
  139.8 83.8 %all_to_all.15 = bf16[128,192,128]{2,1,0:T(8,128)(2,1)} all-to-all(bf16[128,192,128]{2,1,0:T(8,128)(2,1)} %reshape.211), channel_id=1, replica_groups=mesh['eh'=16,'ec'=2,'tp'=4] {'eh','ec','tp'}, dimensions={0} | all-to-all | bytes 12582912 | tf_op jit(solution)/shard_map/all_to_all | solution.py:119
  223.7 10.3 %reshape.212 = bf16[768,4096]{1,0:T(8,128)(2,1)} reshape(bf16[128,192,128]{2,1,0:T(8,128)(2,1)} %all_to_all.15) | data formatting | bytes 12582912 | tf_op jit(solution)/shard_map/reshape | solution.py:120
  234.0 9.1 %fusion.3 = f32[768,768]{1,0:T(8,128)S(1)} fusion(bf16[768,4096]{1,0:T(8,128)(2,1)} %reshape.212, bf16[1,4096,768]{2,1,0:T(8,128)(2,1)} %param.21), kind=kOutput, calls=%fused_computation.6 | convolution fusion | flops 4831838208 | bytes 14942208 | tf_op jit(solution)/shard_map/dot_general | solution.py:121
  243.1 8.0 %multiply_convert_fusion = bf16[768,768]{1,0:T(8,128)(2,1)S(1)} fusion(f32[768,768]{1,0:T(8,128)S(1)} %fusion.3, bf16[768,4096]{1,0:T(8,128)(2,1)S(1)} %copy-done, bf16[1,4096,768]{2,1,0:T(8,128)(2,1)} %param.22), kind=kOutput, calls=%fused_computation.10 | convolution fusion | flops 4835377152 | bytes 16121856 | tf_op jit(solution)/shard_map/dot_general | solution.py:122
  251.1 9.8 %convolution_convert_fusion.1 = bf16[768,4096]{1,0:T(8,128)(2,1)} fusion(bf16[768,768]{1,0:T(8,128)(2,1)S(1)} %multiply_convert_fusion, bf16[1,768,4096]{2,1,0:T(8,128)(2,1)} %param.23), kind=kOutput, calls=%fused_computation.2 | convolution fusion | flops 4834983936 | bytes 13762560 | tf_op jit(solution)/shard_map/dot_general | solution.py:124
  260.9 10.5 %reshape.213 = bf16[128,192,128]{2,1,0:T(8,128)(2,1)} reshape(bf16[768,4096]{1,0:T(8,128)(2,1)} %convolution_convert_fusion.1) | data formatting | bytes 12582912 | tf_op jit(solution)/shard_map/reshape | solution.py:128
  271.4 5.1 %all-to-all-start.2 = ((bf16[128,192,128]{2,1,0:T(8,128)(2,1)}), bf16[128,192,128]{2,1,0:T(8,128)(2,1)}, u32[]{:S(2)}, u32[]{:S(2)}) async-start(bf16[128,192,128]{2,1,0:T(8,128)(2,1)} %reshape.213), calls=%async_computation.2 | async-start | bytes 12582912 | tf_op jit(solution)/shard_map/all_to_all | solution.py:127
  276.5 0.1 add.116
  276.6 0.1 mul.113
  276.7 0.1 reduce_sum.63
  276.8 0.3 fusion.35
  277.1 75.9 %all-to-all-done.2 = bf16[128,192,128]{2,1,0:T(8,128)(2,1)} async-done(((bf16[128,192,128]{2,1,0:T(8,128)(2,1)}), bf16[128,192,128]{2,1,0:T(8,128)(2,1)}, u32[]{:S(2)}, u32[]{:S(2)}) %all-to-all-start.2) | async-done | bytes 6291488 | tf_op jit(solution)/shard_map/all_to_all | solution.py:127
  353.0 10.3 %reshape.214 = bf16[768,4096]{1,0:T(8,128)(2,1)} reshape(bf16[128,192,128]{2,1,0:T(8,128)(2,1)} %all-to-all-done.2) | data formatting | bytes 12582912 | tf_op jit(solution)/shard_map/reshape | solution.py:130
  363.3 6.6 %gather_fusion = bf16[192,4096]{1,0:T(8,128)(2,1)S(1)} fusion(bf16[768,4096]{1,0:T(8,128)(2,1)} %reshape.214, s32[1024]{0:T(1024)S(1)} %pad_clamp_fusion), kind=kCustom, calls=%fused_computation | custom fusion | bytes 3146496 | tf_op jit(solution)/shard_map/gather | solution.py:131
  370.0 1.2 fusion.5
  371.2 0.7 add_convert_fusion
  (31 shorter events, 0.5 us)
Async XLA Ops:
  6.5 4.9 %copy-start.2 = (bf16[2,32,128,128]{3,2,1,0:T(8,128)(2,1)S(1)}, bf16[2,32,128,128]{3,2,1,0:T(8,128)(2,1)}, u32[]{:S(2)}) copy-start(bf16[2,32,128,128]{3,2,1,0:T(8,128)(2,1)} %param.14) | copy-start | bytes 6291460
  6.5 17.6 %all-gather.5.cloned.1.call-start = ((), (), s32[]{:S(2)}) async-start(), calls=%async_computation.4 | async-start | bytes 1572864 | tf_op jit(solution)/shard_map/all_gather | solution.py:75
  7.3 81.0 %all-gather.3.cloned.1.call-start = ((), (), s32[]{:S(2)}) async-start(), calls=%async_computation.3 | async-start | bytes 6684672 | tf_op jit(solution)/shard_map/all_gather | solution.py:76
  94.4 9.0 %copy-start.3 = (s32[3,8,8]{2,1,0:T(8,128)S(1)}, s32[3,8,8]{2,1,0:T(8,128)}, u32[]{:S(2)}) copy-start(s32[3,8,8]{2,1,0:T(8,128)} %param.19) | copy-start | bytes 2308
  94.4 30.3 %all-to-all-start = ((f32[3,64,8,256]{3,2,0,1:T(8,128)}), f32[3,64,8,256]{3,2,0,1:T(8,128)S(1)}, u32[]{:S(2)}, u32[]{:S(2)}) async-start(f32[3,64,8,256]{3,2,0,1:T(8,128)} %copy.82), calls=%async_computation | async-start | bytes 3145728 | tf_op jit(solution)/shard_map/all_to_all | solution.py:81
  103.0 21.8 %copy-start.1 = (bf16[3,8,4096]{2,1,0:T(8,128)(2,1)S(1)}, bf16[3,8,4096]{2,1,0:T(8,128)(2,1)}, u32[]{:S(2)}) copy-start(bf16[3,8,4096]{2,1,0:T(8,128)(2,1)} %param.16) | copy-start | bytes 589828
  103.1 22.0 %copy-start.4 = (f32[4096]{0:T(1024)S(1)}, f32[4096]{0:T(1024)}, u32[]{:S(2)}) copy-start(f32[4096]{0:T(1024)} %param.17) | copy-start | bytes 49156
  234.0 9.1 %copy-start = (bf16[768,4096]{1,0:T(8,128)(2,1)S(1)}, bf16[768,4096]{1,0:T(8,128)(2,1)}, u32[]{:S(2)}) copy-start(bf16[768,4096]{1,0:T(8,128)(2,1)} %reshape.212) | copy-start | bytes 18874372
  271.4 5.4 %copy-start.5 = (f32[3,8,8]{2,1,0:T(8,128)S(1)}, f32[3,8,8]{2,1,0:T(8,128)}, u32[]{:S(2)}) copy-start(f32[3,8,8]{2,1,0:T(8,128)} %param.20) | copy-start | bytes 2308
  271.4 81.6 %all-to-all-start.2 = ((bf16[128,192,128]{2,1,0:T(8,128)(2,1)}), bf16[128,192,128]{2,1,0:T(8,128)(2,1)}, u32[]{:S(2)}, u32[]{:S(2)}) async-start(bf16[128,192,128]{2,1,0:T(8,128)(2,1)} %reshape.213), calls=%async_computation.2 | async-start | bytes 12582912 | tf_op jit(solution)/shard_map/all_to_all | solution.py:127
Sparse Core Ops, SparseCore 0:
  9.0 15.0 all-gather.4
  26.3 61.9 all-gather.2

commit v3 on v2

v3 whole, which is shorter than its diff:
```python
import jax
import jax.numpy as jnp
from jax import lax
from jax.sharding import Mesh, PartitionSpec as P

HEAD_SIZE = 128
TOPK = 8
SLOTS = 256
DECODE_STEPS = 3


masked_score = -1e30
norm_eps = 1e-06


def per_device(
    query,
    step_key_value,
    key_value_cache,
    lengths,
    hidden_in,
    norm_gain,
    w_out,
    routes,
    gate_scores,
    expert_gate,
    expert_up,
    expert_down,
):
    chip_count = lax.axis_size("eh")
    core_count = lax.axis_size("ec")
    ep_count = chip_count * core_count
    tp_count = lax.axis_size("tp")
    steps = query.shape[0]
    row_dev = query.shape[1]
    row_own = hidden_in.shape[1]
    width = hidden_in.shape[2]
    heads_dev = query.shape[2] // HEAD_SIZE
    cache_len = key_value_cache.shape[2]
    expert_count = ep_count * tp_count * expert_gate.shape[0]
    capacity = SLOTS // expert_count
    score_scale = HEAD_SIZE ** (-0.5)
    stored_keys = key_value_cache[0]
    stored_values = key_value_cache[1]
    usable = jnp.arange(cache_len, dtype=jnp.int32)[None, :] < lengths[:, None]

    query_rows = query.reshape(steps, row_dev, heads_dev, HEAD_SIZE)
    incoming_keys = step_key_value[:, 0]
    incoming_values = step_key_value[:, 1]
    cache_scores = (
        jnp.einsum("srhd,rjd->srhj", query_rows, stored_keys, preferred_element_type=jnp.float32)
        * score_scale
    )
    cache_scores = jnp.where(usable[None, :, None, :], cache_scores, masked_score)
    fresh_scores = (
        jnp.einsum("srhd,jrd->srhj", query_rows, incoming_keys, preferred_element_type=jnp.float32)
        * score_scale
    )
    fresh_ok = (
        jnp.arange(steps, dtype=jnp.int32)[None, :] <= jnp.arange(steps, dtype=jnp.int32)[:, None]
    )
    fresh_scores = jnp.where(fresh_ok[:, None, None, :], fresh_scores, masked_score)
    scores = jnp.concatenate([cache_scores, fresh_scores], axis=-1)
    top = jnp.max(scores, axis=-1, keepdims=True)
    raised = jnp.exp(scores - top)
    probs = (raised / jnp.sum(raised, axis=-1, keepdims=True)).astype(jnp.bfloat16)
    attended = jnp.einsum(
        "srhj,rjd->srhd", probs[..., :cache_len], stored_values, preferred_element_type=jnp.float32
    )
    attended = attended + jnp.einsum(
        "srhj,jrd->srhd", probs[..., cache_len:], incoming_values, preferred_element_type=jnp.float32
    )
    attended = attended.astype(jnp.bfloat16).reshape(steps, row_dev, heads_dev * HEAD_SIZE)

    w_pair = lax.all_gather(w_out, "ec", axis=1, tiled=True)
    blocks = width // 128
    wire_shape = (expert_count, capacity * blocks, 128)
    results = []
    for step in range(steps):
        gathered = lax.all_gather(attended[step], "eh", axis=0, tiled=True)
        partial_sums = jnp.dot(gathered, w_pair, preferred_element_type=jnp.float32)
        grouped = partial_sums.reshape(chip_count * tp_count, row_own, -1)
        arrived_sums = lax.all_to_all(
            grouped, ("eh", "tp"), split_axis=0, concat_axis=0, tiled=True
        )
        arrived_sums = arrived_sums.reshape(chip_count, tp_count, row_own, -1)
        projected = jnp.sum(arrived_sums, axis=1).astype(jnp.bfloat16)
        row_major = jnp.transpose(projected, (1, 0, 2)).reshape(row_own, width)

        residual = hidden_in[step].astype(jnp.float32) + row_major.astype(jnp.float32)
        mean_square = jnp.mean(residual * residual, axis=-1, keepdims=True)
        normed = (residual * lax.rsqrt(mean_square + norm_eps) * norm_gain).astype(jnp.bfloat16)
        weights = gate_scores[step] / jnp.sum(gate_scores[step], axis=-1, keepdims=True)

        expert_ids = routes[step].reshape(-1)
        assigned = expert_ids.shape[0]
        matches = (
            expert_ids[:, None] == jnp.arange(expert_count, dtype=jnp.int32)[None, :]
        ).astype(jnp.int32)
        earlier = jnp.cumsum(matches, axis=0) - matches
        slot_rank = jnp.sum(earlier * matches, axis=1)
        slot_index = expert_ids * capacity + slot_rank
        slot_onehot = (
            slot_index[:, None] == jnp.arange(expert_count * capacity, dtype=jnp.int32)[None, :]
        ).astype(jnp.bfloat16)
        row_onehot = (
            (jnp.arange(assigned, dtype=jnp.int32) // TOPK)[:, None]
            == jnp.arange(row_own, dtype=jnp.int32)[None, :]
        ).astype(jnp.bfloat16)
        selector = jnp.einsum(
            "as,ar->sr", slot_onehot, row_onehot, preferred_element_type=jnp.float32
        ).astype(jnp.bfloat16)
        outgoing = jnp.dot(selector, normed, preferred_element_type=jnp.float32).astype(
            jnp.bfloat16
        )
        arrived = lax.all_to_all(
            outgoing.reshape(wire_shape), ("eh", "ec", "tp"), split_axis=0, concat_axis=0,
            tiled=True,
        )
        flat_rows = arrived.reshape(-1, width)
        gate_act = jnp.dot(flat_rows, expert_gate[0], preferred_element_type=jnp.float32)
        up_act = jnp.dot(flat_rows, expert_up[0], preferred_element_type=jnp.float32)
        hidden = (jax.nn.silu(gate_act) * up_act).astype(jnp.bfloat16)
        expert_out = jnp.dot(hidden, expert_down[0], preferred_element_type=jnp.float32).astype(
            jnp.bfloat16
        )
        returned = lax.all_to_all(
            expert_out.reshape(wire_shape), ("eh", "ec", "tp"), split_axis=0, concat_axis=0,
            tiled=True,
        )
        returned = returned.reshape(expert_count * capacity, width)
        selected = returned[slot_index].astype(jnp.float32) * weights.reshape(-1)[:, None]
        expert_mix = jnp.sum(selected.reshape(row_own, TOPK, width), axis=1)
        results.append((residual + expert_mix).astype(jnp.bfloat16))
    return jnp.stack(results)


def solution(mesh):
    chips = mesh.devices.shape[0] // 2
    split_mesh = Mesh(
        mesh.devices.reshape(chips, 2, mesh.devices.shape[1]), ("eh", "ec", "tp")
    )
    ep = ("eh", "ec")
    placed = (
        P(None, ep, "tp"),
        P(None, None, ep, "tp"),
        P(None, ep, None, "tp"),
        P(ep),
        P(None, (*ep, "tp"), None),
        P(),
        P("tp", ep),
        P(None, (*ep, "tp"), None),
        P(None, (*ep, "tp"), None),
        P((*ep, "tp"), None, None),
        P((*ep, "tp"), None, None),
        P((*ep, "tp"), None, None),
    )
    return jax.shard_map(
        per_device,
        mesh=split_mesh,
        in_specs=placed,
        out_specs=P(None, (*ep, "tp"), None),
        check_vma=False,
    )
```

time: 384 us -> 423 us (1.10)
  blocking collectives: 83.8 us -> 0 us
  waiting for transfers between devices: 170 us -> 226 us
  starting transfers between devices: 13.7 us -> 55.8 us
  matrix products: 38.6 us -> 68.4 us
    all_to_all x1 -> x0, blocking collectives: 83.8 us -> none  [per_device(): lax.all_to_all(outgoing, ('eh', 'ec', 'tp'), split_axis=0, concat_axis=0,...]
    all_gather x1 -> x3, waiting for transfers between devices: 64.1 us -> 120 us  [per_device(): gathered = lax.all_gather(attended[step], 'eh', axis=0, tiled=True)]
    all_to_all x1 -> x6, waiting for transfers between devices: 20.6 us -> 65.4 us  [the longest x3 54.8 us: per_device(): lax.all_to_all(outgoing.reshape(wire_shape), ('eh', 'ec', 'tp'), split_ax...]
    all_to_all x1 -> x3, waiting for transfers between devices: 75.9 us -> 31.8 us  [per_device(): lax.all_to_all(expert_out.reshape(wire_shape), ('eh', 'ec', 'tp'), split_...]
    all_to_all x1 -> x6, starting transfers between devices: 8.6 us -> 41.4 us  [the longest x3 24.6 us: per_device(): lax.all_to_all(grouped, ('eh', 'tp'), split_axis=0, concat_axis=0, tiled=...]
    dot_general x1 -> x3, matrix products: 9.82 us -> 32.9 us  [per_device(): jnp.dot(hidden, expert_down[0], preferred_element_type=jnp.float32)]
    all_to_all x1 -> x3, starting transfers between devices: 5.1 us -> 14.3 us  [per_device(): lax.all_to_all(expert_out.reshape(wire_shape), ('eh', 'ec', 'tp'), split_...]
    dot_general x1 -> x3, matrix products: 9.09 us -> 17.8 us  [per_device(): jnp.dot(flat_rows, expert_gate[0], preferred_element_type=jnp.float32)]
  transfers between devices with their start and end apart: 4 -> 13, of which waited for: 4 -> 11; matrix products, arithmetic and copies ran while one was open for 2% -> 28% of each run, Pallas kernels for 0% -> 0%
where the time goes in v3:
time: 423 us; the launch traced here: 421 us
  waiting for transfers between devices  226 us (53%)
  matrix products  68.4 us (16%)
  starting transfers between devices  55.8 us (13%)
  local copies, waits for them, and re-layouts  50.3 us (12%)
  between operations  13.6 us (3%)
  other arithmetic  7.58 us (2%)
    all_gather x3, waiting for transfers between devices, per_device(): gathered = lax.all_gather(attended[step], 'eh', axis=0, tiled=True)  120 us
    all_to_all x3, waiting for transfers between devices, per_device(): lax.all_to_all(outgoing.reshape(wire_shape), ('eh', 'ec', 'tp'), split_ax...  54.8 us
    dot_general x3, matrix products, per_device(): jnp.dot(hidden, expert_down[0], preferred_element_type=jnp.float32)  32.9 us
    all_to_all x3, waiting for transfers between devices, per_device(): lax.all_to_all(expert_out.reshape(wire_shape), ('eh', 'ec', 'tp'), split_...  31.8 us
    all_to_all x3, starting transfers between devices, per_device(): lax.all_to_all(grouped, ('eh', 'tp'), split_axis=0, concat_axis=0, tiled=...  24.6 us
    dot_general x3, matrix products, per_device(): jnp.dot(flat_rows, expert_gate[0], preferred_element_type=jnp.float32)  17.8 us
    all_to_all x3, starting transfers between devices, per_device(): lax.all_to_all(outgoing.reshape(wire_shape), ('eh', 'ec', 'tp'), split_ax...  16.8 us
    all_to_all x3, starting transfers between devices, per_device(): lax.all_to_all(expert_out.reshape(wire_shape), ('eh', 'ec', 'tp'), split_...  14.3 us
  transfers between devices with their start and end apart: 13, of which 11 were waited for; matrix products, arithmetic and copies ran while one was open for 28% of the time, Pallas kernels for 0%

profile of v3, /device:TPU:1, one launch (start us, length us, event | category | flops | bytes accessed | tf_op | source)
XLA Modules:
  0.0 421.4 jit_solution(13521447124906731338)
XLA Ops:
  8.8 1.1 copy.49
  16.5 7.6 %all-gather.7.cloned.1.call-done = bf16[2048,256]{1,0:T(8,128)(2,1)} async-done(((bf16[2048,128]{1,0:T(8,128)(2,1)}), bf16[2048,256]{1,0:T(8,128)(2,1)}) %all-gather.7.cloned.1.call-update) | async-done | bytes 1048592 | tf_op jit(solution)/shard_map/all_gather | solution.py:75
  24.1 46.3 %all-gather.9.cloned.1.call-done = bf16[512,2048]{1,0:T(8,128)(2,1)} async-done(((bf16[32,2048]{1,0:T(8,128)(2,1)}), bf16[512,2048]{1,0:T(8,128)(2,1)}) %all-gather.9.cloned.1.call-update) | async-done | bytes 2097168 | tf_op jit(solution)/shard_map/all_gather | solution.py:80
  70.4 3.4 convolution_bitcast_fusion.1
  73.8 8.2 %all-to-all-start.3 = ((f32[64,8,256]{2,1,0:T(8,128)}), f32[64,8,256]{2,1,0:T(8,128)S(1)}, u32[]{:S(2)}, u32[]{:S(2)}) async-start(f32[64,8,256]{2,1,0:T(8,128)} %convolution_bitcast_fusion.1), calls=%async_computation.3 | async-start | bytes 1048576 | tf_op jit(solution)/shard_map/all_to_all | solution.py:83
  82.3 36.7 %all-gather.11.cloned.1.call-done = bf16[512,2048]{1,0:T(8,128)(2,1)} async-done(((bf16[32,2048]{1,0:T(8,128)(2,1)}), bf16[512,2048]{1,0:T(8,128)(2,1)}) %all-gather.11.cloned.1.call-update) | async-done | bytes 2097168 | tf_op jit(solution)/shard_map/all_gather | solution.py:80
  118.9 3.1 convolution_bitcast_fusion
  122.0 8.2 %all-to-all-start.6 = ((f32[64,8,256]{2,1,0:T(8,128)}), f32[64,8,256]{2,1,0:T(8,128)S(1)}, u32[]{:S(2)}, u32[]{:S(2)}) async-start(f32[64,8,256]{2,1,0:T(8,128)} %convolution_bitcast_fusion), calls=%async_computation.6 | async-start | bytes 1048576 | tf_op jit(solution)/shard_map/all_to_all | solution.py:83
  130.5 37.2 %all-gather.5.cloned.1.call-done = bf16[512,2048]{1,0:T(8,128)(2,1)} async-done(((bf16[32,2048]{1,0:T(8,128)(2,1)}), bf16[512,2048]{1,0:T(8,128)(2,1)}) %all-gather.5.cloned.1.call-update) | async-done | bytes 2097168 | tf_op jit(solution)/shard_map/all_gather | solution.py:80
  167.7 3.1 convolution_bitcast_fusion.2
  170.8 8.3 %all-to-all-start = ((f32[64,8,256]{2,1,0:T(8,128)}), f32[64,8,256]{2,1,0:T(8,128)S(1)}, u32[]{:S(2)}, u32[]{:S(2)}) async-start(f32[64,8,256]{2,1,0:T(8,128)} %convolution_bitcast_fusion.2), calls=%async_computation | async-start | bytes 1048576 | tf_op jit(solution)/shard_map/all_to_all | solution.py:83
  179.5 10.5 %all-to-all-done = f32[64,8,256]{2,1,0:T(8,128)S(1)} async-done(((f32[64,8,256]{2,1,0:T(8,128)}), f32[64,8,256]{2,1,0:T(8,128)S(1)}, u32[]{:S(2)}, u32[]{:S(2)}) %all-to-all-start) | async-done | bytes 524320 | tf_op jit(solution)/shard_map/all_to_all | solution.py:83
  190.2 1.0 convolution_convert_fusion
  191.3 2.4 reshape.368
  193.6 7.0 %all-to-all-start.7 = ((bf16[128,64,128]{2,1,0:T(8,128)(2,1)}), bf16[128,64,128]{2,1,0:T(8,128)(2,1)S(1)}, u32[]{:S(2)}, u32[]{:S(2)}) async-start(bf16[128,64,128]{2,1,0:T(8,128)(2,1)} %reshape.368), calls=%async_computation.7 | async-start | bytes 4194304 | tf_op jit(solution)/shard_map/all_to_all | solution.py:116
  201.0 2.3 convolution_convert_fusion.1
  203.4 4.2 reshape.362
  207.6 23.9 %all-to-all-done.7 = bf16[128,64,128]{2,1,0:T(8,128)(2,1)S(1)} async-done(((bf16[128,64,128]{2,1,0:T(8,128)(2,1)}), bf16[128,64,128]{2,1,0:T(8,128)(2,1)S(1)}, u32[]{:S(2)}, u32[]{:S(2)}) %all-to-all-start.7) | async-done | bytes 2097184 | tf_op jit(solution)/shard_map/all_to_all | solution.py:116
  231.5 5.0 %all-to-all-start.4 = ((bf16[128,64,128]{2,1,0:T(8,128)(2,1)}), bf16[128,64,128]{2,1,0:T(8,128)(2,1)}, u32[]{:S(2)}, u32[]{:S(2)}) async-start(bf16[128,64,128]{2,1,0:T(8,128)(2,1)} %reshape.362), calls=%async_computation.4 | async-start | bytes 4194304 | tf_op jit(solution)/shard_map/all_to_all | solution.py:116
  236.5 2.4 convolution_convert_fusion.2
  238.9 4.2 reshape.356
  243.1 24.0 %all-to-all-done.4 = bf16[128,64,128]{2,1,0:T(8,128)(2,1)} async-done(((bf16[128,64,128]{2,1,0:T(8,128)(2,1)}), bf16[128,64,128]{2,1,0:T(8,128)(2,1)}, u32[]{:S(2)}, u32[]{:S(2)}) %all-to-all-start.4) | async-done | bytes 2097184 | tf_op jit(solution)/shard_map/all_to_all | solution.py:116
  267.1 4.8 %all-to-all-start.1 = ((bf16[128,64,128]{2,1,0:T(8,128)(2,1)}), bf16[128,64,128]{2,1,0:T(8,128)(2,1)}, u32[]{:S(2)}, u32[]{:S(2)}) async-start(bf16[128,64,128]{2,1,0:T(8,128)(2,1)} %reshape.356), calls=%async_computation.1 | async-start | bytes 4194304 | tf_op jit(solution)/shard_map/all_to_all | solution.py:116
  271.9 2.3 reshape.369
  274.3 6.2 %fusion.12 = f32[256,768]{1,0:T(8,128)} fusion(bf16[256,4096]{1,0:T(8,128)(2,1)} %reshape.369, bf16[1,4096,768]{2,1,0:T(8,128)(2,1)} %param.21), kind=kOutput, calls=%fused_computation.15 | convolution fusion | flops 1610612736 | bytes 9175040 | tf_op jit(solution)/shard_map/dot_general | solution.py:121
  280.5 10.8 %fusion.24 = bf16[256,4096]{1,0:T(8,128)(2,1)} fusion(bf16[1,768,4096]{2,1,0:T(8,128)(2,1)} %param.23, bf16[256,4096]{1,0:T(8,128)(2,1)S(1)} %copy-done.1, bf16[1,4096,768]{2,1,0:T(8,128)(2,1)} %param.22, f32[256,768]{1,0:T(8,128)} %fusion.12), kind=kOutput, calls=%fused_computation.26 | convolution fusion | flops 3223453696 | bytes 17563648 | tf_op jit(solution)/shard_map/dot_general | solution.py:124
  291.3 4.2 %reshape.370 = bf16[128,64,128]{2,1,0:T(8,128)(2,1)} reshape(bf16[256,4096]{1,0:T(8,128)(2,1)} %fusion.24) | data formatting | bytes 4194304 | tf_op jit(solution)/shard_map/reshape | solution.py:128
  295.5 7.0 %all-to-all-done.1 = bf16[128,64,128]{2,1,0:T(8,128)(2,1)} async-done(((bf16[128,64,128]{2,1,0:T(8,128)(2,1)}), bf16[128,64,128]{2,1,0:T(8,128)(2,1)}, u32[]{:S(2)}, u32[]{:S(2)}) %all-to-all-start.1) | async-done | bytes 2097184 | tf_op jit(solution)/shard_map/all_to_all | solution.py:116
  302.5 3.8 all-to-all-start.8
  306.3 4.2 reshape.363
  310.5 6.1 %fusion.14 = f32[256,768]{1,0:T(8,128)} fusion(bf16[256,4096]{1,0:T(8,128)(2,1)} %reshape.363, bf16[1,4096,768]{2,1,0:T(8,128)(2,1)} %param.21), kind=kOutput, calls=%fused_computation.17 | convolution fusion | flops 1610612736 | bytes 9175040 | tf_op jit(solution)/shard_map/dot_general | solution.py:121
  316.6 11.4 %fusion.21 = bf16[256,4096]{1,0:T(8,128)(2,1)} fusion(bf16[1,768,4096]{2,1,0:T(8,128)(2,1)} %param.23, bf16[256,4096]{1,0:T(8,128)(2,1)} %reshape.363, bf16[1,4096,768]{2,1,0:T(8,128)(2,1)} %param.22, f32[256,768]{1,0:T(8,128)} %fusion.14), kind=kOutput, calls=%fused_computation.25 | convolution fusion | flops 3223453696 | bytes 17563648 | tf_op jit(solution)/shard_map/dot_general | solution.py:124
  328.0 4.2 reshape.364
  332.2 5.0 %all-to-all-done.8 = bf16[128,64,128]{2,1,0:T(8,128)(2,1)S(1)} async-done(((bf16[128,64,128]{2,1,0:T(8,128)(2,1)}), bf16[128,64,128]{2,1,0:T(8,128)(2,1)S(1)}, u32[]{:S(2)}, u32[]{:S(2)}) %all-to-all-start.8) | async-done | bytes 2097184 | tf_op jit(solution)/shard_map/all_to_all | solution.py:127
  337.2 1.3 copy-done
  338.5 5.3 %all-to-all-start.5 = ((bf16[128,64,128]{2,1,0:T(8,128)(2,1)}), bf16[128,64,128]{2,1,0:T(8,128)(2,1)}, u32[]{:S(2)}, u32[]{:S(2)}) async-start(bf16[128,64,128]{2,1,0:T(8,128)(2,1)} %reshape.364), calls=%async_computation.5 | async-start | bytes 4194304 | tf_op jit(solution)/shard_map/all_to_all | solution.py:127
  343.9 2.8 reshape.357
  346.7 5.4 %fusion.16 = f32[256,768]{1,0:T(8,128)} fusion(bf16[256,4096]{1,0:T(8,128)(2,1)S(1)} %reshape.357, bf16[1,4096,768]{2,1,0:T(8,128)(2,1)} %param.21), kind=kOutput, calls=%fused_computation.19 | convolution fusion | flops 1610612736 | bytes 9175040 | tf_op jit(solution)/shard_map/dot_general | solution.py:121
  352.1 10.8 %fusion.18 = bf16[256,4096]{1,0:T(8,128)(2,1)} fusion(bf16[1,768,4096]{2,1,0:T(8,128)(2,1)} %param.23, bf16[256,4096]{1,0:T(8,128)(2,1)S(1)} %reshape.357, bf16[1,4096,768]{2,1,0:T(8,128)(2,1)} %param.22, f32[256,768]{1,0:T(8,128)} %fusion.16), kind=kOutput, calls=%fused_computation.24 | convolution fusion | flops 3223453696 | bytes 17563648 | tf_op jit(solution)/shard_map/dot_general | solution.py:124
  362.9 4.2 reshape.358
  367.1 7.1 %all-to-all-done.5 = bf16[128,64,128]{2,1,0:T(8,128)(2,1)} async-done(((bf16[128,64,128]{2,1,0:T(8,128)(2,1)}), bf16[128,64,128]{2,1,0:T(8,128)(2,1)}, u32[]{:S(2)}, u32[]{:S(2)}) %all-to-all-start.5) | async-done | bytes 2097184 | tf_op jit(solution)/shard_map/all_to_all | solution.py:127
  374.3 5.1 %all-to-all-start.2 = ((bf16[128,64,128]{2,1,0:T(8,128)(2,1)}), bf16[128,64,128]{2,1,0:T(8,128)(2,1)}, u32[]{:S(2)}, u32[]{:S(2)}) async-start(bf16[128,64,128]{2,1,0:T(8,128)(2,1)} %reshape.358), calls=%async_computation.2 | async-start | bytes 4194304 | tf_op jit(solution)/shard_map/all_to_all | solution.py:127
  380.5 2.8 reshape.371
  384.2 2.8 reshape.365
  388.1 1.1 fusion.51
  389.2 1.1 fusion.52
  390.2 19.7 %all-to-all-done.2 = bf16[128,64,128]{2,1,0:T(8,128)(2,1)} async-done(((bf16[128,64,128]{2,1,0:T(8,128)(2,1)}), bf16[128,64,128]{2,1,0:T(8,128)(2,1)}, u32[]{:S(2)}, u32[]{:S(2)}) %all-to-all-start.2) | async-done | bytes 2097184 | tf_op jit(solution)/shard_map/all_to_all | solution.py:127
  409.9 2.8 reshape.359
  (91 shorter events, 15.4 us)
Async XLA Ops:
  6.5 4.9 %copy-start.6 = (bf16[2,32,128,128]{3,2,1,0:T(8,128)(2,1)S(1)}, bf16[2,32,128,128]{3,2,1,0:T(8,128)(2,1)}, u32[]{:S(2)}) copy-start(bf16[2,32,128,128]{3,2,1,0:T(8,128)(2,1)} %param.14) | copy-start | bytes 6291460
  6.5 17.6 %all-gather.7.cloned.1.call-start = ((), (), s32[]{:S(2)}) async-start(), calls=%async_computation.10 | async-start | bytes 1572864 | tf_op jit(solution)/shard_map/all_gather | solution.py:75
  7.3 63.2 %all-gather.9.cloned.1.call-start = ((), (), s32[]{:S(2)}) async-start(), calls=%async_computation.11 | async-start | bytes 2228224 | tf_op jit(solution)/shard_map/all_gather | solution.py:80
  13.9 2.5 copy-start.9
  14.9 104.0 %all-gather.11.cloned.1.call-start = ((), (), s32[]{:S(2)}) async-start(), calls=%async_computation.12 | async-start | bytes 2228224 | tf_op jit(solution)/shard_map/all_gather | solution.py:80
  15.6 152.1 %all-gather.5.cloned.1.call-start = ((), (), s32[]{:S(2)}) async-start(), calls=%async_computation.9 | async-start | bytes 2228224 | tf_op jit(solution)/shard_map/all_gather | solution.py:80
  24.1 94.8 %copy-start.10 = (bf16[2048,256]{1,0:T(8,128)(2,1)S(1)}, bf16[2048,256]{1,0:T(8,128)(2,1)}, u32[]{:S(2)}) copy-start(bf16[2048,256]{1,0:T(8,128)(2,1)} %all-gather.7.cloned.1.call-done) | copy-start | bytes 3145732
  73.8 48.3 %all-to-all-start.3 = ((f32[64,8,256]{2,1,0:T(8,128)}), f32[64,8,256]{2,1,0:T(8,128)S(1)}, u32[]{:S(2)}, u32[]{:S(2)}) async-start(f32[64,8,256]{2,1,0:T(8,128)} %convolution_bitcast_fusion.1), calls=%async_computation.3 | async-start | bytes 1048576 | tf_op jit(solution)/shard_map/all_to_all | solution.py:83
  122.0 48.8 %all-to-all-start.6 = ((f32[64,8,256]{2,1,0:T(8,128)}), f32[64,8,256]{2,1,0:T(8,128)S(1)}, u32[]{:S(2)}, u32[]{:S(2)}) async-start(f32[64,8,256]{2,1,0:T(8,128)} %convolution_bitcast_fusion), calls=%async_computation.6 | async-start | bytes 1048576 | tf_op jit(solution)/shard_map/all_to_all | solution.py:83
  170.8 19.2 %copy-start.2 = (bf16[3,8,4096]{2,1,0:T(8,128)(2,1)S(1)}, bf16[3,8,4096]{2,1,0:T(8,128)(2,1)}, u32[]{:S(2)}) copy-start(bf16[3,8,4096]{2,1,0:T(8,128)(2,1)} %param.16) | copy-start | bytes 589828
  170.8 19.4 %copy-start.7 = (f32[4096]{0:T(1024)S(1)}, f32[4096]{0:T(1024)}, u32[]{:S(2)}) copy-start(f32[4096]{0:T(1024)} %param.17) | copy-start | bytes 49156
  170.8 19.1 %all-to-all-start = ((f32[64,8,256]{2,1,0:T(8,128)}), f32[64,8,256]{2,1,0:T(8,128)S(1)}, u32[]{:S(2)}, u32[]{:S(2)}) async-start(f32[64,8,256]{2,1,0:T(8,128)} %convolution_bitcast_fusion.2), calls=%async_computation | async-start | bytes 1048576 | tf_op jit(solution)/shard_map/all_to_all | solution.py:83
  193.6 37.9 %all-to-all-start.7 = ((bf16[128,64,128]{2,1,0:T(8,128)(2,1)}), bf16[128,64,128]{2,1,0:T(8,128)(2,1)S(1)}, u32[]{:S(2)}, u32[]{:S(2)}) async-start(bf16[128,64,128]{2,1,0:T(8,128)(2,1)} %reshape.368), calls=%async_computation.7 | async-start | bytes 4194304 | tf_op jit(solution)/shard_map/all_to_all | solution.py:116
  231.5 35.6 %all-to-all-start.4 = ((bf16[128,64,128]{2,1,0:T(8,128)(2,1)}), bf16[128,64,128]{2,1,0:T(8,128)(2,1)}, u32[]{:S(2)}, u32[]{:S(2)}) async-start(bf16[128,64,128]{2,1,0:T(8,128)(2,1)} %reshape.362), calls=%async_computation.4 | async-start | bytes 4194304 | tf_op jit(solution)/shard_map/all_to_all | solution.py:116
  267.1 35.4 %all-to-all-start.1 = ((bf16[128,64,128]{2,1,0:T(8,128)(2,1)}), bf16[128,64,128]{2,1,0:T(8,128)(2,1)}, u32[]{:S(2)}, u32[]{:S(2)}) async-start(bf16[128,64,128]{2,1,0:T(8,128)(2,1)} %reshape.356), calls=%async_computation.1 | async-start | bytes 4194304 | tf_op jit(solution)/shard_map/all_to_all | solution.py:116
  274.3 6.2 %copy-start.1 = (bf16[256,4096]{1,0:T(8,128)(2,1)S(1)}, bf16[256,4096]{1,0:T(8,128)(2,1)}, u32[]{:S(2)}) copy-start(bf16[256,4096]{1,0:T(8,128)(2,1)} %reshape.369) | copy-start | bytes 6291460
  302.5 34.7 %all-to-all-start.8 = ((bf16[128,64,128]{2,1,0:T(8,128)(2,1)}), bf16[128,64,128]{2,1,0:T(8,128)(2,1)S(1)}, u32[]{:S(2)}, u32[]{:S(2)}) async-start(bf16[128,64,128]{2,1,0:T(8,128)(2,1)} %reshape.370), calls=%async_computation.8 | async-start | bytes 4194304 | tf_op jit(solution)/shard_map/all_to_all | solution.py:127
  337.2 1.3 copy-start
  338.5 35.8 %all-to-all-start.5 = ((bf16[128,64,128]{2,1,0:T(8,128)(2,1)}), bf16[128,64,128]{2,1,0:T(8,128)(2,1)}, u32[]{:S(2)}, u32[]{:S(2)}) async-start(bf16[128,64,128]{2,1,0:T(8,128)(2,1)} %reshape.364), calls=%async_computation.5 | async-start | bytes 4194304 | tf_op jit(solution)/shard_map/all_to_all | solution.py:127
  367.1 13.2 %copy-start.8 = (f32[3,8,8]{2,1,0:T(8,128)S(1)}, f32[3,8,8]{2,1,0:T(8,128)}, u32[]{:S(2)}) copy-start(f32[3,8,8]{2,1,0:T(8,128)} %param.20) | copy-start | bytes 2308
  374.3 35.7 %all-to-all-start.2 = ((bf16[128,64,128]{2,1,0:T(8,128)(2,1)}), bf16[128,64,128]{2,1,0:T(8,128)(2,1)}, u32[]{:S(2)}, u32[]{:S(2)}) async-start(bf16[128,64,128]{2,1,0:T(8,128)(2,1)} %reshape.358), calls=%async_computation.2 | async-start | bytes 4194304 | tf_op jit(solution)/shard_map/all_to_all | solution.py:127
  412.8 1.4 copy-start.3
  412.8 1.4 copy-start.4
  412.8 1.4 copy-start.5
Sparse Core Ops, SparseCore 0:
  9.0 15.0 all-gather.6
  26.3 44.1 all-gather.8
  72.6 46.3 all-gather.10
  120.9 46.7 all-gather.4

commit v4 on v1

--- a/solution.py
+++ b/solution.py
@@ -98,21 +98,15 @@
     slot_rank = jnp.sum(earlier * matches, axis=2)
     step_ids = jnp.arange(steps, dtype=jnp.int32)[:, None]
     slot_index = (expert_ids * slots_per + step_ids * capacity + slot_rank).reshape(-1)
-    slot_onehot = (
-        slot_index[:, None] == jnp.arange(expert_count * slots_per, dtype=jnp.int32)[None, :]
-    ).astype(jnp.bfloat16)
     row_ids = (step_ids * row_own + jnp.arange(assigned, dtype=jnp.int32)[None, :] // TOPK).reshape(-1)
-    row_onehot = (
-        row_ids[:, None] == jnp.arange(steps * row_own, dtype=jnp.int32)[None, :]
-    ).astype(jnp.bfloat16)
-    selector = jnp.einsum(
-        "as,ar->sr", slot_onehot, row_onehot, preferred_element_type=jnp.float32
-    ).astype(jnp.bfloat16)
-    outgoing = jnp.dot(
-        selector, normed.reshape(steps * row_own, width), preferred_element_type=jnp.float32
-    ).astype(jnp.bfloat16)
-    wire_shape = (expert_count, slots_per * width // 128, 128)
-    outgoing = outgoing.reshape(wire_shape)
+    empty = steps * row_own
+    source_row = jnp.full((expert_count * slots_per,), empty, jnp.int32).at[slot_index].set(row_ids)
+    blocks = width // 128
+    padded = jnp.concatenate(
+        [normed.reshape(steps * row_own, blocks, 128), jnp.zeros((1, blocks, 128), jnp.bfloat16)]
+    )
+    wire_shape = (expert_count, slots_per * blocks, 128)
+    outgoing = jnp.take(padded, source_row, axis=0).reshape(wire_shape)
     arrived = lax.all_to_all(outgoing, ("ep", "tp"), split_axis=0, concat_axis=0, tiled=True)
     flat_rows = arrived.reshape(-1, width)
     gate_act = jnp.dot(flat_rows, expert_gate[0], preferred_element_type=jnp.float32)
@@ -124,9 +118,11 @@
     returned = lax.all_to_all(
         expert_out.reshape(wire_shape), ("ep", "tp"), split_axis=0, concat_axis=0, tiled=True
     )
-    returned = returned.reshape(expert_count * slots_per, width)
-    selected = returned[slot_index].astype(jnp.float32) * weights.reshape(-1)[:, None]
-    expert_mix = jnp.sum(selected.reshape(steps, row_own, TOPK, width), axis=2)
+    returned = returned.reshape(expert_count * slots_per, blocks, 128)
+    selected = jnp.take(returned, slot_index, axis=0).astype(jnp.float32)
+    selected = selected * weights.reshape(-1)[:, None, None]
+    expert_mix = jnp.sum(selected.reshape(steps, row_own, TOPK, blocks, 128), axis=2)
+    expert_mix = expert_mix.reshape(steps, row_own, width)
     return (residual + expert_mix).astype(jnp.bfloat16)
 
 

time: 379 us -> 359 us (0.947)
  local copies, waits for them, and re-layouts: 54.2 us -> 36.4 us
  other arithmetic: 5.02 us -> 10.5 us
  matrix products: 41.3 us -> 36.9 us
    reshape x2 -> x1, local copies, waits for them, and re-layouts: 20.8 us -> 0.08 us  [per_device(): expert_mix = expert_mix.reshape(steps, row_own, width)]
    select_n x1 -> x3, other arithmetic: 0.01 us -> 5.66 us  [the longest x2 5.65 us: per_device(): outgoing = jnp.take(padded, source_row, axis=0).reshape(wire_shape)]
    dot_general x1 -> x0, matrix products: 4.36 us -> none  [per_device(): jnp.dot(selector, normed.reshape(steps * row_own, width), preferred_eleme...]
    gather x1 -> x2, local copies, waits for them, and re-layouts: 6.7 us -> 8.18 us  [the longest x1 4.44 us: per_device(): outgoing = jnp.take(padded, source_row, axis=0).reshape(wire_shape)]
  transfers between devices with their start and end apart: 3 -> 3, of which waited for: 3 -> 3; matrix products, arithmetic and copies ran while one was open for 0% -> 1% of each run, Pallas kernels for 0% -> 0%
where the time goes in v4:
time: 359 us; the launch traced here: 355 us
  waiting for transfers between devices  165 us (46%)
  blocking collectives  79.7 us (22%)
  matrix products  36.9 us (10%)
  local copies, waits for them, and re-layouts  36.4 us (10%)
  between operations  13.7 us (4%)
  starting transfers between devices  12.5 us (3%)
  other arithmetic  10.5 us (3%)
    all_to_all x1, blocking collectives, per_device(): lax.all_to_all(outgoing, ('ep', 'tp'), split_axis=0, concat_axis=0, tiled...  79.7 us
    all_to_all x1, waiting for transfers between devices, per_device(): lax.all_to_all(expert_out.reshape(wire_shape), ('ep', 'tp'), split_axis=0...  76.1 us
    all_gather x1, waiting for transfers between devices, per_device(): gathered = lax.all_gather(attended, 'ep', axis=1, tiled=True)  65.8 us
    all_to_all x1, waiting for transfers between devices, per_device(): lax.all_to_all(grouped, ('ep', 'tp'), split_axis=1, concat_axis=1, tiled=...  23 us
    reshape x1, local copies, waits for them, and re-layouts, per_device(): expert_out.reshape(wire_shape)  10.4 us
    reshape x1, local copies, waits for them, and re-layouts, per_device(): flat_rows = arrived.reshape(-1, width)  10.3 us
    dot_general x1, matrix products, per_device(): jnp.dot(hidden, expert_down[0], preferred_element_type=jnp.float32)  9.75 us
    dot_general x1, matrix products, per_device(): jnp.dot(flat_rows, expert_gate[0], preferred_element_type=jnp.float32)  9.09 us
  transfers between devices with their start and end apart: 3, of which 3 were waited for; matrix products, arithmetic and copies ran while one was open for 1% of the time, Pallas kernels for 0%

profile of v4, /device:TPU:1, one launch (start us, length us, event | category | flops | bytes accessed | tf_op | source)
XLA Modules:
  0.0 354.7 jit_solution(3874698699593634881)
XLA Ops:
  6.5 1.1 copy.106
  7.7 0.8 fusion.31
  8.4 0.8 fusion.21
  9.2 0.1 copy.88
  9.3 0.1 fusion.30
  9.4 0.1 copy.90
  9.5 0.7 iota_compare_fusion.1
  10.3 0.4 copy.89
  10.7 2.1 fusion.32
  12.9 0.6 fusion.12
  13.5 0.5 divide_convert_fusion
  14.0 0.4 copy-done.4
  14.5 0.4 fusion.13
  14.9 0.2 fusion.11
  15.2 0.9 reshape.205
  16.2 0.1 fusion.25
  16.3 0.1 reduce_window_sum.11
  16.4 0.2 select_reduce_fusion
  16.6 0.1 reduce_sum.62
  16.7 65.8 %all-gather.2.cloned.1.call-done = bf16[3,1024,2048]{2,1,0:T(8,128)(2,1)} async-done(((bf16[3,32,2048]{2,1,0:T(8,128)(2,1)}), bf16[3,1024,2048]{2,1,0:T(8,128)(2,1)}) %all-gather.2.cloned.1.call-update) | async-done | bytes 12582928 | tf_op jit(solution)/shard_map/all_gather | solution.py:73
  82.6 6.4 %convolution_bitcast_fusion = f32[3,128,8,128]{3,2,1,0:T(8,128)S(1)} fusion(bf16[3,1024,2048]{2,1,0:T(8,128)(2,1)} %all-gather.2.cloned.1.call-done, bf16[2048,128]{1,0:T(8,128)(2,1)S(1)} %copy-done), kind=kOutput, calls=%fused_computation.16 | convolution fusion | flops 1610612736 | bytes 14680064 | tf_op jit(solution)/shard_map/srk,kc->src/dot_general | solution.py:74
  89.0 1.3 copy.94
  90.3 7.5 %all-to-all-start = ((f32[3,128,8,128]{3,2,0,1:T(8,128)}), f32[3,128,8,128]{3,2,0,1:T(8,128)S(1)}, u32[]{:S(2)}, u32[]{:S(2)}) async-start(f32[3,128,8,128]{3,2,0,1:T(8,128)} %copy.94), calls=%async_computation | async-start | bytes 3145728 | tf_op jit(solution)/shard_map/all_to_all | solution.py:78
  97.8 0.1 add.128
  97.9 0.1 mul.101
  98.1 0.1 reshape.234
  98.2 1.2 scatter_custom_fusion
  99.4 0.2 broadcast_in_dim.77
  99.7 0.1 copy.97
  99.8 23.0 %all-to-all-done = f32[3,128,8,128]{3,2,0,1:T(8,128)S(1)} async-done(((f32[3,128,8,128]{3,2,0,1:T(8,128)}), f32[3,128,8,128]{3,2,0,1:T(8,128)S(1)}, u32[]{:S(2)}, u32[]{:S(2)}) %all-to-all-start) | async-done | bytes 1572896 | tf_op jit(solution)/shard_map/all_to_all | solution.py:78
  122.9 0.1 bitcast_reduce_fusion
  123.0 0.2 multiply_reduce_fusion.1
  123.2 0.1 fusion.24
  123.3 4.4 %gather_fusion = bf16[768,32,128]{2,1,0:T(8,128)(2,1)} fusion(bf16[25,32,128]{2,1,0:T(8,128)(2,1)S(1)} %concatenate.7, s32[1024]{0:T(1024)S(1)} %pad_clamp_fusion.1), kind=kCustom, calls=%fused_computation | custom fusion | bytes 12585984 | tf_op jit(solution)/shard_map/jit(_take)/gather | solution.py:109
  127.8 5.7 %bitcast_select_fusion = bf16[128,192,128]{2,1,0:T(8,128)(2,1)S(1)} fusion(pred[128,192]{1,0:T(8,128)(4,1)S(1)} %copy.97, bf16[128,192,128]{2,1,0:T(8,128)(2,1)} %bitcast.101), kind=kLoop, calls=%fused_computation.9 | loop fusion | flops 3145728 | bytes 12607488 | tf_op jit(solution)/shard_map/jit(_take)/select_n | solution.py:109
  133.4 79.7 %all_to_all.15 = bf16[128,192,128]{2,1,0:T(8,128)(2,1)} all-to-all(bf16[128,192,128]{2,1,0:T(8,128)(2,1)S(1)} %bitcast_select_fusion), channel_id=1, replica_groups=mesh['ep'=32,'tp'=4] {'ep','tp'}, dimensions={0} | all-to-all | bytes 12582912 | tf_op jit(solution)/shard_map/all_to_all | solution.py:110
  213.1 10.3 %reshape.209 = bf16[768,4096]{1,0:T(8,128)(2,1)} reshape(bf16[128,192,128]{2,1,0:T(8,128)(2,1)} %all_to_all.15) | data formatting | bytes 12582912 | tf_op jit(solution)/shard_map/reshape | solution.py:111
  223.5 9.1 %fusion.3 = f32[768,768]{1,0:T(8,128)S(1)} fusion(bf16[768,4096]{1,0:T(8,128)(2,1)} %reshape.209, bf16[1,4096,768]{2,1,0:T(8,128)(2,1)} %param.21), kind=kOutput, calls=%fused_computation.7 | convolution fusion | flops 4831838208 | bytes 14942208 | tf_op jit(solution)/shard_map/dot_general | solution.py:112
  232.6 8.0 %multiply_convert_fusion = bf16[768,768]{1,0:T(8,128)(2,1)S(1)} fusion(f32[768,768]{1,0:T(8,128)S(1)} %fusion.3, bf16[768,4096]{1,0:T(8,128)(2,1)S(1)} %copy-done.2, bf16[1,4096,768]{2,1,0:T(8,128)(2,1)} %param.22), kind=kOutput, calls=%fused_computation.11 | convolution fusion | flops 4835377152 | bytes 16121856 | tf_op jit(solution)/shard_map/dot_general | solution.py:113
  240.6 9.7 %convolution_convert_fusion = bf16[768,4096]{1,0:T(8,128)(2,1)} fusion(bf16[768,768]{1,0:T(8,128)(2,1)S(1)} %multiply_convert_fusion, bf16[1,768,4096]{2,1,0:T(8,128)(2,1)} %param.23), kind=kOutput, calls=%fused_computation.3 | convolution fusion | flops 4834983936 | bytes 13762560 | tf_op jit(solution)/shard_map/dot_general | solution.py:115
  250.3 10.4 %reshape.210 = bf16[128,192,128]{2,1,0:T(8,128)(2,1)} reshape(bf16[768,4096]{1,0:T(8,128)(2,1)} %convolution_convert_fusion) | data formatting | bytes 12582912 | tf_op jit(solution)/shard_map/reshape | solution.py:119
  260.8 5.0 %all-to-all-start.2 = ((bf16[128,192,128]{2,1,0:T(8,128)(2,1)}), bf16[128,192,128]{2,1,0:T(8,128)(2,1)}, u32[]{:S(2)}, u32[]{:S(2)}) async-start(bf16[128,192,128]{2,1,0:T(8,128)(2,1)} %reshape.210), calls=%async_computation.2 | async-start | bytes 12582912 | tf_op jit(solution)/shard_map/all_to_all | solution.py:118
  265.9 0.3 fusion.27
  266.2 0.1 compare_and_fusion
  266.3 76.1 %all-to-all-done.2 = bf16[128,192,128]{2,1,0:T(8,128)(2,1)} async-done(((bf16[128,192,128]{2,1,0:T(8,128)(2,1)}), bf16[128,192,128]{2,1,0:T(8,128)(2,1)}, u32[]{:S(2)}, u32[]{:S(2)}) %all-to-all-start.2) | async-done | bytes 6291488 | tf_op jit(solution)/shard_map/all_to_all | solution.py:118
  342.4 3.7 %gather_fusion.1 = bf16[192,32,128]{2,1,0:T(8,128)(2,1)S(1)} fusion(bf16[768,32,128]{2,1,0:T(8,128)(2,1)} %bitcast.25, s32[1024]{0:T(1024)S(1)} %pad_clamp_fusion), kind=kCustom, calls=%fused_computation.1 | custom fusion | bytes 3146496 | tf_op jit(solution)/shard_map/jit(_take)/gather | solution.py:122
  346.1 0.9 multiply_reduce_fusion
  347.1 0.7 add_convert_fusion
  (39 shorter events, 0.7 us)
Async XLA Ops:
  6.5 76.0 %copy-start = (bf16[2048,128]{1,0:T(8,128)(2,1)S(1)}, bf16[2048,128]{1,0:T(8,128)(2,1)}, u32[]{:S(2)}) copy-start(bf16[2048,128]{1,0:T(8,128)(2,1)} %param.18) | copy-start | bytes 1572868
  6.5 76.0 %all-gather.2.cloned.1.call-start = ((), (), s32[]{:S(2)}) async-start(), calls=%async_computation.3 | async-start | bytes 12976128 | tf_op jit(solution)/shard_map/all_gather | solution.py:73
  12.9 1.6 copy-start.4
  14.5 1.7 copy-start.5
  90.3 32.7 %copy-start.3 = (bf16[3,8,4096]{2,1,0:T(8,128)(2,1)S(1)}, bf16[3,8,4096]{2,1,0:T(8,128)(2,1)}, u32[]{:S(2)}) copy-start(bf16[3,8,4096]{2,1,0:T(8,128)(2,1)} %param.16) | copy-start | bytes 589828
  90.3 32.9 %copy-start.6 = (f32[4096]{0:T(1024)S(1)}, f32[4096]{0:T(1024)}, u32[]{:S(2)}) copy-start(f32[4096]{0:T(1024)} %param.17) | copy-start | bytes 49156
  90.3 32.6 %all-to-all-start = ((f32[3,128,8,128]{3,2,0,1:T(8,128)}), f32[3,128,8,128]{3,2,0,1:T(8,128)S(1)}, u32[]{:S(2)}, u32[]{:S(2)}) async-start(f32[3,128,8,128]{3,2,0,1:T(8,128)} %copy.94), calls=%async_computation | async-start | bytes 3145728 | tf_op jit(solution)/shard_map/all_to_all | solution.py:78
  223.5 9.1 %copy-start.2 = (bf16[768,4096]{1,0:T(8,128)(2,1)S(1)}, bf16[768,4096]{1,0:T(8,128)(2,1)}, u32[]{:S(2)}) copy-start(bf16[768,4096]{1,0:T(8,128)(2,1)} %reshape.209) | copy-start | bytes 18874372
  260.8 5.1 %copy-start.7 = (f32[3,8,8]{2,1,0:T(8,128)S(1)}, f32[3,8,8]{2,1,0:T(8,128)}, u32[]{:S(2)}) copy-start(f32[3,8,8]{2,1,0:T(8,128)} %param.20) | copy-start | bytes 2308
  260.8 81.6 %all-to-all-start.2 = ((bf16[128,192,128]{2,1,0:T(8,128)(2,1)}), bf16[128,192,128]{2,1,0:T(8,128)(2,1)}, u32[]{:S(2)}, u32[]{:S(2)}) async-start(bf16[128,192,128]{2,1,0:T(8,128)(2,1)} %reshape.210), calls=%async_computation.2 | async-start | bytes 12582912 | tf_op jit(solution)/shard_map/all_to_all | solution.py:118
  342.4 5.4 %copy-start.1 = (bf16[2048,128]{1,0:T(8,128)(2,1)S(1)}, bf16[2048,128]{1,0:T(8,128)(2,1)}, u32[]{:S(2)}) copy-start(bf16[2048,128]{1,0:T(8,128)(2,1)} %param.18) | copy-start | bytes 1572868
Sparse Core Ops, SparseCore 0:
  16.2 66.2 all-gather.1

commit v5 on v4

--- a/solution.py
+++ b/solution.py
@@ -1,7 +1,7 @@
 import jax
 import jax.numpy as jnp
 from jax import lax
-from jax.sharding import PartitionSpec as P
+from jax.sharding import Mesh, PartitionSpec as P
 
 HEAD_SIZE = 128
 TOPK = 8
@@ -27,7 +27,9 @@
     expert_up,
     expert_down,
 ):
-    ep_count = lax.axis_size("ep")
+    x_count = lax.axis_size("x")
+    yc_count = lax.axis_size("y") * lax.axis_size("c")
+    ep_count = x_count * yc_count
     tp_count = lax.axis_size("tp")
     steps = query.shape[0]
     row_dev = query.shape[1]
@@ -70,18 +72,19 @@
     )
     attended = attended.astype(jnp.bfloat16).reshape(steps, row_dev, heads_dev * HEAD_SIZE)
 
-    gathered = lax.all_gather(attended, "ep", axis=1, tiled=True)
+    w_cols = lax.all_gather(w_out, "x", axis=1, tiled=True)
+    gathered = lax.all_gather(attended, ("y", "c"), axis=1, tiled=True)
     partial_sums = jnp.einsum(
-        "srk,kc->src", gathered, w_out, preferred_element_type=jnp.float32
+        "srk,kc->src", gathered, w_cols, preferred_element_type=jnp.float32
     )
-    grouped = partial_sums.reshape(steps, ep_count * tp_count, row_own, -1)
+    grouped = partial_sums.reshape(steps, yc_count * tp_count, row_own, -1)
     arrived_sums = lax.all_to_all(
-        grouped, ("ep", "tp"), split_axis=1, concat_axis=1, tiled=True
+        grouped, ("y", "c", "tp"), split_axis=1, concat_axis=1, tiled=True
     )
-    arrived_sums = arrived_sums.reshape(steps, ep_count, tp_count, row_own, -1)
+    arrived_sums = arrived_sums.reshape(steps, yc_count, tp_count, row_own, x_count, -1)
     summed = jnp.sum(arrived_sums, axis=2)
     projected = summed.astype(jnp.bfloat16)
-    row_major = jnp.transpose(projected, (0, 2, 1, 3)).reshape(steps, row_own, width)
+    row_major = jnp.transpose(projected, (0, 2, 3, 1, 4)).reshape(steps, row_own, width)
 
     residual = hidden_in.astype(jnp.float32) + row_major.astype(jnp.float32)
     mean_square = jnp.mean(residual * residual, axis=-1, keepdims=True)
@@ -107,7 +110,7 @@
     )
     wire_shape = (expert_count, slots_per * blocks, 128)
     outgoing = jnp.take(padded, source_row, axis=0).reshape(wire_shape)
-    arrived = lax.all_to_all(outgoing, ("ep", "tp"), split_axis=0, concat_axis=0, tiled=True)
+    arrived = lax.all_to_all(outgoing, ("x", "y", "c", "tp"), split_axis=0, concat_axis=0, tiled=True)
     flat_rows = arrived.reshape(-1, width)
     gate_act = jnp.dot(flat_rows, expert_gate[0], preferred_element_type=jnp.float32)
     up_act = jnp.dot(flat_rows, expert_up[0], preferred_element_type=jnp.float32)
@@ -116,7 +119,7 @@
         jnp.bfloat16
     )
     returned = lax.all_to_all(
-        expert_out.reshape(wire_shape), ("ep", "tp"), split_axis=0, concat_axis=0, tiled=True
+        expert_out.reshape(wire_shape), ("x", "y", "c", "tp"), split_axis=0, concat_axis=0, tiled=True
     )
     returned = returned.reshape(expert_count * slots_per, blocks, 128)
     selected = jnp.take(returned, slot_index, axis=0).astype(jnp.float32)
@@ -127,24 +130,30 @@
 
 
 def solution(mesh):
+    ep_size, tp_size = mesh.devices.shape
+    x_size = ep_size // 8
+    split_mesh = Mesh(
+        mesh.devices.reshape(x_size, ep_size // (2 * x_size), 2, tp_size), ("x", "y", "c", "tp")
+    )
+    ep = ("x", "y", "c")
     placed = (
-        P(None, "ep", "tp"),
-        P(None, None, "ep", "tp"),
-        P(None, "ep", None, "tp"),
-        P("ep"),
-        P(None, ("ep", "tp"), None),
+        P(None, ep, "tp"),
+        P(None, None, ep, "tp"),
+        P(None, ep, None, "tp"),
+        P(ep),
+        P(None, (*ep, "tp"), None),
         P(),
-        P("tp", "ep"),
-        P(None, ("ep", "tp"), None),
-        P(None, ("ep", "tp"), None),
-        P(("ep", "tp"), None, None),
-        P(("ep", "tp"), None, None),
-        P(("ep", "tp"), None, None),
+        P("tp", ep),
+        P(None, (*ep, "tp"), None),
+        P(None, (*ep, "tp"), None),
+        P((*ep, "tp"), None, None),
+        P((*ep, "tp"), None, None),
+        P((*ep, "tp"), None, None),
     )
     return jax.shard_map(
         per_device,
-        mesh=mesh,
+        mesh=split_mesh,
         in_specs=placed,
-        out_specs=P(None, ("ep", "tp"), None),
+        out_specs=P(None, (*ep, "tp"), None),
         check_vma=False,
     )

time: 359 us -> 350 us (0.975)
  waiting for transfers between devices: 165 us -> 158 us
    all_gather x1 -> x2, waiting for transfers between devices: 65.8 us -> 61.8 us  [the longest x1 32.1 us: per_device(): gathered = lax.all_gather(attended, ('y', 'c'), axis=1, tiled=True)]
    all_to_all x2, waiting for transfers between devices: 99.2 us -> 95.4 us  [the longest x1 76.1 us: per_device(): lax.all_to_all(expert_out.reshape(wire_shape), ('x', 'y', 'c', 'tp'), spl...]
  transfers between devices with their start and end apart: 3 -> 4, of which waited for: 3 -> 4; matrix products, arithmetic and copies ran while one was open for 1% -> 3% of each run, Pallas kernels for 0% -> 0%
where the time goes in v5:
time: 350 us; the launch traced here: 345 us
  waiting for transfers between devices  158 us (45%)
  blocking collectives  82.6 us (24%)
  local copies, waits for them, and re-layouts  36.2 us (10%)
  matrix products  33.6 us (10%)
  between operations  13.8 us (4%)
  starting transfers between devices  11 us (3%)
  other arithmetic  9.88 us (3%)
    all_to_all x1, blocking collectives, per_device(): lax.all_to_all(outgoing, ('x', 'y', 'c', 'tp'), split_axis=0, concat_axis...  82.6 us
    all_to_all x1, waiting for transfers between devices, per_device(): lax.all_to_all(expert_out.reshape(wire_shape), ('x', 'y', 'c', 'tp'), spl...  76.1 us
    all_gather x1, waiting for transfers between devices, per_device(): gathered = lax.all_gather(attended, ('y', 'c'), axis=1, tiled=True)  32.1 us
    all_gather x1, waiting for transfers between devices, per_device(): w_cols = lax.all_gather(w_out, 'x', axis=1, tiled=True)  29.7 us
    all_to_all x1, waiting for transfers between devices, per_device(): lax.all_to_all(grouped, ('y', 'c', 'tp'), split_axis=1, concat_axis=1, ti...  19.3 us
    reshape x1, local copies, waits for them, and re-layouts, per_device(): expert_out.reshape(wire_shape)  10.4 us
    reshape x1, local copies, waits for them, and re-layouts, per_device(): flat_rows = arrived.reshape(-1, width)  10.3 us
    dot_general x1, matrix products, per_device(): jnp.dot(hidden, expert_down[0], preferred_element_type=jnp.float32)  9.75 us
  transfers between devices with their start and end apart: 4, of which 4 were waited for; matrix products, arithmetic and copies ran while one was open for 3% of the time, Pallas kernels for 0%

profile of v5, /device:TPU:1, one launch (start us, length us, event | category | flops | bytes accessed | tf_op | source)
XLA Modules:
  0.0 345.0 jit_solution(11709251769016919157)
XLA Ops:
  6.5 0.7 all-gather.5.cloned.1.call-update
  7.3 1.1 copy.101
  8.4 0.8 fusion.35
  9.1 0.8 fusion.25
  9.9 0.1 copy.82
  10.1 0.1 fusion.34
  10.2 0.1 copy.84
  10.2 0.4 copy.83
  10.8 0.9 fusion.36
  11.7 0.6 fusion.17
  12.3 0.5 divide_convert_fusion
  12.8 0.4 fusion.18
  13.3 0.2 fusion.16
  13.6 0.9 reshape.205
  14.6 0.1 fusion.29
  14.7 0.1 reduce_window_sum.11
  14.8 0.2 select_reduce_fusion
  15.0 0.1 reduce_sum.62
  15.1 29.7 %all-gather.5.cloned.1.call-done = bf16[2048,512]{1,0:T(8,128)(2,1)} async-done(((bf16[2048,128]{1,0:T(8,128)(2,1)}), bf16[2048,512]{1,0:T(8,128)(2,1)}) %all-gather.5.cloned.1.call-update) | async-done | bytes 2097168 | tf_op jit(solution)/shard_map/all_gather | solution.py:75
  44.8 32.1 %all-gather.3.cloned.1.call-done = bf16[3,256,2048]{2,1,0:T(8,128)(2,1)} async-done(((bf16[3,32,2048]{2,1,0:T(8,128)(2,1)}), bf16[3,256,2048]{2,1,0:T(8,128)(2,1)}) %all-gather.3.cloned.1.call-update) | async-done | bytes 3145744 | tf_op jit(solution)/shard_map/all_gather | solution.py:76
  76.9 4.3 %fusion.10 = f32[3,32,8,512]{3,2,1,0:T(8,128)S(1)} fusion(bf16[3,256,2048]{2,1,0:T(8,128)(2,1)} %all-gather.3.cloned.1.call-done, bf16[2048,512]{1,0:T(8,128)(2,1)} %all-gather.5.cloned.1.call-done), kind=kOutput, calls=%fused_computation.17 | convolution fusion | flops 1610612736 | bytes 6815744 | tf_op jit(solution)/shard_map/srk,kc->src/dot_general | solution.py:77
  81.2 1.3 copy.88
  82.5 6.0 %all-to-all-start = ((f32[3,32,8,512]{3,2,0,1:T(8,128)}), f32[3,32,8,512]{3,2,0,1:T(8,128)S(1)}, u32[]{:S(2)}, u32[]{:S(2)}) async-start(f32[3,32,8,512]{3,2,0,1:T(8,128)} %copy.88), calls=%async_computation | async-start | bytes 3145728 | tf_op jit(solution)/shard_map/all_to_all | solution.py:81
  88.6 0.1 add.128
  88.7 0.1 mul.101
  88.8 0.1 reshape.234
  88.9 1.2 scatter_custom_fusion
  90.2 0.2 broadcast_in_dim.77
  90.4 0.1 copy.92
  90.6 19.3 %all-to-all-done = f32[3,32,8,512]{3,2,0,1:T(8,128)S(1)} async-done(((f32[3,32,8,512]{3,2,0,1:T(8,128)}), f32[3,32,8,512]{3,2,0,1:T(8,128)S(1)}, u32[]{:S(2)}, u32[]{:S(2)}) %all-to-all-start) | async-done | bytes 1572896 | tf_op jit(solution)/shard_map/all_to_all | solution.py:81
  109.9 0.2 reduce_sum.59
  110.1 0.2 copy.90
  110.4 0.1 multiply_reduce_fusion.1
  110.6 0.1 fusion.28
  110.8 4.4 %gather_fusion = bf16[768,32,128]{2,1,0:T(8,128)(2,1)} fusion(bf16[25,32,128]{2,1,0:T(8,128)(2,1)S(1)} %concatenate.7, s32[1024]{0:T(1024)S(1)} %pad_clamp_fusion.1), kind=kCustom, calls=%fused_computation | custom fusion | bytes 12585984 | tf_op jit(solution)/shard_map/jit(_take)/gather | solution.py:112
  115.2 5.7 %bitcast_select_fusion = bf16[128,192,128]{2,1,0:T(8,128)(2,1)S(1)} fusion(pred[128,192]{1,0:T(8,128)(4,1)S(1)} %copy.92, bf16[128,192,128]{2,1,0:T(8,128)(2,1)} %bitcast.92), kind=kLoop, calls=%fused_computation.9 | loop fusion | flops 3145728 | bytes 12607488 | tf_op jit(solution)/shard_map/jit(_take)/select_n | solution.py:112
  120.9 82.6 %all_to_all.15 = bf16[128,192,128]{2,1,0:T(8,128)(2,1)} all-to-all(bf16[128,192,128]{2,1,0:T(8,128)(2,1)S(1)} %bitcast_select_fusion), channel_id=1, replica_groups=mesh['x'=4,'y'=4,'c'=2,'tp'=4] {'x','y','c','tp'}, dimensions={0} | all-to-all | bytes 12582912 | tf_op jit(solution)/shard_map/all_to_all | solution.py:113
  203.5 10.3 %reshape.209 = bf16[768,4096]{1,0:T(8,128)(2,1)} reshape(bf16[128,192,128]{2,1,0:T(8,128)(2,1)} %all_to_all.15) | data formatting | bytes 12582912 | tf_op jit(solution)/shard_map/reshape | solution.py:114
  213.9 9.1 %fusion.3 = f32[768,768]{1,0:T(8,128)S(1)} fusion(bf16[768,4096]{1,0:T(8,128)(2,1)} %reshape.209, bf16[1,4096,768]{2,1,0:T(8,128)(2,1)} %param.21), kind=kOutput, calls=%fused_computation.7 | convolution fusion | flops 4831838208 | bytes 14942208 | tf_op jit(solution)/shard_map/dot_general | solution.py:115
  223.0 8.0 %multiply_convert_fusion = bf16[768,768]{1,0:T(8,128)(2,1)S(1)} fusion(f32[768,768]{1,0:T(8,128)S(1)} %fusion.3, bf16[768,4096]{1,0:T(8,128)(2,1)S(1)} %copy-done, bf16[1,4096,768]{2,1,0:T(8,128)(2,1)} %param.22), kind=kOutput, calls=%fused_computation.11 | convolution fusion | flops 4835377152 | bytes 16121856 | tf_op jit(solution)/shard_map/dot_general | solution.py:116
  231.0 9.7 %convolution_convert_fusion = bf16[768,4096]{1,0:T(8,128)(2,1)} fusion(bf16[768,768]{1,0:T(8,128)(2,1)S(1)} %multiply_convert_fusion, bf16[1,768,4096]{2,1,0:T(8,128)(2,1)} %param.23), kind=kOutput, calls=%fused_computation.3 | convolution fusion | flops 4834983936 | bytes 13762560 | tf_op jit(solution)/shard_map/dot_general | solution.py:118
  240.7 10.4 %reshape.210 = bf16[128,192,128]{2,1,0:T(8,128)(2,1)} reshape(bf16[768,4096]{1,0:T(8,128)(2,1)} %convolution_convert_fusion) | data formatting | bytes 12582912 | tf_op jit(solution)/shard_map/reshape | solution.py:122
  251.2 5.0 %all-to-all-start.2 = ((bf16[128,192,128]{2,1,0:T(8,128)(2,1)}), bf16[128,192,128]{2,1,0:T(8,128)(2,1)}, u32[]{:S(2)}, u32[]{:S(2)}) async-start(bf16[128,192,128]{2,1,0:T(8,128)(2,1)} %reshape.210), calls=%async_computation.2 | async-start | bytes 12582912 | tf_op jit(solution)/shard_map/all_to_all | solution.py:121
  256.3 0.3 fusion.31
  256.7 76.1 %all-to-all-done.2 = bf16[128,192,128]{2,1,0:T(8,128)(2,1)} async-done(((bf16[128,192,128]{2,1,0:T(8,128)(2,1)}), bf16[128,192,128]{2,1,0:T(8,128)(2,1)}, u32[]{:S(2)}, u32[]{:S(2)}) %all-to-all-start.2) | async-done | bytes 6291488 | tf_op jit(solution)/shard_map/all_to_all | solution.py:121
  332.8 3.7 %gather_fusion.1 = bf16[192,32,128]{2,1,0:T(8,128)(2,1)S(1)} fusion(bf16[768,32,128]{2,1,0:T(8,128)(2,1)} %bitcast.25, s32[1024]{0:T(1024)S(1)} %pad_clamp_fusion), kind=kCustom, calls=%fused_computation.1 | custom fusion | bytes 3146496 | tf_op jit(solution)/shard_map/jit(_take)/gather | solution.py:125
  336.5 0.9 multiply_reduce_fusion
  337.4 0.7 add_convert_fusion
  (43 shorter events, 1.0 us)
Async XLA Ops:
  6.5 4.1 %copy-start.5 = (s32[32]{0:T(128)S(1)}, s32[32]{0:T(128)}, u32[]{:S(2)}) copy-start(s32[32]{0:T(128)} %param.15) | copy-start | bytes 388
  6.5 4.2 %copy-start.2 = (bf16[2,32,128,128]{3,2,1,0:T(8,128)(2,1)S(1)}, bf16[2,32,128,128]{3,2,1,0:T(8,128)(2,1)}, u32[]{:S(2)}) copy-start(bf16[2,32,128,128]{3,2,1,0:T(8,128)(2,1)} %param.14) | copy-start | bytes 6291460
  6.5 38.2 %all-gather.5.cloned.1.call-start = ((), (), s32[]{:S(2)}) async-start(), calls=%async_computation.4 | async-start | bytes 2621440 | tf_op jit(solution)/shard_map/all_gather | solution.py:75
  7.3 69.7 %all-gather.3.cloned.1.call-start = ((), (), s32[]{:S(2)}) async-start(), calls=%async_computation.3 | async-start | bytes 3538944 | tf_op jit(solution)/shard_map/all_gather | solution.py:76
  12.8 1.7 copy-start.3
  82.5 27.4 %all-to-all-start = ((f32[3,32,8,512]{3,2,0,1:T(8,128)}), f32[3,32,8,512]{3,2,0,1:T(8,128)S(1)}, u32[]{:S(2)}, u32[]{:S(2)}) async-start(f32[3,32,8,512]{3,2,0,1:T(8,128)} %copy.88), calls=%async_computation | async-start | bytes 3145728 | tf_op jit(solution)/shard_map/all_to_all | solution.py:81
  88.5 21.9 %copy-start.1 = (bf16[3,8,4096]{2,1,0:T(8,128)(2,1)S(1)}, bf16[3,8,4096]{2,1,0:T(8,128)(2,1)}, u32[]{:S(2)}) copy-start(bf16[3,8,4096]{2,1,0:T(8,128)(2,1)} %param.16) | copy-start | bytes 589828
  88.7 21.9 %copy-start.4 = (f32[4096]{0:T(1024)S(1)}, f32[4096]{0:T(1024)}, u32[]{:S(2)}) copy-start(f32[4096]{0:T(1024)} %param.17) | copy-start | bytes 49156
  213.9 9.1 %copy-start = (bf16[768,4096]{1,0:T(8,128)(2,1)S(1)}, bf16[768,4096]{1,0:T(8,128)(2,1)}, u32[]{:S(2)}) copy-start(bf16[768,4096]{1,0:T(8,128)(2,1)} %reshape.209) | copy-start | bytes 18874372
  251.2 5.1 %copy-start.6 = (f32[3,8,8]{2,1,0:T(8,128)S(1)}, f32[3,8,8]{2,1,0:T(8,128)}, u32[]{:S(2)}) copy-start(f32[3,8,8]{2,1,0:T(8,128)} %param.20) | copy-start | bytes 2308
  251.2 81.6 %all-to-all-start.2 = ((bf16[128,192,128]{2,1,0:T(8,128)(2,1)}), bf16[128,192,128]{2,1,0:T(8,128)(2,1)}, u32[]{:S(2)}, u32[]{:S(2)}) async-start(bf16[128,192,128]{2,1,0:T(8,128)(2,1)} %reshape.210), calls=%async_computation.2 | async-start | bytes 12582912 | tf_op jit(solution)/shard_map/all_to_all | solution.py:121
Sparse Core Ops, SparseCore 0:
  9.0 35.7 all-gather.4
  46.5 30.4 all-gather.2

commit v6 on v5

--- a/solution.py
+++ b/solution.py
@@ -72,7 +72,14 @@
     )
     attended = attended.astype(jnp.bfloat16).reshape(steps, row_dev, heads_dev * HEAD_SIZE)
 
-    w_cols = lax.all_gather(w_out, "x", axis=1, tiled=True)
+    x_here = lax.axis_index("x")
+    shifted = [w_out] + [
+        lax.ppermute(w_out, "x", [(i, (i + k) % x_count) for i in range(x_count)])
+        for k in range(1, x_count)
+    ]
+    order = (x_here - jnp.arange(x_count, dtype=jnp.int32)) % x_count
+    w_cols = jnp.take(jnp.stack(shifted), order, axis=0)
+    w_cols = jnp.transpose(w_cols, (1, 0, 2)).reshape(w_out.shape[0], -1)
     gathered = lax.all_gather(attended, ("y", "c"), axis=1, tiled=True)
     partial_sums = jnp.einsum(
         "srk,kc->src", gathered, w_cols, preferred_element_type=jnp.float32

time: 350 us -> 327 us (0.934)
  waiting for transfers between devices: 158 us -> 116 us
  starting transfers between devices: 11 us -> 20.4 us
  local copies, waits for them, and re-layouts: 36.2 us -> 40.9 us
  other arithmetic: 9.88 us -> 13.9 us
    all_gather x1, waiting for transfers between devices: 32.1 us -> 0.01 us  [per_device(): gathered = lax.all_gather(attended, ('y', 'c'), axis=1, tiled=True)]
    all_gather x1 -> x0, waiting for transfers between devices: 29.7 us -> none  [per_device(): w_cols = lax.all_gather(w_out, 'x', axis=1, tiled=True)]
    ppermute x0 -> x3, waiting for transfers between devices: none -> 20.8 us  [per_device(): lax.ppermute(w_out, 'x', [(i, (i + k) % x_count) for i in range(x_count)])]
    ppermute x0 -> x3, starting transfers between devices: none -> 5.7 us  [per_device(): lax.ppermute(w_out, 'x', [(i, (i + k) % x_count) for i in range(x_count)])]
    all_to_all x1, starting transfers between devices: 5.96 us -> 9.64 us  [per_device(): lax.all_to_all(grouped, ('y', 'c', 'tp'), split_axis=1, concat_axis=1, ti...]
  transfers between devices with their start and end apart: 4 -> 6, of which waited for: 4 -> 4; matrix products, arithmetic and copies ran while one was open for 3% -> 4% of each run, Pallas kernels for 0% -> 0%
where the time goes in v6:
time: 327 us; the launch traced here: 322 us
  waiting for transfers between devices  116 us (35%)
  blocking collectives  82.1 us (25%)
  local copies, waits for them, and re-layouts  40.9 us (13%)
  matrix products  34.8 us (11%)
  starting transfers between devices  20.4 us (6%)
  other arithmetic  13.9 us (4%)
  between operations  13.8 us (4%)
    all_to_all x1, blocking collectives, per_device(): lax.all_to_all(outgoing, ('x', 'y', 'c', 'tp'), split_axis=0, concat_axis...  82.1 us
    all_to_all x1, waiting for transfers between devices, per_device(): lax.all_to_all(expert_out.reshape(wire_shape), ('x', 'y', 'c', 'tp'), spl...  76.1 us
    ppermute x3, waiting for transfers between devices, per_device(): lax.ppermute(w_out, 'x', [(i, (i + k) % x_count) for i in range(x_count)])  20.8 us
    all_to_all x1, waiting for transfers between devices, per_device(): lax.all_to_all(grouped, ('y', 'c', 'tp'), split_axis=1, concat_axis=1, ti...  19.3 us
    reshape x1, local copies, waits for them, and re-layouts, per_device(): expert_out.reshape(wire_shape)  10.4 us
    reshape x1, local copies, waits for them, and re-layouts, per_device(): flat_rows = arrived.reshape(-1, width)  10.3 us
    dot_general x1, matrix products, per_device(): jnp.dot(hidden, expert_down[0], preferred_element_type=jnp.float32)  9.74 us
    all_to_all x1, starting transfers between devices, per_device(): lax.all_to_all(grouped, ('y', 'c', 'tp'), split_axis=1, concat_axis=1, ti...  9.64 us
  transfers between devices with their start and end apart: 6, of which 4 were waited for; matrix products, arithmetic and copies ran while one was open for 4% of the time, Pallas kernels for 0%

profile of v6, /device:TPU:1, one launch (start us, length us, event | category | flops | bytes accessed | tf_op | source)
XLA Modules:
  0.0 322.1 jit_solution(16264182608803970640)
XLA Ops:
  6.5 1.2 copy.128
  7.8 0.8 fusion.35
  8.5 0.8 fusion.22
  9.6 0.7 iota_compare_fusion.1
  10.4 0.4 copy.103
  10.8 0.9 fusion.36
  11.8 0.6 fusion.14
  12.4 0.5 divide_convert_fusion
  12.9 0.4 fusion.15
  13.3 0.2 fusion.13
  13.6 0.9 reshape.261
  14.5 2.1 collective-permute-start
  16.6 2.5 collective-permute-start.1
  19.1 1.2 collective-permute-start.2
  20.4 0.1 reduce_window_sum.11
  20.6 0.2 select_reduce_fusion
  20.9 8.3 %collective-permute-done = bf16[2048,128]{1,0:T(8,128)(2,1)S(1)} collective-permute-done((bf16[2048,128]{1,0:T(8,128)(2,1)S(1)}, bf16[2048,128]{1,0:T(8,128)(2,1)S(1)}, u32[]{:S(2)}, u32[]{:S(2)}) %collective-permute-start) | collective-permute-done | bytes 524320 | tf_op jit(solution)/shard_map/ppermute | solution.py:77
  29.2 12.5 %collective-permute-done.1 = bf16[2048,128]{1,0:T(8,128)(2,1)S(1)} collective-permute-done((bf16[2048,128]{1,0:T(8,128)(2,1)S(1)}, bf16[2048,128]{1,0:T(8,128)(2,1)S(1)}, u32[]{:S(2)}, u32[]{:S(2)}) %collective-permute-start.1) | collective-permute-done | bytes 524320 | tf_op jit(solution)/shard_map/ppermute | solution.py:77
  41.7 0.8 copy-done.5
  42.5 0.2 copy-done.6
  42.6 1.5 pad_maximum_fusion
  44.1 2.2 gather_fusion
  46.3 1.9 select_bitcast_fusion
  48.2 2.7 copy.108
  50.9 5.6 %fusion.5 = f32[3,32,8,512]{3,2,0,1:T(8,128)} fusion(bf16[2048,512,1,1]{0,1,2,3:T(8,128)(2,1)} %bitcast.105, bf16[3,256,2048]{2,1,0:T(8,128)(2,1)} %all-gather.2.cloned.1.call-done), kind=kOutput, calls=%fused_computation.11 | convolution fusion | flops 1610612736 | bytes 6815744 | tf_op jit(solution)/shard_map/srk,kc->src/dot_general | solution.py:84
  56.5 9.6 %all-to-all-start = ((f32[3,32,8,512]{3,2,0,1:T(8,128)}), f32[3,32,8,512]{3,2,0,1:T(8,128)S(1)}, u32[]{:S(2)}, u32[]{:S(2)}) async-start(f32[3,32,8,512]{3,2,0,1:T(8,128)} %fusion.5), calls=%async_computation | async-start | bytes 3145728 | tf_op jit(solution)/shard_map/all_to_all | solution.py:88
  66.6 1.2 scatter_custom_fusion
  67.8 0.2 broadcast_in_dim.89
  68.1 0.1 copy.114
  68.2 19.3 %all-to-all-done = f32[3,32,8,512]{3,2,0,1:T(8,128)S(1)} async-done(((f32[3,32,8,512]{3,2,0,1:T(8,128)}), f32[3,32,8,512]{3,2,0,1:T(8,128)S(1)}, u32[]{:S(2)}, u32[]{:S(2)}) %all-to-all-start) | async-done | bytes 1572896 | tf_op jit(solution)/shard_map/all_to_all | solution.py:88
  87.5 0.2 reduce_sum.59
  87.7 0.2 copy.112
  88.0 0.1 multiply_reduce_fusion.1
  88.2 0.1 fusion.25
  88.4 4.4 %gather_fusion.1 = bf16[768,32,128]{2,1,0:T(8,128)(2,1)} fusion(bf16[25,32,128]{2,1,0:T(8,128)(2,1)S(1)} %concatenate.7, s32[1024]{0:T(1024)S(1)} %pad_clamp_fusion.1), kind=kCustom, calls=%fused_computation.1 | custom fusion | bytes 12585984 | tf_op jit(solution)/shard_map/jit(_take)/gather | solution.py:119
  92.8 5.7 %bitcast_select_fusion = bf16[128,192,128]{2,1,0:T(8,128)(2,1)S(1)} fusion(pred[128,192]{1,0:T(8,128)(4,1)S(1)} %copy.114, bf16[128,192,128]{2,1,0:T(8,128)(2,1)} %bitcast.102), kind=kLoop, calls=%fused_computation.10 | loop fusion | flops 3145728 | bytes 12607488 | tf_op jit(solution)/shard_map/jit(_take)/select_n | solution.py:119
  98.5 82.1 %all_to_all.15 = bf16[128,192,128]{2,1,0:T(8,128)(2,1)} all-to-all(bf16[128,192,128]{2,1,0:T(8,128)(2,1)S(1)} %bitcast_select_fusion), channel_id=1, replica_groups=mesh['x'=4,'y'=4,'c'=2,'tp'=4] {'x','y','c','tp'}, dimensions={0} | all-to-all | bytes 12582912 | tf_op jit(solution)/shard_map/all_to_all | solution.py:120
  180.6 10.3 %reshape.265 = bf16[768,4096]{1,0:T(8,128)(2,1)} reshape(bf16[128,192,128]{2,1,0:T(8,128)(2,1)} %all_to_all.15) | data formatting | bytes 12582912 | tf_op jit(solution)/shard_map/reshape | solution.py:121
  191.0 9.1 %fusion.3 = f32[768,768]{1,0:T(8,128)S(1)} fusion(bf16[768,4096]{1,0:T(8,128)(2,1)} %reshape.265, bf16[1,4096,768]{2,1,0:T(8,128)(2,1)} %param.21), kind=kOutput, calls=%fused_computation.8 | convolution fusion | flops 4831838208 | bytes 14942208 | tf_op jit(solution)/shard_map/dot_general | solution.py:122
  200.1 8.0 %multiply_convert_fusion = bf16[768,768]{1,0:T(8,128)(2,1)S(1)} fusion(f32[768,768]{1,0:T(8,128)S(1)} %fusion.3, bf16[768,4096]{1,0:T(8,128)(2,1)S(1)} %copy-done, bf16[1,4096,768]{2,1,0:T(8,128)(2,1)} %param.22), kind=kOutput, calls=%fused_computation.14 | convolution fusion | flops 4835377152 | bytes 16121856 | tf_op jit(solution)/shard_map/dot_general | solution.py:123
  208.1 9.7 %convolution_convert_fusion = bf16[768,4096]{1,0:T(8,128)(2,1)} fusion(bf16[768,768]{1,0:T(8,128)(2,1)S(1)} %multiply_convert_fusion, bf16[1,768,4096]{2,1,0:T(8,128)(2,1)} %param.23), kind=kOutput, calls=%fused_computation.4 | convolution fusion | flops 4834983936 | bytes 13762560 | tf_op jit(solution)/shard_map/dot_general | solution.py:125
  217.9 10.4 %reshape.266 = bf16[128,192,128]{2,1,0:T(8,128)(2,1)} reshape(bf16[768,4096]{1,0:T(8,128)(2,1)} %convolution_convert_fusion) | data formatting | bytes 12582912 | tf_op jit(solution)/shard_map/reshape | solution.py:129
  228.3 5.0 %all-to-all-start.2 = ((bf16[128,192,128]{2,1,0:T(8,128)(2,1)}), bf16[128,192,128]{2,1,0:T(8,128)(2,1)}, u32[]{:S(2)}, u32[]{:S(2)}) async-start(bf16[128,192,128]{2,1,0:T(8,128)(2,1)} %reshape.266), calls=%async_computation.2 | async-start | bytes 12582912 | tf_op jit(solution)/shard_map/all_to_all | solution.py:128
  233.4 0.3 fusion.28
  233.8 76.1 %all-to-all-done.2 = bf16[128,192,128]{2,1,0:T(8,128)(2,1)} async-done(((bf16[128,192,128]{2,1,0:T(8,128)(2,1)}), bf16[128,192,128]{2,1,0:T(8,128)(2,1)}, u32[]{:S(2)}, u32[]{:S(2)}) %all-to-all-start.2) | async-done | bytes 6291488 | tf_op jit(solution)/shard_map/all_to_all | solution.py:128
  309.9 3.7 %gather_fusion.2 = bf16[192,32,128]{2,1,0:T(8,128)(2,1)S(1)} fusion(bf16[768,32,128]{2,1,0:T(8,128)(2,1)} %bitcast.32, s32[1024]{0:T(1024)S(1)} %pad_clamp_fusion), kind=kCustom, calls=%fused_computation.2 | custom fusion | bytes 3146496 | tf_op jit(solution)/shard_map/jit(_take)/gather | solution.py:132
  313.6 0.9 multiply_reduce_fusion
  314.6 0.7 add_convert_fusion
  (58 shorter events, 1.7 us)
Async XLA Ops:
  6.5 4.3 %copy-start.2 = (bf16[2,32,128,128]{3,2,1,0:T(8,128)(2,1)S(1)}, bf16[2,32,128,128]{3,2,1,0:T(8,128)(2,1)}, u32[]{:S(2)}) copy-start(bf16[2,32,128,128]{3,2,1,0:T(8,128)(2,1)} %param.14) | copy-start | bytes 6291460
  6.5 44.3 %all-gather.2.cloned.1.call-start = ((), (), s32[]{:S(2)}) async-start(), calls=%async_computation.3 | async-start | bytes 3538944 | tf_op jit(solution)/shard_map/all_gather | solution.py:83
  12.9 1.7 copy-start.3
  12.9 7.4 %copy-start.7 = (s32[3,8,8]{2,1,0:T(8,128)S(1)}, s32[3,8,8]{2,1,0:T(8,128)}, u32[]{:S(2)}) copy-start(s32[3,8,8]{2,1,0:T(8,128)} %param.19) | copy-start | bytes 2308
  13.3 29.3 %copy-start.4 = (bf16[2048,128]{1,0:T(8,128)(2,1)S(1)}, bf16[2048,128]{1,0:T(8,128)(2,1)}, u32[]{:S(2)}) copy-start(bf16[2048,128]{1,0:T(8,128)(2,1)} %param.18) | copy-start | bytes 1572868
  14.5 14.6 %collective-permute-start = (bf16[2048,128]{1,0:T(8,128)(2,1)S(1)}, bf16[2048,128]{1,0:T(8,128)(2,1)S(1)}, u32[]{:S(2)}, u32[]{:S(2)}) collective-permute-start(bf16[2048,128]{1,0:T(8,128)(2,1)S(1)} %copy-done.3), channel_id=1, source_target_pairs={{0,32},{32,64},{64,96},{96,0},{1,33},{33,65},{65,97},{97,1},{2,34}... | collective-permute-start | bytes 1572872 | tf_op jit(solution)/shard_map/ppermute | solution.py:77
  16.6 25.0 %collective-permute-start.1 = (bf16[2048,128]{1,0:T(8,128)(2,1)S(1)}, bf16[2048,128]{1,0:T(8,128)(2,1)S(1)}, u32[]{:S(2)}, u32[]{:S(2)}) collective-permute-start(bf16[2048,128]{1,0:T(8,128)(2,1)S(1)} %copy-done.3), channel_id=1, source_target_pairs={{0,64},{32,96},{64,0},{96,32},{1,65},{33,97},{65,1},{97,33},{2,66}... | collective-permute-start | bytes 1572872 | tf_op jit(solution)/shard_map/ppermute | solution.py:77
  19.1 22.6 %collective-permute-start.2 = (bf16[2048,128]{1,0:T(8,128)(2,1)S(1)}, bf16[2048,128]{1,0:T(8,128)(2,1)S(1)}, u32[]{:S(2)}, u32[]{:S(2)}) collective-permute-start(bf16[2048,128]{1,0:T(8,128)(2,1)S(1)} %copy-done.3), channel_id=1, source_target_pairs={{0,96},{32,0},{64,32},{96,64},{1,97},{33,1},{65,33},{97,65},{2,98}... | collective-permute-start | bytes 1572872 | tf_op jit(solution)/shard_map/ppermute | solution.py:77
  41.7 0.8 copy-start.5
  41.7 1.0 copy-start.6
  56.5 31.0 %all-to-all-start = ((f32[3,32,8,512]{3,2,0,1:T(8,128)}), f32[3,32,8,512]{3,2,0,1:T(8,128)S(1)}, u32[]{:S(2)}, u32[]{:S(2)}) async-start(f32[3,32,8,512]{3,2,0,1:T(8,128)} %fusion.5), calls=%async_computation | async-start | bytes 3145728 | tf_op jit(solution)/shard_map/all_to_all | solution.py:88
  66.1 21.9 %copy-start.1 = (bf16[3,8,4096]{2,1,0:T(8,128)(2,1)S(1)}, bf16[3,8,4096]{2,1,0:T(8,128)(2,1)}, u32[]{:S(2)}) copy-start(bf16[3,8,4096]{2,1,0:T(8,128)(2,1)} %param.16) | copy-start | bytes 589828
  66.3 21.9 %copy-start.8 = (f32[4096]{0:T(1024)S(1)}, f32[4096]{0:T(1024)}, u32[]{:S(2)}) copy-start(f32[4096]{0:T(1024)} %param.17) | copy-start | bytes 49156
  191.0 9.1 %copy-start = (bf16[768,4096]{1,0:T(8,128)(2,1)S(1)}, bf16[768,4096]{1,0:T(8,128)(2,1)}, u32[]{:S(2)}) copy-start(bf16[768,4096]{1,0:T(8,128)(2,1)} %reshape.265) | copy-start | bytes 18874372
  228.3 5.1 %copy-start.9 = (f32[3,8,8]{2,1,0:T(8,128)S(1)}, f32[3,8,8]{2,1,0:T(8,128)}, u32[]{:S(2)}) copy-start(f32[3,8,8]{2,1,0:T(8,128)} %param.20) | copy-start | bytes 2308
  228.3 81.6 %all-to-all-start.2 = ((bf16[128,192,128]{2,1,0:T(8,128)(2,1)}), bf16[128,192,128]{2,1,0:T(8,128)(2,1)}, u32[]{:S(2)}, u32[]{:S(2)}) async-start(bf16[128,192,128]{2,1,0:T(8,128)(2,1)} %reshape.266), calls=%async_computation.2 | async-start | bytes 12582912 | tf_op jit(solution)/shard_map/all_to_all | solution.py:128
Sparse Core Ops, SparseCore 0:
  14.7 31.2 all-gather.1

commit v7 on v6

--- a/solution.py
+++ b/solution.py
@@ -78,7 +78,7 @@
         for k in range(1, x_count)
     ]
     order = (x_here - jnp.arange(x_count, dtype=jnp.int32)) % x_count
-    w_cols = jnp.take(jnp.stack(shifted), order, axis=0)
+    w_cols = jnp.take(jnp.stack(shifted), order, axis=0, mode="clip")
     w_cols = jnp.transpose(w_cols, (1, 0, 2)).reshape(w_out.shape[0], -1)
     gathered = lax.all_gather(attended, ("y", "c"), axis=1, tiled=True)
     partial_sums = jnp.einsum(
@@ -115,21 +115,34 @@
     padded = jnp.concatenate(
         [normed.reshape(steps * row_own, blocks, 128), jnp.zeros((1, blocks, 128), jnp.bfloat16)]
     )
-    wire_shape = (expert_count, slots_per * blocks, 128)
-    outgoing = jnp.take(padded, source_row, axis=0).reshape(wire_shape)
-    arrived = lax.all_to_all(outgoing, ("x", "y", "c", "tp"), split_axis=0, concat_axis=0, tiled=True)
-    flat_rows = arrived.reshape(-1, width)
-    gate_act = jnp.dot(flat_rows, expert_gate[0], preferred_element_type=jnp.float32)
-    up_act = jnp.dot(flat_rows, expert_up[0], preferred_element_type=jnp.float32)
-    hidden = (jax.nn.silu(gate_act) * up_act).astype(jnp.bfloat16)
-    expert_out = jnp.dot(hidden, expert_down[0], preferred_element_type=jnp.float32).astype(
-        jnp.bfloat16
-    )
-    returned = lax.all_to_all(
-        expert_out.reshape(wire_shape), ("x", "y", "c", "tp"), split_axis=0, concat_axis=0, tiled=True
-    )
-    returned = returned.reshape(expert_count * slots_per, blocks, 128)
-    selected = jnp.take(returned, slot_index, axis=0).astype(jnp.float32)
+    source_by_step = source_row.reshape(expert_count, steps, capacity)
+    chunks = ((0, steps - 1), (steps - 1, steps)) if steps > 1 else ((0, steps),)
+    group = ("x", "y", "c", "tp")
+    picked = []
+    for first, last in chunks:
+        span = (last - first) * capacity
+        wire_shape = (expert_count, span * blocks, 128)
+        chunk_rows = source_by_step[:, first:last].reshape(-1)
+        outgoing = jnp.take(padded, chunk_rows, axis=0, mode="clip").reshape(wire_shape)
+        arrived = lax.all_to_all(outgoing, group, split_axis=0, concat_axis=0, tiled=True)
+        flat_rows = arrived.reshape(-1, width)
+        gate_act = jnp.dot(flat_rows, expert_gate[0], preferred_element_type=jnp.float32)
+        up_act = jnp.dot(flat_rows, expert_up[0], preferred_element_type=jnp.float32)
+        hidden = (jax.nn.silu(gate_act) * up_act).astype(jnp.bfloat16)
+        expert_out = jnp.dot(
+            hidden, expert_down[0], preferred_element_type=jnp.float32
+        ).astype(jnp.bfloat16)
+        returned = lax.all_to_all(
+            expert_out.reshape(wire_shape), group, split_axis=0, concat_axis=0, tiled=True
+        )
+        returned = returned.reshape(expert_count * span, blocks, 128)
+        local_slot = (
+            expert_ids[first:last] * span
+            + (step_ids[first:last] - first) * capacity
+            + slot_rank[first:last]
+        ).reshape(-1)
+        picked.append(jnp.take(returned, local_slot, axis=0, mode="clip"))
+    selected = jnp.concatenate(picked).astype(jnp.float32)
     selected = selected * weights.reshape(-1)[:, None, None]
     expert_mix = jnp.sum(selected.reshape(steps, row_own, TOPK, blocks, 128), axis=2)
     expert_mix = expert_mix.reshape(steps, row_own, width)

time: 327 us -> 304 us (0.930)
  blocking collectives: 82.1 us -> 0 us
  waiting for transfers between devices: 116 us -> 147 us
  starting transfers between devices: 20.4 us -> 40.9 us
  matrix products: 34.8 us -> 49.8 us
  other arithmetic: 13.9 us -> 6.24 us
    all_to_all x1 -> x0, blocking collectives: 82.1 us -> none  [per_device(): lax.all_to_all(outgoing, ('x', 'y', 'c', 'tp'), split_axis=0, concat_axis...]
    all_to_all x1 -> x4, waiting for transfers between devices: 76.1 us -> 107 us  [the longest x2 56.5 us: per_device(): lax.all_to_all(outgoing, group, split_axis=0, concat_axis=0, tiled=True)]
    all_to_all x1 -> x4, starting transfers between devices: 5.02 us -> 25.6 us  [the longest x2 14.2 us: per_device(): lax.all_to_all(expert_out.reshape(wire_shape), group, split_axis=0, conca...]
    dot_general x1 -> x2, matrix products: 9.74 us -> 27.8 us  [per_device(): jnp.dot(hidden, expert_down[0], preferred_element_type=jnp.float32)]
    dot_general x1 -> x0, matrix products: 8.01 us -> none  [per_device(): jnp.dot(flat_rows, expert_up[0], preferred_element_type=jnp.float32)]
    select_n x5 -> x2, other arithmetic: 7.52 us -> 0.02 us  [the longest x1 0.01 us: per_device(): order = (x_here - jnp.arange(x_count, dtype=jnp.int32)) % x_count]
    dot_general x1 -> x2, matrix products: 9.11 us -> 14.8 us  [per_device(): jnp.dot(flat_rows, expert_gate[0], preferred_element_type=jnp.float32)]
    gather x3 -> x5, local copies, waits for them, and re-layouts: 10.3 us -> 11.5 us  [the longest x2 5.76 us: per_device(): jnp.take(padded, chunk_rows, axis=0, mode='clip').reshape(wire_shape)]
  transfers between devices with their start and end apart: 6 -> 9, of which waited for: 4 -> 6; matrix products, arithmetic and copies ran while one was open for 4% -> 26% of each run, Pallas kernels for 0% -> 0%
where the time goes in v7:
time: 304 us; the launch traced here: 302 us
  waiting for transfers between devices  147 us (48%)
  matrix products  49.8 us (16%)
  local copies, waits for them, and re-layouts  43.9 us (14%)
  starting transfers between devices  40.9 us (13%)
  between operations  14.4 us (5%)
  other arithmetic  6.24 us (2%)
    all_to_all x2, waiting for transfers between devices, per_device(): lax.all_to_all(outgoing, group, split_axis=0, concat_axis=0, tiled=True)  56.5 us
    all_to_all x2, waiting for transfers between devices, per_device(): lax.all_to_all(expert_out.reshape(wire_shape), group, split_axis=0, conca...  50.4 us
    dot_general x2, matrix products, per_device(): jnp.dot(hidden, expert_down[0], preferred_element_type=jnp.float32)  27.8 us
    ppermute x3, waiting for transfers between devices, per_device(): lax.ppermute(w_out, 'x', [(i, (i + k) % x_count) for i in range(x_count)])  21.3 us
    all_to_all x1, waiting for transfers between devices, per_device(): lax.all_to_all(grouped, ('y', 'c', 'tp'), split_axis=1, concat_axis=1, ti...  18.7 us
    dot_general x2, matrix products, per_device(): jnp.dot(flat_rows, expert_gate[0], preferred_element_type=jnp.float32)  14.8 us
    all_to_all x2, starting transfers between devices, per_device(): lax.all_to_all(expert_out.reshape(wire_shape), group, split_axis=0, conca...  14.2 us
    reshape x2, local copies, waits for them, and re-layouts, per_device(): expert_out.reshape(wire_shape)  11.6 us
  transfers between devices with their start and end apart: 9, of which 6 were waited for; matrix products, arithmetic and copies ran while one was open for 26% of the time, Pallas kernels for 0%

profile of v7, /device:TPU:1, one launch (start us, length us, event | category | flops | bytes accessed | tf_op | source)
XLA Modules:
  0.0 302.3 jit_solution(2467947340433030158)
XLA Ops:
  6.5 1.2 copy.114
  7.8 0.8 fusion.61
  8.5 0.8 fusion.47
  9.6 0.7 iota_compare_fusion.1
  10.4 0.4 copy.91
  10.8 0.9 fusion.62
  11.8 0.6 fusion.34
  12.4 0.5 divide_convert_fusion
  12.9 0.4 fusion.35
  13.3 0.2 fusion.33
  13.6 0.9 reshape.275
  14.5 2.1 collective-permute-start
  16.6 2.5 collective-permute-start.1
  19.1 1.2 collective-permute-start.2
  20.4 8.8 %collective-permute-done = bf16[2048,128]{1,0:T(8,128)(2,1)S(1)} collective-permute-done((bf16[2048,128]{1,0:T(8,128)(2,1)S(1)}, bf16[2048,128]{1,0:T(8,128)(2,1)S(1)}, u32[]{:S(2)}, u32[]{:S(2)}) %collective-permute-start) | collective-permute-done | bytes 524320 | tf_op jit(solution)/shard_map/ppermute | solution.py:77
  29.2 12.5 %collective-permute-done.1 = bf16[2048,128]{1,0:T(8,128)(2,1)S(1)} collective-permute-done((bf16[2048,128]{1,0:T(8,128)(2,1)S(1)}, bf16[2048,128]{1,0:T(8,128)(2,1)S(1)}, u32[]{:S(2)}, u32[]{:S(2)}) %collective-permute-start.1) | collective-permute-done | bytes 524320 | tf_op jit(solution)/shard_map/ppermute | solution.py:77
  41.7 0.8 copy-done.4
  42.6 1.5 pad_maximum_fusion
  44.1 2.2 gather_fusion
  46.3 2.9 copy.96
  49.2 4.8 %fusion.19 = f32[3,32,8,512]{3,2,0,1:T(8,128)} fusion(bf16[2048,512,1,1]{0,1,2,3:T(8,128)(2,1)S(1)} %bitcast.130, bf16[3,256,2048]{2,1,0:T(8,128)(2,1)} %all-gather.2.cloned.1.call-done), kind=kOutput, calls=%fused_computation.22 | convolution fusion | flops 1610612736 | bytes 6815744 | tf_op jit(solution)/shard_map/srk,kc->src/dot_general | solution.py:84
  54.1 9.6 %all-to-all-start = ((f32[3,32,8,512]{3,2,0,1:T(8,128)}), f32[3,32,8,512]{3,2,0,1:T(8,128)S(1)}, u32[]{:S(2)}, u32[]{:S(2)}) async-start(f32[3,32,8,512]{3,2,0,1:T(8,128)} %fusion.19), calls=%async_computation | async-start | bytes 3145728 | tf_op jit(solution)/shard_map/all_to_all | solution.py:88
  64.7 1.2 scatter_custom_fusion
  66.5 18.7 %all-to-all-done = f32[3,32,8,512]{3,2,0,1:T(8,128)S(1)} async-done(((f32[3,32,8,512]{3,2,0,1:T(8,128)}), f32[3,32,8,512]{3,2,0,1:T(8,128)S(1)}, u32[]{:S(2)}, u32[]{:S(2)}) %all-to-all-start) | async-done | bytes 1572896 | tf_op jit(solution)/shard_map/all_to_all | solution.py:88
  85.4 0.2 copy.100
  86.0 2.2 gather_fusion.3
  88.2 6.5 %all-to-all-start.3 = ((bf16[128,64,128]{2,1,0:T(8,128)(2,1)}), bf16[128,64,128]{2,1,0:T(8,128)(2,1)S(1)}, u32[]{:S(2)}, u32[]{:S(2)}) async-start(bf16[128,64,128]{2,1,0:T(8,128)(2,1)} %bitcast.33), calls=%async_computation.3 | async-start | bytes 4194304 | tf_op jit(solution)/shard_map/all_to_all | solution.py:127
  95.0 3.5 %gather_fusion.1 = bf16[512,32,128]{2,1,0:T(8,128)(2,1)} fusion(bf16[25,32,128]{2,1,0:T(8,128)(2,1)S(1)} %concatenate.10, s32[1024]{0:T(1024)S(1)} %pad_clamp_fusion.3), kind=kCustom, calls=%fused_computation.1 | custom fusion | bytes 8390656 | tf_op jit(solution)/shard_map/jit(_take)/gather | solution.py:126
  98.6 27.0 %all-to-all-done.3 = bf16[128,64,128]{2,1,0:T(8,128)(2,1)S(1)} async-done(((bf16[128,64,128]{2,1,0:T(8,128)(2,1)}), bf16[128,64,128]{2,1,0:T(8,128)(2,1)S(1)}, u32[]{:S(2)}, u32[]{:S(2)}) %all-to-all-start.3) | async-done | bytes 2097184 | tf_op jit(solution)/shard_map/all_to_all | solution.py:127
  125.5 4.9 %all-to-all-start.1 = ((bf16[128,128,128]{2,1,0:T(8,128)(2,1)}), bf16[128,128,128]{2,1,0:T(8,128)(2,1)}, u32[]{:S(2)}, u32[]{:S(2)}) async-start(bf16[128,128,128]{2,1,0:T(8,128)(2,1)} %bitcast.125), calls=%async_computation.1 | async-start | bytes 8388608 | tf_op jit(solution)/shard_map/all_to_all | solution.py:127
  130.4 2.3 reshape.285
  132.8 6.2 %fusion.8 = f32[256,768]{1,0:T(8,128)} fusion(bf16[256,4096]{1,0:T(8,128)(2,1)} %reshape.285, bf16[1,4096,768]{2,1,0:T(8,128)(2,1)} %param.21), kind=kOutput, calls=%fused_computation.14 | convolution fusion | flops 1610612736 | bytes 9175040 | tf_op jit(solution)/shard_map/dot_general | solution.py:129
  139.0 10.7 %fusion.15 = bf16[256,4096]{1,0:T(8,128)(2,1)} fusion(bf16[1,768,4096]{2,1,0:T(8,128)(2,1)} %param.23, bf16[256,4096]{1,0:T(8,128)(2,1)S(1)} %copy-done, bf16[1,4096,768]{2,1,0:T(8,128)(2,1)} %param.22, f32[256,768]{1,0:T(8,128)} %fusion.8), kind=kOutput, calls=%fused_computation.19 | convolution fusion | flops 3223453696 | bytes 17563648 | tf_op jit(solution)/shard_map/dot_general | solution.py:132
  149.7 4.2 %reshape.286 = bf16[128,64,128]{2,1,0:T(8,128)(2,1)} reshape(bf16[256,4096]{1,0:T(8,128)(2,1)} %fusion.15) | data formatting | bytes 4194304 | tf_op jit(solution)/shard_map/reshape | solution.py:136
  153.9 29.6 %all-to-all-done.1 = bf16[128,128,128]{2,1,0:T(8,128)(2,1)} async-done(((bf16[128,128,128]{2,1,0:T(8,128)(2,1)}), bf16[128,128,128]{2,1,0:T(8,128)(2,1)}, u32[]{:S(2)}, u32[]{:S(2)}) %all-to-all-start.1) | async-done | bytes 4194336 | tf_op jit(solution)/shard_map/all_to_all | solution.py:127
  183.5 3.8 %all-to-all-start.4 = ((bf16[128,64,128]{2,1,0:T(8,128)(2,1)}), bf16[128,64,128]{2,1,0:T(8,128)(2,1)S(1)}, u32[]{:S(2)}, u32[]{:S(2)}) async-start(bf16[128,64,128]{2,1,0:T(8,128)(2,1)} %reshape.286), calls=%async_computation.4 | async-start | bytes 4194304 | tf_op jit(solution)/shard_map/all_to_all | solution.py:135
  187.3 7.3 %reshape.281 = bf16[512,4096]{1,0:T(8,128)(2,1)} reshape(bf16[128,128,128]{2,1,0:T(8,128)(2,1)} %all-to-all-done.1) | data formatting | bytes 8388608 | tf_op jit(solution)/shard_map/reshape | solution.py:128
  194.6 8.6 %fusion.10 = f32[512,768]{1,0:T(8,128)} fusion(bf16[512,4096]{1,0:T(8,128)(2,1)} %reshape.281, bf16[1,4096,768]{2,1,0:T(8,128)(2,1)} %param.21), kind=kOutput, calls=%fused_computation.16 | convolution fusion | flops 3221225472 | bytes 12058624 | tf_op jit(solution)/shard_map/dot_general | solution.py:129
  203.2 17.1 %fusion.12 = bf16[512,4096]{1,0:T(8,128)(2,1)} fusion(bf16[1,768,4096]{2,1,0:T(8,128)(2,1)} %param.23, f32[512,768]{1,0:T(8,128)} %fusion.10, bf16[512,4096]{1,0:T(8,128)(2,1)} %reshape.281, bf16[1,4096,768]{2,1,0:T(8,128)(2,1)} %param.22), kind=kOutput, calls=%fused_computation.18 | convolution fusion | flops 6446907392 | bytes 22544384 | tf_op jit(solution)/shard_map/dot_general | solution.py:132
  220.3 7.4 %reshape.282 = bf16[128,128,128]{2,1,0:T(8,128)(2,1)} reshape(bf16[512,4096]{1,0:T(8,128)(2,1)} %fusion.12) | data formatting | bytes 8388608 | tf_op jit(solution)/shard_map/reshape | solution.py:136
  227.7 10.3 %all-to-all-start.2 = ((bf16[128,128,128]{2,1,0:T(8,128)(2,1)}), bf16[128,128,128]{2,1,0:T(8,128)(2,1)}, u32[]{:S(2)}, u32[]{:S(2)}) async-start(bf16[128,128,128]{2,1,0:T(8,128)(2,1)} %reshape.282), calls=%async_computation.2 | async-start | bytes 8388608 | tf_op jit(solution)/shard_map/all_to_all | solution.py:135
  238.3 0.5 slice.56
  239.7 0.3 fusion.53
  239.9 0.7 gather_fusion.4
  240.6 50.4 %all-to-all-done.2 = bf16[128,128,128]{2,1,0:T(8,128)(2,1)} async-done(((bf16[128,128,128]{2,1,0:T(8,128)(2,1)}), bf16[128,128,128]{2,1,0:T(8,128)(2,1)}, u32[]{:S(2)}, u32[]{:S(2)}) %all-to-all-start.2) | async-done | bytes 4194336 | tf_op jit(solution)/shard_map/all_to_all | solution.py:135
  291.0 2.9 gather_fusion.2
  294.1 0.6 fusion.18
  294.7 0.7 add_convert_fusion
  (74 shorter events, 3.6 us)
Async XLA Ops:
  6.5 4.3 %copy-start.2 = (bf16[2,32,128,128]{3,2,1,0:T(8,128)(2,1)S(1)}, bf16[2,32,128,128]{3,2,1,0:T(8,128)(2,1)}, u32[]{:S(2)}) copy-start(bf16[2,32,128,128]{3,2,1,0:T(8,128)(2,1)} %param.14) | copy-start | bytes 6291460
  6.5 42.7 %all-gather.2.cloned.1.call-start = ((), (), s32[]{:S(2)}) async-start(), calls=%async_computation.5 | async-start | bytes 3538944 | tf_op jit(solution)/shard_map/all_gather | solution.py:83
  13.3 1.2 copy-start.3
  13.3 7.0 %copy-start.6 = (s32[3,8,8]{2,1,0:T(8,128)S(1)}, s32[3,8,8]{2,1,0:T(8,128)}, u32[]{:S(2)}) copy-start(s32[3,8,8]{2,1,0:T(8,128)} %param.19) | copy-start | bytes 2308
  14.5 14.6 %collective-permute-start = (bf16[2048,128]{1,0:T(8,128)(2,1)S(1)}, bf16[2048,128]{1,0:T(8,128)(2,1)S(1)}, u32[]{:S(2)}, u32[]{:S(2)}) collective-permute-start(bf16[2048,128]{1,0:T(8,128)(2,1)S(1)} %copy-done.3), channel_id=1, source_target_pairs={{0,32},{32,64},{64,96},{96,0},{1,33},{33,65},{65,97},{97,1},{2,34}... | collective-permute-start | bytes 1572872 | tf_op jit(solution)/shard_map/ppermute | solution.py:77
  16.6 25.0 %collective-permute-start.1 = (bf16[2048,128]{1,0:T(8,128)(2,1)S(1)}, bf16[2048,128]{1,0:T(8,128)(2,1)S(1)}, u32[]{:S(2)}, u32[]{:S(2)}) collective-permute-start(bf16[2048,128]{1,0:T(8,128)(2,1)S(1)} %copy-done.3), channel_id=1, source_target_pairs={{0,64},{32,96},{64,0},{96,32},{1,65},{33,97},{65,1},{97,33},{2,66}... | collective-permute-start | bytes 1572872 | tf_op jit(solution)/shard_map/ppermute | solution.py:77
  19.1 22.6 %collective-permute-start.2 = (bf16[2048,128]{1,0:T(8,128)(2,1)S(1)}, bf16[2048,128]{1,0:T(8,128)(2,1)S(1)}, u32[]{:S(2)}, u32[]{:S(2)}) collective-permute-start(bf16[2048,128]{1,0:T(8,128)(2,1)S(1)} %copy-done.3), channel_id=1, source_target_pairs={{0,96},{32,0},{64,32},{96,64},{1,97},{33,1},{65,33},{97,65},{2,98}... | collective-permute-start | bytes 1572872 | tf_op jit(solution)/shard_map/ppermute | solution.py:77
  41.7 0.8 copy-start.4
  41.7 1.0 copy-start.5
  54.1 31.0 %all-to-all-start = ((f32[3,32,8,512]{3,2,0,1:T(8,128)}), f32[3,32,8,512]{3,2,0,1:T(8,128)S(1)}, u32[]{:S(2)}, u32[]{:S(2)}) async-start(f32[3,32,8,512]{3,2,0,1:T(8,128)} %fusion.19), calls=%async_computation | async-start | bytes 3145728 | tf_op jit(solution)/shard_map/all_to_all | solution.py:88
  66.1 19.6 %copy-start.1 = (bf16[3,8,4096]{2,1,0:T(8,128)(2,1)S(1)}, bf16[3,8,4096]{2,1,0:T(8,128)(2,1)}, u32[]{:S(2)}) copy-start(bf16[3,8,4096]{2,1,0:T(8,128)(2,1)} %param.16) | copy-start | bytes 589828
  85.1 0.7 copy-start.7
  88.2 37.3 %all-to-all-start.3 = ((bf16[128,64,128]{2,1,0:T(8,128)(2,1)}), bf16[128,64,128]{2,1,0:T(8,128)(2,1)S(1)}, u32[]{:S(2)}, u32[]{:S(2)}) async-start(bf16[128,64,128]{2,1,0:T(8,128)(2,1)} %bitcast.33), calls=%async_computation.3 | async-start | bytes 4194304 | tf_op jit(solution)/shard_map/all_to_all | solution.py:127
  125.5 57.9 %all-to-all-start.1 = ((bf16[128,128,128]{2,1,0:T(8,128)(2,1)}), bf16[128,128,128]{2,1,0:T(8,128)(2,1)}, u32[]{:S(2)}, u32[]{:S(2)}) async-start(bf16[128,128,128]{2,1,0:T(8,128)(2,1)} %bitcast.125), calls=%async_computation.1 | async-start | bytes 8388608 | tf_op jit(solution)/shard_map/all_to_all | solution.py:127
  132.8 6.2 %copy-start = (bf16[256,4096]{1,0:T(8,128)(2,1)S(1)}, bf16[256,4096]{1,0:T(8,128)(2,1)}, u32[]{:S(2)}) copy-start(bf16[256,4096]{1,0:T(8,128)(2,1)} %reshape.285) | copy-start | bytes 6291460
  183.5 44.3 %all-to-all-start.4 = ((bf16[128,64,128]{2,1,0:T(8,128)(2,1)}), bf16[128,64,128]{2,1,0:T(8,128)(2,1)S(1)}, u32[]{:S(2)}, u32[]{:S(2)}) async-start(bf16[128,64,128]{2,1,0:T(8,128)(2,1)} %reshape.286), calls=%async_computation.4 | async-start | bytes 4194304 | tf_op jit(solution)/shard_map/all_to_all | solution.py:135
  227.7 11.9 %copy-start.8 = (f32[3,8,8]{2,1,0:T(8,128)S(1)}, f32[3,8,8]{2,1,0:T(8,128)}, u32[]{:S(2)}) copy-start(f32[3,8,8]{2,1,0:T(8,128)} %param.20) | copy-start | bytes 2308
  227.7 63.2 %all-to-all-start.2 = ((bf16[128,128,128]{2,1,0:T(8,128)(2,1)}), bf16[128,128,128]{2,1,0:T(8,128)(2,1)}, u32[]{:S(2)}, u32[]{:S(2)}) async-start(bf16[128,128,128]{2,1,0:T(8,128)(2,1)} %reshape.282), calls=%async_computation.2 | async-start | bytes 8388608 | tf_op jit(solution)/shard_map/all_to_all | solution.py:135
Sparse Core Ops, SparseCore 0:
  14.6 31.2 all-gather.1

commit v8 on v7

--- a/solution.py
+++ b/solution.py
@@ -84,12 +84,12 @@
     partial_sums = jnp.einsum(
         "srk,kc->src", gathered, w_cols, preferred_element_type=jnp.float32
     )
-    grouped = partial_sums.reshape(steps, yc_count * tp_count, row_own, -1)
+    grouped = partial_sums.astype(jnp.bfloat16).reshape(steps, yc_count * tp_count, row_own, -1)
     arrived_sums = lax.all_to_all(
         grouped, ("y", "c", "tp"), split_axis=1, concat_axis=1, tiled=True
     )
     arrived_sums = arrived_sums.reshape(steps, yc_count, tp_count, row_own, x_count, -1)
-    summed = jnp.sum(arrived_sums, axis=2)
+    summed = jnp.sum(arrived_sums.astype(jnp.float32), axis=2)
     projected = summed.astype(jnp.bfloat16)
     row_major = jnp.transpose(projected, (0, 2, 3, 1, 4)).reshape(steps, row_own, width)
 

time: 304 us -> 295 us (0.970)
  waiting for transfers between devices: 147 us -> 139 us
    all_to_all x1, waiting for transfers between devices: 18.7 us -> 11.5 us  [per_device(): lax.all_to_all(grouped, ('y', 'c', 'tp'), split_axis=1, concat_axis=1, ti...]
  transfers between devices with their start and end apart: 9 -> 9, of which waited for: 6 -> 6; matrix products, arithmetic and copies ran while one was open for 26% -> 27% of each run, Pallas kernels for 0% -> 0%
where the time goes in v8:
time: 295 us; the launch traced here: 294 us
  waiting for transfers between devices  139 us (47%)
  matrix products  48.7 us (17%)
  local copies, waits for them, and re-layouts  44.9 us (15%)
  starting transfers between devices  40.4 us (14%)
  between operations  14.5 us (5%)
  other arithmetic  6.22 us (2%)
    all_to_all x2, waiting for transfers between devices, per_device(): lax.all_to_all(outgoing, group, split_axis=0, concat_axis=0, tiled=True)  56.5 us
    all_to_all x2, waiting for transfers between devices, per_device(): lax.all_to_all(expert_out.reshape(wire_shape), group, split_axis=0, conca...  50.4 us
    dot_general x2, matrix products, per_device(): jnp.dot(hidden, expert_down[0], preferred_element_type=jnp.float32)  27.8 us
    ppermute x3, waiting for transfers between devices, per_device(): lax.ppermute(w_out, 'x', [(i, (i + k) % x_count) for i in range(x_count)])  20.5 us
    dot_general x2, matrix products, per_device(): jnp.dot(flat_rows, expert_gate[0], preferred_element_type=jnp.float32)  14.8 us
    all_to_all x2, starting transfers between devices, per_device(): lax.all_to_all(expert_out.reshape(wire_shape), group, split_axis=0, conca...  14.1 us
    reshape x2, local copies, waits for them, and re-layouts, per_device(): expert_out.reshape(wire_shape)  11.6 us
    all_to_all x1, waiting for transfers between devices, per_device(): lax.all_to_all(grouped, ('y', 'c', 'tp'), split_axis=1, concat_axis=1, ti...  11.5 us
  transfers between devices with their start and end apart: 9, of which 6 were waited for; matrix products, arithmetic and copies ran while one was open for 27% of the time, Pallas kernels for 0%

profile of v8, /device:TPU:1, one launch (start us, length us, event | category | flops | bytes accessed | tf_op | source)
XLA Modules:
  0.0 293.6 jit_solution(14567345966308424462)
XLA Ops:
  6.5 1.2 copy.111
  7.8 0.8 fusion.60
  8.5 0.8 fusion.46
  9.6 0.7 iota_compare_fusion.1
  10.4 0.4 copy.91
  10.8 0.9 fusion.61
  11.8 0.6 fusion.33
  12.4 0.5 divide_convert_fusion
  12.9 0.4 fusion.34
  13.3 0.2 fusion.32
  13.6 0.9 reshape.276
  14.5 2.1 collective-permute-start
  16.6 2.5 collective-permute-start.1
  19.1 1.2 collective-permute-start.2
  21.1 8.0 %collective-permute-done = bf16[2048,128]{1,0:T(8,128)(2,1)S(1)} collective-permute-done((bf16[2048,128]{1,0:T(8,128)(2,1)S(1)}, bf16[2048,128]{1,0:T(8,128)(2,1)S(1)}, u32[]{:S(2)}, u32[]{:S(2)}) %collective-permute-start) | collective-permute-done | bytes 524320 | tf_op jit(solution)/shard_map/ppermute | solution.py:77
  29.2 12.5 %collective-permute-done.1 = bf16[2048,128]{1,0:T(8,128)(2,1)S(1)} collective-permute-done((bf16[2048,128]{1,0:T(8,128)(2,1)S(1)}, bf16[2048,128]{1,0:T(8,128)(2,1)S(1)}, u32[]{:S(2)}, u32[]{:S(2)}) %collective-permute-start.1) | collective-permute-done | bytes 524320 | tf_op jit(solution)/shard_map/ppermute | solution.py:77
  41.7 0.8 copy-done.4
  42.6 1.5 pad_maximum_fusion
  44.1 2.2 gather_fusion
  46.3 2.9 copy.96
  49.2 3.7 %fusion.22 = bf16[3,32,8,512]{3,2,1,0:T(8,128)(2,1)S(1)} fusion(bf16[3,256,2048]{2,1,0:T(8,128)(2,1)} %all-gather.2.cloned.1.call-done, bf16[2048,512,1]{0,1,2:T(8,128)(2,1)S(1)} %bitcast.127), kind=kOutput, calls=%fused_computation.29 | convolution fusion | flops 1611005952 | bytes 6029312 | tf_op jit(solution)/shard_map/srk,kc->src/dot_general | solution.py:84
  53.0 0.9 copy.98
  53.9 9.6 %all-to-all-start = ((bf16[3,32,8,512]{3,2,0,1:T(8,128)(2,1)}), bf16[3,32,8,512]{3,2,0,1:T(8,128)(2,1)S(1)}, u32[]{:S(2)}, u32[]{:S(2)}) async-start(bf16[3,32,8,512]{3,2,0,1:T(8,128)(2,1)} %copy.98), calls=%async_computation | async-start | bytes 1572864 | tf_op jit(solution)/shard_map/all_to_all | solution.py:88
  63.7 1.2 scatter_custom_fusion
  65.5 11.5 %all-to-all-done = bf16[3,32,8,512]{3,2,0,1:T(8,128)(2,1)S(1)} async-done(((bf16[3,32,8,512]{3,2,0,1:T(8,128)(2,1)}), bf16[3,32,8,512]{3,2,0,1:T(8,128)(2,1)S(1)}, u32[]{:S(2)}, u32[]{:S(2)}) %all-to-all-start) | async-done | bytes 786464 | tf_op jit(solution)/shard_map/all_to_all | solution.py:88
  77.9 2.2 gather_fusion.3
  80.1 6.0 %all-to-all-start.3 = ((bf16[128,64,128]{2,1,0:T(8,128)(2,1)}), bf16[128,64,128]{2,1,0:T(8,128)(2,1)S(1)}, u32[]{:S(2)}, u32[]{:S(2)}) async-start(bf16[128,64,128]{2,1,0:T(8,128)(2,1)} %bitcast.33), calls=%async_computation.3 | async-start | bytes 4194304 | tf_op jit(solution)/shard_map/all_to_all | solution.py:127
  86.4 3.5 %gather_fusion.1 = bf16[512,32,128]{2,1,0:T(8,128)(2,1)} fusion(bf16[25,32,128]{2,1,0:T(8,128)(2,1)S(1)} %concatenate.10, s32[1024]{0:T(1024)S(1)} %pad_clamp_fusion.3), kind=kCustom, calls=%fused_computation.1 | custom fusion | bytes 8390656 | tf_op jit(solution)/shard_map/jit(_take)/gather | solution.py:126
  89.9 27.0 %all-to-all-done.3 = bf16[128,64,128]{2,1,0:T(8,128)(2,1)S(1)} async-done(((bf16[128,64,128]{2,1,0:T(8,128)(2,1)}), bf16[128,64,128]{2,1,0:T(8,128)(2,1)S(1)}, u32[]{:S(2)}, u32[]{:S(2)}) %all-to-all-start.3) | async-done | bytes 2097184 | tf_op jit(solution)/shard_map/all_to_all | solution.py:127
  116.9 4.9 %all-to-all-start.1 = ((bf16[128,128,128]{2,1,0:T(8,128)(2,1)}), bf16[128,128,128]{2,1,0:T(8,128)(2,1)}, u32[]{:S(2)}, u32[]{:S(2)}) async-start(bf16[128,128,128]{2,1,0:T(8,128)(2,1)} %bitcast.122), calls=%async_computation.1 | async-start | bytes 8388608 | tf_op jit(solution)/shard_map/all_to_all | solution.py:127
  121.8 2.3 reshape.287
  124.1 6.2 %fusion.8 = f32[256,768]{1,0:T(8,128)} fusion(bf16[256,4096]{1,0:T(8,128)(2,1)} %reshape.287, bf16[1,4096,768]{2,1,0:T(8,128)(2,1)} %param.21), kind=kOutput, calls=%fused_computation.14 | convolution fusion | flops 1610612736 | bytes 9175040 | tf_op jit(solution)/shard_map/dot_general | solution.py:129
  130.4 10.7 %fusion.15 = bf16[256,4096]{1,0:T(8,128)(2,1)} fusion(bf16[1,768,4096]{2,1,0:T(8,128)(2,1)} %param.23, bf16[256,4096]{1,0:T(8,128)(2,1)S(1)} %copy-done, bf16[1,4096,768]{2,1,0:T(8,128)(2,1)} %param.22, f32[256,768]{1,0:T(8,128)} %fusion.8), kind=kOutput, calls=%fused_computation.19 | convolution fusion | flops 3223453696 | bytes 17563648 | tf_op jit(solution)/shard_map/dot_general | solution.py:132
  141.0 4.2 %reshape.288 = bf16[128,64,128]{2,1,0:T(8,128)(2,1)} reshape(bf16[256,4096]{1,0:T(8,128)(2,1)} %fusion.15) | data formatting | bytes 4194304 | tf_op jit(solution)/shard_map/reshape | solution.py:136
  145.2 29.6 %all-to-all-done.1 = bf16[128,128,128]{2,1,0:T(8,128)(2,1)} async-done(((bf16[128,128,128]{2,1,0:T(8,128)(2,1)}), bf16[128,128,128]{2,1,0:T(8,128)(2,1)}, u32[]{:S(2)}, u32[]{:S(2)}) %all-to-all-start.1) | async-done | bytes 4194336 | tf_op jit(solution)/shard_map/all_to_all | solution.py:127
  174.8 3.8 %all-to-all-start.4 = ((bf16[128,64,128]{2,1,0:T(8,128)(2,1)}), bf16[128,64,128]{2,1,0:T(8,128)(2,1)S(1)}, u32[]{:S(2)}, u32[]{:S(2)}) async-start(bf16[128,64,128]{2,1,0:T(8,128)(2,1)} %reshape.288), calls=%async_computation.4 | async-start | bytes 4194304 | tf_op jit(solution)/shard_map/all_to_all | solution.py:135
  178.6 7.3 %reshape.283 = bf16[512,4096]{1,0:T(8,128)(2,1)} reshape(bf16[128,128,128]{2,1,0:T(8,128)(2,1)} %all-to-all-done.1) | data formatting | bytes 8388608 | tf_op jit(solution)/shard_map/reshape | solution.py:128
  185.9 8.6 %fusion.10 = f32[512,768]{1,0:T(8,128)} fusion(bf16[512,4096]{1,0:T(8,128)(2,1)} %reshape.283, bf16[1,4096,768]{2,1,0:T(8,128)(2,1)} %param.21), kind=kOutput, calls=%fused_computation.16 | convolution fusion | flops 3221225472 | bytes 12058624 | tf_op jit(solution)/shard_map/dot_general | solution.py:129
  194.5 17.1 %fusion.12 = bf16[512,4096]{1,0:T(8,128)(2,1)} fusion(bf16[1,768,4096]{2,1,0:T(8,128)(2,1)} %param.23, f32[512,768]{1,0:T(8,128)} %fusion.10, bf16[512,4096]{1,0:T(8,128)(2,1)} %reshape.283, bf16[1,4096,768]{2,1,0:T(8,128)(2,1)} %param.22), kind=kOutput, calls=%fused_computation.18 | convolution fusion | flops 6446907392 | bytes 22544384 | tf_op jit(solution)/shard_map/dot_general | solution.py:132
  211.6 7.4 %reshape.284 = bf16[128,128,128]{2,1,0:T(8,128)(2,1)} reshape(bf16[512,4096]{1,0:T(8,128)(2,1)} %fusion.12) | data formatting | bytes 8388608 | tf_op jit(solution)/shard_map/reshape | solution.py:136
  219.1 10.4 %all-to-all-start.2 = ((bf16[128,128,128]{2,1,0:T(8,128)(2,1)}), bf16[128,128,128]{2,1,0:T(8,128)(2,1)}, u32[]{:S(2)}, u32[]{:S(2)}) async-start(bf16[128,128,128]{2,1,0:T(8,128)(2,1)} %reshape.284), calls=%async_computation.2 | async-start | bytes 8388608 | tf_op jit(solution)/shard_map/all_to_all | solution.py:135
  229.7 0.5 slice.56
  231.0 0.3 fusion.52
  231.3 0.7 gather_fusion.4
  231.9 50.4 %all-to-all-done.2 = bf16[128,128,128]{2,1,0:T(8,128)(2,1)} async-done(((bf16[128,128,128]{2,1,0:T(8,128)(2,1)}), bf16[128,128,128]{2,1,0:T(8,128)(2,1)}, u32[]{:S(2)}, u32[]{:S(2)}) %all-to-all-start.2) | async-done | bytes 4194336 | tf_op jit(solution)/shard_map/all_to_all | solution.py:135
  282.3 2.9 %gather_fusion.2 = bf16[128,32,128]{2,1,0:T(8,128)(2,1)S(1)} fusion(bf16[512,32,128]{2,1,0:T(8,128)(2,1)} %bitcast.31, s32[1024]{0:T(1024)S(1)} %pad_clamp_fusion.2), kind=kCustom, calls=%fused_computation.2 | custom fusion | bytes 2097664 | tf_op jit(solution)/shard_map/jit(_take)/gather | solution.py:144
  285.4 0.6 fusion.18
  286.1 0.7 add_convert_fusion
  (75 shorter events, 3.8 us)
Async XLA Ops:
  6.5 4.3 %copy-start.2 = (bf16[2,32,128,128]{3,2,1,0:T(8,128)(2,1)S(1)}, bf16[2,32,128,128]{3,2,1,0:T(8,128)(2,1)}, u32[]{:S(2)}) copy-start(bf16[2,32,128,128]{3,2,1,0:T(8,128)(2,1)} %param.14) | copy-start | bytes 6291460
  6.5 42.7 %all-gather.2.cloned.1.call-start = ((), (), s32[]{:S(2)}) async-start(), calls=%async_computation.5 | async-start | bytes 3538944 | tf_op jit(solution)/shard_map/all_gather | solution.py:83
  13.3 1.2 copy-start.3
  13.3 7.0 %copy-start.6 = (s32[3,8,8]{2,1,0:T(8,128)S(1)}, s32[3,8,8]{2,1,0:T(8,128)}, u32[]{:S(2)}) copy-start(s32[3,8,8]{2,1,0:T(8,128)} %param.19) | copy-start | bytes 2308
  14.5 14.6 %collective-permute-start = (bf16[2048,128]{1,0:T(8,128)(2,1)S(1)}, bf16[2048,128]{1,0:T(8,128)(2,1)S(1)}, u32[]{:S(2)}, u32[]{:S(2)}) collective-permute-start(bf16[2048,128]{1,0:T(8,128)(2,1)S(1)} %copy-done.3), channel_id=1, source_target_pairs={{0,32},{32,64},{64,96},{96,0},{1,33},{33,65},{65,97},{97,1},{2,34}... | collective-permute-start | bytes 1572872 | tf_op jit(solution)/shard_map/ppermute | solution.py:77
  16.6 25.0 %collective-permute-start.1 = (bf16[2048,128]{1,0:T(8,128)(2,1)S(1)}, bf16[2048,128]{1,0:T(8,128)(2,1)S(1)}, u32[]{:S(2)}, u32[]{:S(2)}) collective-permute-start(bf16[2048,128]{1,0:T(8,128)(2,1)S(1)} %copy-done.3), channel_id=1, source_target_pairs={{0,64},{32,96},{64,0},{96,32},{1,65},{33,97},{65,1},{97,33},{2,66}... | collective-permute-start | bytes 1572872 | tf_op jit(solution)/shard_map/ppermute | solution.py:77
  19.1 22.6 %collective-permute-start.2 = (bf16[2048,128]{1,0:T(8,128)(2,1)S(1)}, bf16[2048,128]{1,0:T(8,128)(2,1)S(1)}, u32[]{:S(2)}, u32[]{:S(2)}) collective-permute-start(bf16[2048,128]{1,0:T(8,128)(2,1)S(1)} %copy-done.3), channel_id=1, source_target_pairs={{0,96},{32,0},{64,32},{96,64},{1,97},{33,1},{65,33},{97,65},{2,98}... | collective-permute-start | bytes 1572872 | tf_op jit(solution)/shard_map/ppermute | solution.py:77
  41.7 0.8 copy-start.4
  41.7 1.0 copy-start.5
  53.9 23.2 %all-to-all-start = ((bf16[3,32,8,512]{3,2,0,1:T(8,128)(2,1)}), bf16[3,32,8,512]{3,2,0,1:T(8,128)(2,1)S(1)}, u32[]{:S(2)}, u32[]{:S(2)}) async-start(bf16[3,32,8,512]{3,2,0,1:T(8,128)(2,1)} %copy.98), calls=%async_computation | async-start | bytes 1572864 | tf_op jit(solution)/shard_map/all_to_all | solution.py:88
  63.5 14.0 %copy-start.1 = (bf16[3,8,4096]{2,1,0:T(8,128)(2,1)S(1)}, bf16[3,8,4096]{2,1,0:T(8,128)(2,1)}, u32[]{:S(2)}) copy-start(bf16[3,8,4096]{2,1,0:T(8,128)(2,1)} %param.16) | copy-start | bytes 589828
  64.9 12.8 %copy-start.7 = (f32[4096]{0:T(1024)S(1)}, f32[4096]{0:T(1024)}, u32[]{:S(2)}) copy-start(f32[4096]{0:T(1024)} %param.17) | copy-start | bytes 49156
  80.1 36.8 %all-to-all-start.3 = ((bf16[128,64,128]{2,1,0:T(8,128)(2,1)}), bf16[128,64,128]{2,1,0:T(8,128)(2,1)S(1)}, u32[]{:S(2)}, u32[]{:S(2)}) async-start(bf16[128,64,128]{2,1,0:T(8,128)(2,1)} %bitcast.33), calls=%async_computation.3 | async-start | bytes 4194304 | tf_op jit(solution)/shard_map/all_to_all | solution.py:127
  116.9 57.9 %all-to-all-start.1 = ((bf16[128,128,128]{2,1,0:T(8,128)(2,1)}), bf16[128,128,128]{2,1,0:T(8,128)(2,1)}, u32[]{:S(2)}, u32[]{:S(2)}) async-start(bf16[128,128,128]{2,1,0:T(8,128)(2,1)} %bitcast.122), calls=%async_computation.1 | async-start | bytes 8388608 | tf_op jit(solution)/shard_map/all_to_all | solution.py:127
  124.1 6.2 %copy-start = (bf16[256,4096]{1,0:T(8,128)(2,1)S(1)}, bf16[256,4096]{1,0:T(8,128)(2,1)}, u32[]{:S(2)}) copy-start(bf16[256,4096]{1,0:T(8,128)(2,1)} %reshape.287) | copy-start | bytes 6291460
  174.8 44.3 %all-to-all-start.4 = ((bf16[128,64,128]{2,1,0:T(8,128)(2,1)}), bf16[128,64,128]{2,1,0:T(8,128)(2,1)S(1)}, u32[]{:S(2)}, u32[]{:S(2)}) async-start(bf16[128,64,128]{2,1,0:T(8,128)(2,1)} %reshape.288), calls=%async_computation.4 | async-start | bytes 4194304 | tf_op jit(solution)/shard_map/all_to_all | solution.py:135
  219.1 11.9 %copy-start.8 = (f32[3,8,8]{2,1,0:T(8,128)S(1)}, f32[3,8,8]{2,1,0:T(8,128)}, u32[]{:S(2)}) copy-start(f32[3,8,8]{2,1,0:T(8,128)} %param.20) | copy-start | bytes 2308
  219.1 63.2 %all-to-all-start.2 = ((bf16[128,128,128]{2,1,0:T(8,128)(2,1)}), bf16[128,128,128]{2,1,0:T(8,128)(2,1)}, u32[]{:S(2)}, u32[]{:S(2)}) async-start(bf16[128,128,128]{2,1,0:T(8,128)(2,1)} %reshape.284), calls=%async_computation.2 | async-start | bytes 8388608 | tf_op jit(solution)/shard_map/all_to_all | solution.py:135
Sparse Core Ops, SparseCore 0:
  14.6 31.2 all-gather.1

commit v9 on v7

--- a/solution.py
+++ b/solution.py
@@ -77,12 +77,9 @@
         lax.ppermute(w_out, "x", [(i, (i + k) % x_count) for i in range(x_count)])
         for k in range(1, x_count)
     ]
-    order = (x_here - jnp.arange(x_count, dtype=jnp.int32)) % x_count
-    w_cols = jnp.take(jnp.stack(shifted), order, axis=0, mode="clip")
-    w_cols = jnp.transpose(w_cols, (1, 0, 2)).reshape(w_out.shape[0], -1)
     gathered = lax.all_gather(attended, ("y", "c"), axis=1, tiled=True)
     partial_sums = jnp.einsum(
-        "srk,kc->src", gathered, w_cols, preferred_element_type=jnp.float32
+        "srk,jkc->srjc", gathered, jnp.stack(shifted), preferred_element_type=jnp.float32
     )
     grouped = partial_sums.reshape(steps, yc_count * tp_count, row_own, -1)
     arrived_sums = lax.all_to_all(
@@ -90,6 +87,8 @@
     )
     arrived_sums = arrived_sums.reshape(steps, yc_count, tp_count, row_own, x_count, -1)
     summed = jnp.sum(arrived_sums, axis=2)
+    order = (x_here - jnp.arange(x_count, dtype=jnp.int32)) % x_count
+    summed = jnp.take(summed, order, axis=3, mode="clip")
     projected = summed.astype(jnp.bfloat16)
     row_major = jnp.transpose(projected, (0, 2, 3, 1, 4)).reshape(steps, row_own, width)
 

time: 304 us -> 299 us (0.984)
  waiting for transfers between devices: 147 us -> 151 us
  starting transfers between devices: 40.9 us -> 37.7 us
    all_gather x1, waiting for transfers between devices: 0.02 us -> 4.32 us  [per_device(): gathered = lax.all_gather(attended, ('y', 'c'), axis=1, tiled=True)]
    all_to_all x1, starting transfers between devices: 9.63 us -> 5.96 us  [per_device(): lax.all_to_all(grouped, ('y', 'c', 'tp'), split_axis=1, concat_axis=1, ti...]
  transfers between devices with their start and end apart: 9 -> 9, of which waited for: 6 -> 7; matrix products, arithmetic and copies ran while one was open for 26% -> 24% of each run, Pallas kernels for 0% -> 0%
where the time goes in v9:
time: 299 us; the launch traced here: 298 us
  waiting for transfers between devices  151 us (51%)
  matrix products  48.7 us (16%)
  local copies, waits for them, and re-layouts  41.2 us (14%)
  starting transfers between devices  37.7 us (13%)
  between operations  14.5 us (5%)
  other arithmetic  4.78 us (2%)
    all_to_all x2, waiting for transfers between devices, per_device(): lax.all_to_all(outgoing, group, split_axis=0, concat_axis=0, tiled=True)  56.5 us
    all_to_all x2, waiting for transfers between devices, per_device(): lax.all_to_all(expert_out.reshape(wire_shape), group, split_axis=0, conca...  50.4 us
    dot_general x2, matrix products, per_device(): jnp.dot(hidden, expert_down[0], preferred_element_type=jnp.float32)  27.8 us
    ppermute x3, waiting for transfers between devices, per_device(): lax.ppermute(w_out, 'x', [(i, (i + k) % x_count) for i in range(x_count)])  21.1 us
    all_to_all x1, waiting for transfers between devices, per_device(): lax.all_to_all(grouped, ('y', 'c', 'tp'), split_axis=1, concat_axis=1, ti...  18.9 us
    dot_general x2, matrix products, per_device(): jnp.dot(flat_rows, expert_gate[0], preferred_element_type=jnp.float32)  14.8 us
    all_to_all x2, starting transfers between devices, per_device(): lax.all_to_all(expert_out.reshape(wire_shape), group, split_axis=0, conca...  14.2 us
    all_to_all x2, starting transfers between devices, per_device(): lax.all_to_all(outgoing, group, split_axis=0, concat_axis=0, tiled=True)  11.9 us
  transfers between devices with their start and end apart: 9, of which 7 were waited for; matrix products, arithmetic and copies ran while one was open for 24% of the time, Pallas kernels for 0%

profile of v9, /device:TPU:1, one launch (start us, length us, event | category | flops | bytes accessed | tf_op | source)
XLA Modules:
  0.0 298.1 jit_solution(17962922811590225706)
XLA Ops:
  6.5 1.2 copy.104
  7.8 0.8 fusion.68
  8.5 0.8 fusion.53
  9.6 0.7 iota_compare_fusion.1
  10.4 0.4 copy.87
  10.8 0.9 fusion.69
  11.8 0.6 fusion.40
  12.4 0.5 divide_convert_fusion
  12.9 0.4 fusion.41
  13.3 0.2 fusion.39
  13.6 0.9 reshape.273
  14.5 2.1 collective-permute-start
  16.6 2.5 collective-permute-start.1
  19.1 1.2 collective-permute-start.2
  20.5 8.6 %collective-permute-done = bf16[2048,128]{1,0:T(8,128)(2,1)S(1)} collective-permute-done((bf16[2048,128]{1,0:T(8,128)(2,1)S(1)}, bf16[2048,128]{1,0:T(8,128)(2,1)S(1)}, u32[]{:S(2)}, u32[]{:S(2)}) %collective-permute-start) | collective-permute-done | bytes 524320 | tf_op jit(solution)/shard_map/ppermute | solution.py:77
  29.2 12.5 %collective-permute-done.1 = bf16[2048,128]{1,0:T(8,128)(2,1)S(1)} collective-permute-done((bf16[2048,128]{1,0:T(8,128)(2,1)S(1)}, bf16[2048,128]{1,0:T(8,128)(2,1)S(1)}, u32[]{:S(2)}, u32[]{:S(2)}) %collective-permute-start.1) | collective-permute-done | bytes 524320 | tf_op jit(solution)/shard_map/ppermute | solution.py:77
  41.7 4.3 %all-gather.2.cloned.1.call-done = bf16[3,256,2048]{2,1,0:T(8,128)(2,1)} async-done(((bf16[3,32,2048]{2,1,0:T(8,128)(2,1)}), bf16[3,256,2048]{2,1,0:T(8,128)(2,1)}) %all-gather.2.cloned.1.call-update) | async-done | bytes 3145744 | tf_op jit(solution)/shard_map/all_gather | solution.py:80
  46.0 3.7 %fusion.19 = f32[3,256,4,128]{3,1,2,0:T(8,128)S(1)} fusion(bf16[3,256,2048]{2,1,0:T(8,128)(2,1)} %all-gather.2.cloned.1.call-done, bf16[1,2048,128]{2,1,0:T(8,128)(2,1)S(1)} %bitcast.134, bf16[1,2048,128]{2,1,0:T(8,128)(2,1)S(1)} %bitcast.133, bf16[1,2048,128]{2,1,0:T(8,128)(2,1)S(1)} %bitcast.132, bf16[1,2048,128]{2,1,0:T(8,128)(2,1)S(1)} %bitcast.131), kind=kOutput, calls=%fused_computation.22 | convolution fusion | flops 1619001344 | bytes 6815744 | tf_op jit(solution)/shard_map/srk,jkc->srjc/dot_general | solution.py:81
  49.7 1.0 copy.92
  50.7 0.6 reshape.274
  51.3 1.3 copy.93
  52.6 6.0 %all-to-all-start = ((f32[3,32,8,512]{3,2,0,1:T(8,128)}), f32[3,32,8,512]{3,2,0,1:T(8,128)S(1)}, u32[]{:S(2)}, u32[]{:S(2)}) async-start(f32[3,32,8,512]{3,2,0,1:T(8,128)} %copy.93), calls=%async_computation | async-start | bytes 3145728 | tf_op jit(solution)/shard_map/all_to_all | solution.py:85
  59.3 1.2 scatter_custom_fusion
  61.1 18.9 %all-to-all-done = f32[3,32,8,512]{3,2,0,1:T(8,128)S(1)} async-done(((f32[3,32,8,512]{3,2,0,1:T(8,128)}), f32[3,32,8,512]{3,2,0,1:T(8,128)S(1)}, u32[]{:S(2)}, u32[]{:S(2)}) %all-to-all-start) | async-done | bytes 1572896 | tf_op jit(solution)/shard_map/all_to_all | solution.py:85
  80.2 0.6 gather_fusion
  81.3 2.2 gather_fusion.3
  83.6 7.0 %all-to-all-start.3 = ((bf16[128,64,128]{2,1,0:T(8,128)(2,1)}), bf16[128,64,128]{2,1,0:T(8,128)(2,1)S(1)}, u32[]{:S(2)}, u32[]{:S(2)}) async-start(bf16[128,64,128]{2,1,0:T(8,128)(2,1)} %bitcast.32), calls=%async_computation.3 | async-start | bytes 4194304 | tf_op jit(solution)/shard_map/all_to_all | solution.py:126
  90.8 3.5 %gather_fusion.1 = bf16[512,32,128]{2,1,0:T(8,128)(2,1)} fusion(bf16[25,32,128]{2,1,0:T(8,128)(2,1)S(1)} %concatenate.10, s32[1024]{0:T(1024)S(1)} %pad_clamp_fusion.3), kind=kCustom, calls=%fused_computation.1 | custom fusion | bytes 8390656 | tf_op jit(solution)/shard_map/jit(_take)/gather | solution.py:125
  94.4 27.0 %all-to-all-done.3 = bf16[128,64,128]{2,1,0:T(8,128)(2,1)S(1)} async-done(((bf16[128,64,128]{2,1,0:T(8,128)(2,1)}), bf16[128,64,128]{2,1,0:T(8,128)(2,1)S(1)}, u32[]{:S(2)}, u32[]{:S(2)}) %all-to-all-start.3) | async-done | bytes 2097184 | tf_op jit(solution)/shard_map/all_to_all | solution.py:126
  121.3 4.9 %all-to-all-start.1 = ((bf16[128,128,128]{2,1,0:T(8,128)(2,1)}), bf16[128,128,128]{2,1,0:T(8,128)(2,1)}, u32[]{:S(2)}, u32[]{:S(2)}) async-start(bf16[128,128,128]{2,1,0:T(8,128)(2,1)} %bitcast.122), calls=%async_computation.1 | async-start | bytes 8388608 | tf_op jit(solution)/shard_map/all_to_all | solution.py:126
  126.2 2.3 reshape.283
  128.6 6.2 %fusion.8 = f32[256,768]{1,0:T(8,128)} fusion(bf16[256,4096]{1,0:T(8,128)(2,1)} %reshape.283, bf16[1,4096,768]{2,1,0:T(8,128)(2,1)} %param.21), kind=kOutput, calls=%fused_computation.14 | convolution fusion | flops 1610612736 | bytes 9175040 | tf_op jit(solution)/shard_map/dot_general | solution.py:128
  134.8 10.7 %fusion.15 = bf16[256,4096]{1,0:T(8,128)(2,1)} fusion(bf16[1,768,4096]{2,1,0:T(8,128)(2,1)} %param.23, bf16[256,4096]{1,0:T(8,128)(2,1)S(1)} %copy-done, bf16[1,4096,768]{2,1,0:T(8,128)(2,1)} %param.22, f32[256,768]{1,0:T(8,128)} %fusion.8), kind=kOutput, calls=%fused_computation.19 | convolution fusion | flops 3223453696 | bytes 17563648 | tf_op jit(solution)/shard_map/dot_general | solution.py:131
  145.5 4.2 %reshape.284 = bf16[128,64,128]{2,1,0:T(8,128)(2,1)} reshape(bf16[256,4096]{1,0:T(8,128)(2,1)} %fusion.15) | data formatting | bytes 4194304 | tf_op jit(solution)/shard_map/reshape | solution.py:135
  149.7 29.6 %all-to-all-done.1 = bf16[128,128,128]{2,1,0:T(8,128)(2,1)} async-done(((bf16[128,128,128]{2,1,0:T(8,128)(2,1)}), bf16[128,128,128]{2,1,0:T(8,128)(2,1)}, u32[]{:S(2)}, u32[]{:S(2)}) %all-to-all-start.1) | async-done | bytes 4194336 | tf_op jit(solution)/shard_map/all_to_all | solution.py:126
  179.3 3.8 %all-to-all-start.4 = ((bf16[128,64,128]{2,1,0:T(8,128)(2,1)}), bf16[128,64,128]{2,1,0:T(8,128)(2,1)S(1)}, u32[]{:S(2)}, u32[]{:S(2)}) async-start(bf16[128,64,128]{2,1,0:T(8,128)(2,1)} %reshape.284), calls=%async_computation.4 | async-start | bytes 4194304 | tf_op jit(solution)/shard_map/all_to_all | solution.py:134
  183.1 7.3 %reshape.279 = bf16[512,4096]{1,0:T(8,128)(2,1)} reshape(bf16[128,128,128]{2,1,0:T(8,128)(2,1)} %all-to-all-done.1) | data formatting | bytes 8388608 | tf_op jit(solution)/shard_map/reshape | solution.py:127
  190.4 8.6 %fusion.10 = f32[512,768]{1,0:T(8,128)} fusion(bf16[512,4096]{1,0:T(8,128)(2,1)} %reshape.279, bf16[1,4096,768]{2,1,0:T(8,128)(2,1)} %param.21), kind=kOutput, calls=%fused_computation.16 | convolution fusion | flops 3221225472 | bytes 12058624 | tf_op jit(solution)/shard_map/dot_general | solution.py:128
  199.0 17.1 %fusion.12 = bf16[512,4096]{1,0:T(8,128)(2,1)} fusion(bf16[1,768,4096]{2,1,0:T(8,128)(2,1)} %param.23, f32[512,768]{1,0:T(8,128)} %fusion.10, bf16[512,4096]{1,0:T(8,128)(2,1)} %reshape.279, bf16[1,4096,768]{2,1,0:T(8,128)(2,1)} %param.22), kind=kOutput, calls=%fused_computation.18 | convolution fusion | flops 6446907392 | bytes 22544384 | tf_op jit(solution)/shard_map/dot_general | solution.py:131
  216.1 7.4 %reshape.280 = bf16[128,128,128]{2,1,0:T(8,128)(2,1)} reshape(bf16[512,4096]{1,0:T(8,128)(2,1)} %fusion.12) | data formatting | bytes 8388608 | tf_op jit(solution)/shard_map/reshape | solution.py:135
  223.5 10.4 %all-to-all-start.2 = ((bf16[128,128,128]{2,1,0:T(8,128)(2,1)}), bf16[128,128,128]{2,1,0:T(8,128)(2,1)}, u32[]{:S(2)}, u32[]{:S(2)}) async-start(bf16[128,128,128]{2,1,0:T(8,128)(2,1)} %reshape.280), calls=%async_computation.2 | async-start | bytes 8388608 | tf_op jit(solution)/shard_map/all_to_all | solution.py:134
  234.2 0.5 slice.56
  235.5 0.3 fusion.59
  235.7 0.7 gather_fusion.4
  236.4 50.4 %all-to-all-done.2 = bf16[128,128,128]{2,1,0:T(8,128)(2,1)} async-done(((bf16[128,128,128]{2,1,0:T(8,128)(2,1)}), bf16[128,128,128]{2,1,0:T(8,128)(2,1)}, u32[]{:S(2)}, u32[]{:S(2)}) %all-to-all-start.2) | async-done | bytes 4194336 | tf_op jit(solution)/shard_map/all_to_all | solution.py:134
  286.8 2.9 gather_fusion.2
  289.9 0.6 fusion.18
  290.5 0.7 add_convert_fusion
  (72 shorter events, 3.5 us)
Async XLA Ops:
  6.5 4.3 %copy-start.2 = (bf16[2,32,128,128]{3,2,1,0:T(8,128)(2,1)S(1)}, bf16[2,32,128,128]{3,2,1,0:T(8,128)(2,1)}, u32[]{:S(2)}) copy-start(bf16[2,32,128,128]{3,2,1,0:T(8,128)(2,1)} %param.14) | copy-start | bytes 6291460
  6.5 39.5 %all-gather.2.cloned.1.call-start = ((), (), s32[]{:S(2)}) async-start(), calls=%async_computation.5 | async-start | bytes 3538944 | tf_op jit(solution)/shard_map/all_gather | solution.py:80
  13.3 1.2 copy-start.5
  13.3 7.0 %copy-start.3 = (s32[3,8,8]{2,1,0:T(8,128)S(1)}, s32[3,8,8]{2,1,0:T(8,128)}, u32[]{:S(2)}) copy-start(s32[3,8,8]{2,1,0:T(8,128)} %param.19) | copy-start | bytes 2308
  14.5 14.6 %collective-permute-start = (bf16[2048,128]{1,0:T(8,128)(2,1)S(1)}, bf16[2048,128]{1,0:T(8,128)(2,1)S(1)}, u32[]{:S(2)}, u32[]{:S(2)}) collective-permute-start(bf16[2048,128]{1,0:T(8,128)(2,1)S(1)} %copy-done.5), channel_id=1, source_target_pairs={{0,32},{32,64},{64,96},{96,0},{1,33},{33,65},{65,97},{97,1},{2,34}... | collective-permute-start | bytes 1572872 | tf_op jit(solution)/shard_map/ppermute | solution.py:77
  16.6 25.0 %collective-permute-start.1 = (bf16[2048,128]{1,0:T(8,128)(2,1)S(1)}, bf16[2048,128]{1,0:T(8,128)(2,1)S(1)}, u32[]{:S(2)}, u32[]{:S(2)}) collective-permute-start(bf16[2048,128]{1,0:T(8,128)(2,1)S(1)} %copy-done.5), channel_id=1, source_target_pairs={{0,64},{32,96},{64,0},{96,32},{1,65},{33,97},{65,1},{97,33},{2,66}... | collective-permute-start | bytes 1572872 | tf_op jit(solution)/shard_map/ppermute | solution.py:77
  19.1 22.6 %collective-permute-start.2 = (bf16[2048,128]{1,0:T(8,128)(2,1)S(1)}, bf16[2048,128]{1,0:T(8,128)(2,1)S(1)}, u32[]{:S(2)}, u32[]{:S(2)}) collective-permute-start(bf16[2048,128]{1,0:T(8,128)(2,1)S(1)} %copy-done.5), channel_id=1, source_target_pairs={{0,96},{32,0},{64,32},{96,64},{1,97},{33,1},{65,33},{97,65},{2,98}... | collective-permute-start | bytes 1572872 | tf_op jit(solution)/shard_map/ppermute | solution.py:77
  52.6 27.4 %all-to-all-start = ((f32[3,32,8,512]{3,2,0,1:T(8,128)}), f32[3,32,8,512]{3,2,0,1:T(8,128)S(1)}, u32[]{:S(2)}, u32[]{:S(2)}) async-start(f32[3,32,8,512]{3,2,0,1:T(8,128)} %copy.93), calls=%async_computation | async-start | bytes 3145728 | tf_op jit(solution)/shard_map/all_to_all | solution.py:85
  80.0 1.0 copy-start.1
  80.1 1.0 copy-start.4
  83.6 37.8 %all-to-all-start.3 = ((bf16[128,64,128]{2,1,0:T(8,128)(2,1)}), bf16[128,64,128]{2,1,0:T(8,128)(2,1)S(1)}, u32[]{:S(2)}, u32[]{:S(2)}) async-start(bf16[128,64,128]{2,1,0:T(8,128)(2,1)} %bitcast.32), calls=%async_computation.3 | async-start | bytes 4194304 | tf_op jit(solution)/shard_map/all_to_all | solution.py:126
  121.3 57.9 %all-to-all-start.1 = ((bf16[128,128,128]{2,1,0:T(8,128)(2,1)}), bf16[128,128,128]{2,1,0:T(8,128)(2,1)}, u32[]{:S(2)}, u32[]{:S(2)}) async-start(bf16[128,128,128]{2,1,0:T(8,128)(2,1)} %bitcast.122), calls=%async_computation.1 | async-start | bytes 8388608 | tf_op jit(solution)/shard_map/all_to_all | solution.py:126
  128.6 6.2 %copy-start = (bf16[256,4096]{1,0:T(8,128)(2,1)S(1)}, bf16[256,4096]{1,0:T(8,128)(2,1)}, u32[]{:S(2)}) copy-start(bf16[256,4096]{1,0:T(8,128)(2,1)} %reshape.283) | copy-start | bytes 6291460
  179.3 44.3 %all-to-all-start.4 = ((bf16[128,64,128]{2,1,0:T(8,128)(2,1)}), bf16[128,64,128]{2,1,0:T(8,128)(2,1)S(1)}, u32[]{:S(2)}, u32[]{:S(2)}) async-start(bf16[128,64,128]{2,1,0:T(8,128)(2,1)} %reshape.284), calls=%async_computation.4 | async-start | bytes 4194304 | tf_op jit(solution)/shard_map/all_to_all | solution.py:134
  223.5 11.9 %copy-start.6 = (f32[3,8,8]{2,1,0:T(8,128)S(1)}, f32[3,8,8]{2,1,0:T(8,128)}, u32[]{:S(2)}) copy-start(f32[3,8,8]{2,1,0:T(8,128)} %param.20) | copy-start | bytes 2308
  223.5 63.2 %all-to-all-start.2 = ((bf16[128,128,128]{2,1,0:T(8,128)(2,1)}), bf16[128,128,128]{2,1,0:T(8,128)(2,1)}, u32[]{:S(2)}, u32[]{:S(2)}) async-start(bf16[128,128,128]{2,1,0:T(8,128)(2,1)} %reshape.280), calls=%async_computation.2 | async-start | bytes 8388608 | tf_op jit(solution)/shard_map/all_to_all | solution.py:134
Sparse Core Ops, SparseCore 0:
  14.6 31.2 all-gather.1

commit v10 on v9

--- a/solution.py
+++ b/solution.py
@@ -114,14 +114,16 @@
     padded = jnp.concatenate(
         [normed.reshape(steps * row_own, blocks, 128), jnp.zeros((1, blocks, 128), jnp.bfloat16)]
     )
-    source_by_step = source_row.reshape(expert_count, steps, capacity)
-    chunks = ((0, steps - 1), (steps - 1, steps)) if steps > 1 else ((0, steps),)
+    source_by_slot = source_row.reshape(expert_count, slots_per)
+    half = slots_per // 2
+    chunks = ((0, half), (half, slots_per))
     group = ("x", "y", "c", "tp")
+    slot_of = (step_ids * capacity + slot_rank).reshape(-1)
     picked = []
     for first, last in chunks:
-        span = (last - first) * capacity
+        span = last - first
         wire_shape = (expert_count, span * blocks, 128)
-        chunk_rows = source_by_step[:, first:last].reshape(-1)
+        chunk_rows = source_by_slot[:, first:last].reshape(-1)
         outgoing = jnp.take(padded, chunk_rows, axis=0, mode="clip").reshape(wire_shape)
         arrived = lax.all_to_all(outgoing, group, split_axis=0, concat_axis=0, tiled=True)
         flat_rows = arrived.reshape(-1, width)
@@ -135,13 +137,10 @@
             expert_out.reshape(wire_shape), group, split_axis=0, concat_axis=0, tiled=True
         )
         returned = returned.reshape(expert_count * span, blocks, 128)
-        local_slot = (
-            expert_ids[first:last] * span
-            + (step_ids[first:last] - first) * capacity
-            + slot_rank[first:last]
-        ).reshape(-1)
+        local_slot = expert_ids.reshape(-1) * span + jnp.clip(slot_of - first, 0, span - 1)
         picked.append(jnp.take(returned, local_slot, axis=0, mode="clip"))
-    selected = jnp.concatenate(picked).astype(jnp.float32)
+    in_second = (slot_of >= half)[:, None, None]
+    selected = jnp.where(in_second, picked[1], picked[0]).astype(jnp.float32)
     selected = selected * weights.reshape(-1)[:, None, None]
     expert_mix = jnp.sum(selected.reshape(steps, row_own, TOPK, blocks, 128), axis=2)
     expert_mix = expert_mix.reshape(steps, row_own, width)

time: 299 us -> 289 us (0.967)
  waiting for transfers between devices: 151 us -> 142 us
  starting transfers between devices: 37.7 us -> 32.1 us
    all_to_all x2, waiting for transfers between devices: 56.5 us -> 50.3 us  [per_device(): lax.all_to_all(outgoing, group, split_axis=0, concat_axis=0, tiled=True)]
    all_to_all x2, starting transfers between devices: 14.2 us -> 8.64 us  [per_device(): lax.all_to_all(expert_out.reshape(wire_shape), group, split_axis=0, conca...]
  transfers between devices with their start and end apart: 9 -> 9, of which waited for: 7 -> 8; matrix products, arithmetic and copies ran while one was open for 24% -> 25% of each run, Pallas kernels for 0% -> 0%
where the time goes in v10:
time: 289 us; the launch traced here: 288 us
  waiting for transfers between devices  142 us (49%)
  matrix products  49.8 us (17%)
  local copies, waits for them, and re-layouts  43 us (15%)
  starting transfers between devices  32.1 us (11%)
  between operations  13.8 us (5%)
  other arithmetic  7.29 us (3%)
    all_to_all x2, waiting for transfers between devices, per_device(): lax.all_to_all(outgoing, group, split_axis=0, concat_axis=0, tiled=True)  50.3 us
    all_to_all x2, waiting for transfers between devices, per_device(): lax.all_to_all(expert_out.reshape(wire_shape), group, split_axis=0, conca...  47.7 us
    dot_general x2, matrix products, per_device(): jnp.dot(hidden, expert_down[0], preferred_element_type=jnp.float32)  27.5 us
    ppermute x3, waiting for transfers between devices, per_device(): lax.ppermute(w_out, 'x', [(i, (i + k) % x_count) for i in range(x_count)])  20.8 us
    all_to_all x1, waiting for transfers between devices, per_device(): lax.all_to_all(grouped, ('y', 'c', 'tp'), split_axis=1, concat_axis=1, ti...  19.2 us
    dot_general x2, matrix products, per_device(): jnp.dot(flat_rows, expert_gate[0], preferred_element_type=jnp.float32)  14.9 us
    all_to_all x2, starting transfers between devices, per_device(): lax.all_to_all(outgoing, group, split_axis=0, concat_axis=0, tiled=True)  11.8 us
    reshape x2, local copies, waits for them, and re-layouts, per_device(): expert_out.reshape(wire_shape)  11.7 us
  transfers between devices with their start and end apart: 9, of which 8 were waited for; matrix products, arithmetic and copies ran while one was open for 25% of the time, Pallas kernels for 0%

profile of v10, /device:TPU:1, one launch (start us, length us, event | category | flops | bytes accessed | tf_op | source)
XLA Modules:
  0.0 288.3 jit_solution(11158558798281536217)
XLA Ops:
  6.5 1.1 copy.104
  7.6 0.8 fusion.73
  8.4 0.8 fusion.57
  9.5 0.7 iota_compare_fusion.1
  10.2 0.4 copy.87
  10.6 2.3 fusion.74
  13.0 0.6 fusion.43
  13.6 0.5 divide_convert_fusion
  14.1 0.4 fusion.44
  14.8 0.9 reshape.315
  15.8 2.1 collective-permute-start
  17.9 2.5 collective-permute-start.1
  20.3 1.1 collective-permute-start.2
  22.1 8.3 %collective-permute-done = bf16[2048,128]{1,0:T(8,128)(2,1)S(1)} collective-permute-done((bf16[2048,128]{1,0:T(8,128)(2,1)S(1)}, bf16[2048,128]{1,0:T(8,128)(2,1)S(1)}, u32[]{:S(2)}, u32[]{:S(2)}) %collective-permute-start) | collective-permute-done | bytes 524320 | tf_op jit(solution)/shard_map/ppermute | solution.py:77
  30.4 12.5 %collective-permute-done.1 = bf16[2048,128]{1,0:T(8,128)(2,1)S(1)} collective-permute-done((bf16[2048,128]{1,0:T(8,128)(2,1)S(1)}, bf16[2048,128]{1,0:T(8,128)(2,1)S(1)}, u32[]{:S(2)}, u32[]{:S(2)}) %collective-permute-start.1) | collective-permute-done | bytes 524320 | tf_op jit(solution)/shard_map/ppermute | solution.py:77
  42.9 4.3 %all-gather.2.cloned.1.call-done = bf16[3,256,2048]{2,1,0:T(8,128)(2,1)} async-done(((bf16[3,32,2048]{2,1,0:T(8,128)(2,1)}), bf16[3,256,2048]{2,1,0:T(8,128)(2,1)}) %all-gather.2.cloned.1.call-update) | async-done | bytes 3145744 | tf_op jit(solution)/shard_map/all_gather | solution.py:80
  47.2 3.7 %fusion.18 = f32[3,256,4,128]{3,1,2,0:T(8,128)S(1)} fusion(bf16[3,256,2048]{2,1,0:T(8,128)(2,1)} %all-gather.2.cloned.1.call-done, bf16[1,2048,128]{2,1,0:T(8,128)(2,1)S(1)} %bitcast.137, bf16[1,2048,128]{2,1,0:T(8,128)(2,1)S(1)} %bitcast.136, bf16[1,2048,128]{2,1,0:T(8,128)(2,1)S(1)} %bitcast.135, bf16[1,2048,128]{2,1,0:T(8,128)(2,1)S(1)} %bitcast.134), kind=kOutput, calls=%fused_computation.20 | convolution fusion | flops 1619001344 | bytes 6815744 | tf_op jit(solution)/shard_map/srk,jkc->srjc/dot_general | solution.py:81
  50.9 1.0 copy.92
  51.9 0.6 reshape.316
  52.6 1.3 copy.93
  53.9 6.0 %all-to-all-start = ((f32[3,32,8,512]{3,2,0,1:T(8,128)}), f32[3,32,8,512]{3,2,0,1:T(8,128)S(1)}, u32[]{:S(2)}, u32[]{:S(2)}) async-start(f32[3,32,8,512]{3,2,0,1:T(8,128)} %copy.93), calls=%async_computation | async-start | bytes 3145728 | tf_op jit(solution)/shard_map/all_to_all | solution.py:85
  60.4 1.2 scatter_custom_fusion
  62.1 19.2 %all-to-all-done = f32[3,32,8,512]{3,2,0,1:T(8,128)S(1)} async-done(((f32[3,32,8,512]{3,2,0,1:T(8,128)}), f32[3,32,8,512]{3,2,0,1:T(8,128)S(1)}, u32[]{:S(2)}, u32[]{:S(2)}) %all-to-all-start) | async-done | bytes 1572896 | tf_op jit(solution)/shard_map/all_to_all | solution.py:85
  81.4 0.6 gather_fusion
  82.6 3.1 %gather_fusion.3 = bf16[384,32,128]{2,1,0:T(8,128)(2,1)} fusion(bf16[25,32,128]{2,1,0:T(8,128)(2,1)S(1)} %concatenate.7, s32[1024]{0:T(1024)S(1)} %pad_clamp_fusion.1), kind=kCustom, calls=%fused_computation.3 | custom fusion | bytes 6292992 | tf_op jit(solution)/shard_map/jit(_take)/gather | solution.py:127
  85.7 7.0 %all-to-all-start.3 = ((bf16[128,96,128]{2,1,0:T(8,128)(2,1)}), bf16[128,96,128]{2,1,0:T(8,128)(2,1)S(1)}, u32[]{:S(2)}, u32[]{:S(2)}) async-start(bf16[128,96,128]{2,1,0:T(8,128)(2,1)} %bitcast.122), calls=%async_computation.3 | async-start | bytes 6291456 | tf_op jit(solution)/shard_map/all_to_all | solution.py:128
  93.0 3.2 %gather_fusion.1 = bf16[384,32,128]{2,1,0:T(8,128)(2,1)} fusion(bf16[25,32,128]{2,1,0:T(8,128)(2,1)S(1)} %concatenate.7, s32[1024]{0:T(1024)S(1)} %pad_clamp_fusion.3), kind=kCustom, calls=%fused_computation.1 | custom fusion | bytes 6292992 | tf_op jit(solution)/shard_map/jit(_take)/gather | solution.py:127
  96.2 38.5 %all-to-all-done.3 = bf16[128,96,128]{2,1,0:T(8,128)(2,1)S(1)} async-done(((bf16[128,96,128]{2,1,0:T(8,128)(2,1)}), bf16[128,96,128]{2,1,0:T(8,128)(2,1)S(1)}, u32[]{:S(2)}, u32[]{:S(2)}) %all-to-all-start.3) | async-done | bytes 3145760 | tf_op jit(solution)/shard_map/all_to_all | solution.py:128
  134.8 4.8 %all-to-all-start.1 = ((bf16[128,96,128]{2,1,0:T(8,128)(2,1)}), bf16[128,96,128]{2,1,0:T(8,128)(2,1)}, u32[]{:S(2)}, u32[]{:S(2)}) async-start(bf16[128,96,128]{2,1,0:T(8,128)(2,1)} %bitcast.121), calls=%async_computation.1 | async-start | bytes 6291456 | tf_op jit(solution)/shard_map/all_to_all | solution.py:128
  139.6 3.4 %reshape.325 = bf16[384,4096]{1,0:T(8,128)(2,1)} reshape(bf16[128,96,128]{2,1,0:T(8,128)(2,1)S(1)} %all-to-all-done.3) | data formatting | bytes 6291456 | tf_op jit(solution)/shard_map/reshape | solution.py:129
  142.9 7.5 %fusion.8 = f32[384,768]{1,0:T(8,128)} fusion(bf16[384,4096]{1,0:T(8,128)(2,1)} %reshape.325, bf16[1,4096,768]{2,1,0:T(8,128)(2,1)} %param.21), kind=kOutput, calls=%fused_computation.14 | convolution fusion | flops 2415919104 | bytes 10616832 | tf_op jit(solution)/shard_map/dot_general | solution.py:130
  150.5 13.3 %fusion.15 = bf16[384,4096]{1,0:T(8,128)(2,1)} fusion(bf16[1,768,4096]{2,1,0:T(8,128)(2,1)} %param.23, bf16[384,4096]{1,0:T(8,128)(2,1)S(1)} %copy-done.3, bf16[1,4096,768]{2,1,0:T(8,128)(2,1)} %param.22, f32[384,768]{1,0:T(8,128)} %fusion.8), kind=kOutput, calls=%fused_computation.19 | convolution fusion | flops 4835180544 | bytes 20054016 | tf_op jit(solution)/shard_map/dot_general | solution.py:133
  163.8 5.9 %reshape.326 = bf16[128,96,128]{2,1,0:T(8,128)(2,1)} reshape(bf16[384,4096]{1,0:T(8,128)(2,1)} %fusion.15) | data formatting | bytes 6291456 | tf_op jit(solution)/shard_map/reshape | solution.py:137
  169.6 11.8 %all-to-all-done.1 = bf16[128,96,128]{2,1,0:T(8,128)(2,1)} async-done(((bf16[128,96,128]{2,1,0:T(8,128)(2,1)}), bf16[128,96,128]{2,1,0:T(8,128)(2,1)}, u32[]{:S(2)}, u32[]{:S(2)}) %all-to-all-start.1) | async-done | bytes 3145760 | tf_op jit(solution)/shard_map/all_to_all | solution.py:128
  181.4 3.8 %all-to-all-start.4 = ((bf16[128,96,128]{2,1,0:T(8,128)(2,1)}), bf16[128,96,128]{2,1,0:T(8,128)(2,1)S(1)}, u32[]{:S(2)}, u32[]{:S(2)}) async-start(bf16[128,96,128]{2,1,0:T(8,128)(2,1)} %reshape.326), calls=%async_computation.4 | async-start | bytes 6291456 | tf_op jit(solution)/shard_map/all_to_all | solution.py:136
  185.3 5.8 %reshape.321 = bf16[384,4096]{1,0:T(8,128)(2,1)} reshape(bf16[128,96,128]{2,1,0:T(8,128)(2,1)} %all-to-all-done.1) | data formatting | bytes 6291456 | tf_op jit(solution)/shard_map/reshape | solution.py:129
  191.0 7.4 %fusion.10 = f32[384,768]{1,0:T(8,128)} fusion(bf16[384,4096]{1,0:T(8,128)(2,1)} %reshape.321, bf16[1,4096,768]{2,1,0:T(8,128)(2,1)} %param.21), kind=kOutput, calls=%fused_computation.16 | convolution fusion | flops 2415919104 | bytes 10616832 | tf_op jit(solution)/shard_map/dot_general | solution.py:130
  198.4 14.2 %fusion.12 = bf16[384,4096]{1,0:T(8,128)(2,1)} fusion(bf16[1,768,4096]{2,1,0:T(8,128)(2,1)} %param.23, bf16[384,4096]{1,0:T(8,128)(2,1)} %reshape.321, bf16[1,4096,768]{2,1,0:T(8,128)(2,1)} %param.22, f32[384,768]{1,0:T(8,128)} %fusion.10), kind=kOutput, calls=%fused_computation.18 | convolution fusion | flops 4835180544 | bytes 20054016 | tf_op jit(solution)/shard_map/dot_general | solution.py:133
  212.6 5.9 %reshape.322 = bf16[128,96,128]{2,1,0:T(8,128)(2,1)} reshape(bf16[384,4096]{1,0:T(8,128)(2,1)} %fusion.12) | data formatting | bytes 6291456 | tf_op jit(solution)/shard_map/reshape | solution.py:137
  218.5 8.9 %all-to-all-done.4 = bf16[128,96,128]{2,1,0:T(8,128)(2,1)S(1)} async-done(((bf16[128,96,128]{2,1,0:T(8,128)(2,1)}), bf16[128,96,128]{2,1,0:T(8,128)(2,1)S(1)}, u32[]{:S(2)}, u32[]{:S(2)}) %all-to-all-start.4) | async-done | bytes 3145760 | tf_op jit(solution)/shard_map/all_to_all | solution.py:136
  227.4 4.8 %all-to-all-start.2 = ((bf16[128,96,128]{2,1,0:T(8,128)(2,1)}), bf16[128,96,128]{2,1,0:T(8,128)(2,1)}, u32[]{:S(2)}, u32[]{:S(2)}) async-start(bf16[128,96,128]{2,1,0:T(8,128)(2,1)} %reshape.322), calls=%async_computation.2 | async-start | bytes 6291456 | tf_op jit(solution)/shard_map/all_to_all | solution.py:136
  232.3 0.6 pad_clamp_fusion.2
  233.2 2.0 gather_fusion.4
  235.2 38.8 %all-to-all-done.2 = bf16[128,96,128]{2,1,0:T(8,128)(2,1)} async-done(((bf16[128,96,128]{2,1,0:T(8,128)(2,1)}), bf16[128,96,128]{2,1,0:T(8,128)(2,1)}, u32[]{:S(2)}, u32[]{:S(2)}) %all-to-all-start.2) | async-done | bytes 3145760 | tf_op jit(solution)/shard_map/all_to_all | solution.py:136
  274.0 3.0 %gather_fusion.2 = bf16[192,32,128]{2,1,0:T(8,128)(2,1)S(1)} fusion(bf16[384,32,128]{2,1,0:T(8,128)(2,1)} %bitcast.30, s32[1024]{0:T(1024)} %pad_clamp_fusion.2), kind=kCustom, calls=%fused_computation.2 | custom fusion | bytes 3146496 | tf_op jit(solution)/shard_map/jit(_take)/gather | solution.py:141
  277.0 1.7 multiply_reduce_fusion
  278.8 1.1 reshape.328
  279.8 1.7 add_convert_fusion
  (68 shorter events, 3.5 us)
Async XLA Ops:
  6.5 40.7 %all-gather.2.cloned.1.call-start = ((), (), s32[]{:S(2)}) async-start(), calls=%async_computation.5 | async-start | bytes 3538944 | tf_op jit(solution)/shard_map/all_gather | solution.py:80
  10.6 3.5 %copy-start.5 = (bf16[2,32,128,128]{3,2,1,0:T(8,128)(2,1)S(1)}, bf16[2,32,128,128]{3,2,1,0:T(8,128)(2,1)}, u32[]{:S(2)}) copy-start(bf16[2,32,128,128]{3,2,1,0:T(8,128)(2,1)} %param.14) | copy-start | bytes 6291460
  14.1 1.7 copy-start.8
  14.1 7.4 %copy-start.6 = (s32[3,8,8]{2,1,0:T(8,128)S(1)}, s32[3,8,8]{2,1,0:T(8,128)}, u32[]{:S(2)}) copy-start(s32[3,8,8]{2,1,0:T(8,128)} %param.19) | copy-start | bytes 2308
  15.8 14.6 %collective-permute-start = (bf16[2048,128]{1,0:T(8,128)(2,1)S(1)}, bf16[2048,128]{1,0:T(8,128)(2,1)S(1)}, u32[]{:S(2)}, u32[]{:S(2)}) collective-permute-start(bf16[2048,128]{1,0:T(8,128)(2,1)S(1)} %copy-done.8), channel_id=1, source_target_pairs={{0,32},{32,64},{64,96},{96,0},{1,33},{33,65},{65,97},{97,1},{2,34}... | collective-permute-start | bytes 1572872 | tf_op jit(solution)/shard_map/ppermute | solution.py:77
  17.9 25.0 %collective-permute-start.1 = (bf16[2048,128]{1,0:T(8,128)(2,1)S(1)}, bf16[2048,128]{1,0:T(8,128)(2,1)S(1)}, u32[]{:S(2)}, u32[]{:S(2)}) collective-permute-start(bf16[2048,128]{1,0:T(8,128)(2,1)S(1)} %copy-done.8), channel_id=1, source_target_pairs={{0,64},{32,96},{64,0},{96,32},{1,65},{33,97},{65,1},{97,33},{2,66}... | collective-permute-start | bytes 1572872 | tf_op jit(solution)/shard_map/ppermute | solution.py:77
  20.3 22.6 %collective-permute-start.2 = (bf16[2048,128]{1,0:T(8,128)(2,1)S(1)}, bf16[2048,128]{1,0:T(8,128)(2,1)S(1)}, u32[]{:S(2)}, u32[]{:S(2)}) collective-permute-start(bf16[2048,128]{1,0:T(8,128)(2,1)S(1)} %copy-done.8), channel_id=1, source_target_pairs={{0,96},{32,0},{64,32},{96,64},{1,97},{33,1},{65,33},{97,65},{2,98}... | collective-permute-start | bytes 1572872 | tf_op jit(solution)/shard_map/ppermute | solution.py:77
  53.9 27.4 %all-to-all-start = ((f32[3,32,8,512]{3,2,0,1:T(8,128)}), f32[3,32,8,512]{3,2,0,1:T(8,128)S(1)}, u32[]{:S(2)}, u32[]{:S(2)}) async-start(f32[3,32,8,512]{3,2,0,1:T(8,128)} %copy.93), calls=%async_computation | async-start | bytes 3145728 | tf_op jit(solution)/shard_map/all_to_all | solution.py:85
  59.8 22.4 %copy-start.4 = (bf16[3,8,4096]{2,1,0:T(8,128)(2,1)S(1)}, bf16[3,8,4096]{2,1,0:T(8,128)(2,1)}, u32[]{:S(2)}) copy-start(bf16[3,8,4096]{2,1,0:T(8,128)(2,1)} %param.16) | copy-start | bytes 589828
  59.8 22.6 %copy-start.7 = (f32[4096]{0:T(1024)S(1)}, f32[4096]{0:T(1024)}, u32[]{:S(2)}) copy-start(f32[4096]{0:T(1024)} %param.17) | copy-start | bytes 49156
  82.2 3.5 %copy-start.1 = (f32[3,8,4096]{2,1,0:T(8,128)}, f32[3,8,4096]{2,1,0:T(8,128)S(1)}, u32[]{:S(2)}) copy-start(f32[3,8,4096]{2,1,0:T(8,128)S(1)} %reshape.329) | copy-start | bytes 1179652
  85.7 49.0 %all-to-all-start.3 = ((bf16[128,96,128]{2,1,0:T(8,128)(2,1)}), bf16[128,96,128]{2,1,0:T(8,128)(2,1)S(1)}, u32[]{:S(2)}, u32[]{:S(2)}) async-start(bf16[128,96,128]{2,1,0:T(8,128)(2,1)} %bitcast.122), calls=%async_computation.3 | async-start | bytes 6291456 | tf_op jit(solution)/shard_map/all_to_all | solution.py:128
  134.8 46.7 %all-to-all-start.1 = ((bf16[128,96,128]{2,1,0:T(8,128)(2,1)}), bf16[128,96,128]{2,1,0:T(8,128)(2,1)}, u32[]{:S(2)}, u32[]{:S(2)}) async-start(bf16[128,96,128]{2,1,0:T(8,128)(2,1)} %bitcast.121), calls=%async_computation.1 | async-start | bytes 6291456 | tf_op jit(solution)/shard_map/all_to_all | solution.py:128
  142.9 7.5 %copy-start.3 = (bf16[384,4096]{1,0:T(8,128)(2,1)S(1)}, bf16[384,4096]{1,0:T(8,128)(2,1)}, u32[]{:S(2)}) copy-start(bf16[384,4096]{1,0:T(8,128)(2,1)} %reshape.325) | copy-start | bytes 9437188
  181.4 46.0 %all-to-all-start.4 = ((bf16[128,96,128]{2,1,0:T(8,128)(2,1)}), bf16[128,96,128]{2,1,0:T(8,128)(2,1)S(1)}, u32[]{:S(2)}, u32[]{:S(2)}) async-start(bf16[128,96,128]{2,1,0:T(8,128)(2,1)} %reshape.326), calls=%async_computation.4 | async-start | bytes 6291456 | tf_op jit(solution)/shard_map/all_to_all | solution.py:136
  218.5 14.5 %copy-start.9 = (f32[3,8,8]{2,1,0:T(8,128)S(1)}, f32[3,8,8]{2,1,0:T(8,128)}, u32[]{:S(2)}) copy-start(f32[3,8,8]{2,1,0:T(8,128)} %param.20) | copy-start | bytes 2308
  227.4 46.7 %all-to-all-start.2 = ((bf16[128,96,128]{2,1,0:T(8,128)(2,1)}), bf16[128,96,128]{2,1,0:T(8,128)(2,1)}, u32[]{:S(2)}, u32[]{:S(2)}) async-start(bf16[128,96,128]{2,1,0:T(8,128)(2,1)} %reshape.322), calls=%async_computation.2 | async-start | bytes 6291456 | tf_op jit(solution)/shard_map/all_to_all | solution.py:136
  235.2 41.8 %copy-start = (bf16[192,32,128]{2,1,0:T(8,128)(2,1)S(1)}, bf16[192,32,128]{2,1,0:T(8,128)(2,1)}, u32[]{:S(2)}) copy-start(bf16[192,32,128]{2,1,0:T(8,128)(2,1)} %gather_fusion.4) | copy-start | bytes 4718596
  274.0 5.8 %copy-start.2 = (f32[3,8,4096]{2,1,0:T(8,128)S(1)}, f32[3,8,4096]{2,1,0:T(8,128)}, u32[]{:S(2)}) copy-start(f32[3,8,4096]{2,1,0:T(8,128)} %copy-done.1) | copy-start | bytes 1179652
Sparse Core Ops, SparseCore 0:
  15.9 31.2 all-gather.1

commit v11 on v10

--- a/solution.py
+++ b/solution.py
@@ -45,30 +45,30 @@
     usable = jnp.arange(cache_len, dtype=jnp.int32)[None, :] < lengths[:, None]
 
     query_rows = query.reshape(steps, row_dev, heads_dev, HEAD_SIZE)
-    incoming_keys = step_key_value[:, 0]
-    incoming_values = step_key_value[:, 1]
-    cache_scores = (
-        jnp.einsum("srhd,rjd->srhj", query_rows, stored_keys, preferred_element_type=jnp.float32)
-        * score_scale
+    all_keys = jnp.concatenate([stored_keys, jnp.transpose(step_key_value[:, 0], (1, 0, 2))], axis=1)
+    all_values = jnp.concatenate(
+        [stored_values, jnp.transpose(step_key_value[:, 1], (1, 0, 2))], axis=1
     )
-    cache_scores = jnp.where(usable[None, :, None, :], cache_scores, masked_score)
-    fresh_scores = (
-        jnp.einsum("srhd,jrd->srhj", query_rows, incoming_keys, preferred_element_type=jnp.float32)
+    scores = (
+        jnp.einsum("srhd,rjd->srhj", query_rows, all_keys, preferred_element_type=jnp.float32)
         * score_scale
     )
     fresh_ok = (
         jnp.arange(steps, dtype=jnp.int32)[None, :] <= jnp.arange(steps, dtype=jnp.int32)[:, None]
     )
-    fresh_scores = jnp.where(fresh_ok[:, None, None, :], fresh_scores, masked_score)
-    scores = jnp.concatenate([cache_scores, fresh_scores], axis=-1)
+    allowed = jnp.concatenate(
+        [
+            jnp.broadcast_to(usable[None], (steps, row_dev, cache_len)),
+            jnp.broadcast_to(fresh_ok[:, None, :], (steps, row_dev, steps)),
+        ],
+        axis=-1,
+    )
+    scores = jnp.where(allowed[:, :, None, :], scores, masked_score)
     top = jnp.max(scores, axis=-1, keepdims=True)
     raised = jnp.exp(scores - top)
     probs = (raised / jnp.sum(raised, axis=-1, keepdims=True)).astype(jnp.bfloat16)
     attended = jnp.einsum(
-        "srhj,rjd->srhd", probs[..., :cache_len], stored_values, preferred_element_type=jnp.float32
-    )
-    attended = attended + jnp.einsum(
-        "srhj,jrd->srhd", probs[..., cache_len:], incoming_values, preferred_element_type=jnp.float32
+        "srhj,rjd->srhd", probs, all_values, preferred_element_type=jnp.float32
     )
     attended = attended.astype(jnp.bfloat16).reshape(steps, row_dev, heads_dev * HEAD_SIZE)
 

time: 289 us -> 288 us (level)
  no operation moved by 1% of the time
where the time goes in v11:
time: 288 us; the launch traced here: 287 us
  waiting for transfers between devices  142 us (49%)
  matrix products  50.2 us (17%)
  local copies, waits for them, and re-layouts  43.1 us (15%)
  starting transfers between devices  32.2 us (11%)
  between operations  13.8 us (5%)
  other arithmetic  5.46 us (2%)
    all_to_all x2, waiting for transfers between devices, per_device(): lax.all_to_all(outgoing, group, split_axis=0, concat_axis=0, tiled=True)  50.3 us
    all_to_all x2, waiting for transfers between devices, per_device(): lax.all_to_all(expert_out.reshape(wire_shape), group, split_axis=0, conca...  47.6 us
    dot_general x2, matrix products, per_device(): jnp.dot(hidden, expert_down[0], preferred_element_type=jnp.float32)  27.5 us
    ppermute x3, waiting for transfers between devices, per_device(): lax.ppermute(w_out, 'x', [(i, (i + k) % x_count) for i in range(x_count)])  20.8 us
    all_to_all x1, waiting for transfers between devices, per_device(): lax.all_to_all(grouped, ('y', 'c', 'tp'), split_axis=1, concat_axis=1, ti...  19.2 us
    dot_general x2, matrix products, per_device(): jnp.dot(flat_rows, expert_gate[0], preferred_element_type=jnp.float32)  14.9 us
    all_to_all x2, starting transfers between devices, per_device(): lax.all_to_all(outgoing, group, split_axis=0, concat_axis=0, tiled=True)  11.9 us
    reshape x2, local copies, waits for them, and re-layouts, per_device(): expert_out.reshape(wire_shape)  11.7 us
  transfers between devices with their start and end apart: 9, of which 8 were waited for; matrix products, arithmetic and copies ran while one was open for 25% of the time, Pallas kernels for 0%

profile of v11, /device:TPU:1, one launch (start us, length us, event | category | flops | bytes accessed | tf_op | source)
XLA Modules:
  0.0 287.0 jit_solution(15540248975061048900)
XLA Ops:
  6.5 0.8 fusion.76
  7.4 1.7 slice_bitcast_fusion
  9.4 2.1 fusion.77
  11.5 2.0 fusion.41
  13.5 0.9 reshape.312
  14.5 2.1 collective-permute-start
  16.6 2.5 collective-permute-start.1
  19.0 1.2 collective-permute-start.2
  20.5 0.2 select_reduce_fusion
  20.8 8.3 %collective-permute-done = bf16[2048,128]{1,0:T(8,128)(2,1)S(1)} collective-permute-done((bf16[2048,128]{1,0:T(8,128)(2,1)S(1)}, bf16[2048,128]{1,0:T(8,128)(2,1)S(1)}, u32[]{:S(2)}, u32[]{:S(2)}) %collective-permute-start) | collective-permute-done | bytes 524320 | tf_op jit(solution)/shard_map/ppermute | solution.py:77
  29.1 12.5 %collective-permute-done.1 = bf16[2048,128]{1,0:T(8,128)(2,1)S(1)} collective-permute-done((bf16[2048,128]{1,0:T(8,128)(2,1)S(1)}, bf16[2048,128]{1,0:T(8,128)(2,1)S(1)}, u32[]{:S(2)}, u32[]{:S(2)}) %collective-permute-start.1) | collective-permute-done | bytes 524320 | tf_op jit(solution)/shard_map/ppermute | solution.py:77
  41.6 4.3 %all-gather.2.cloned.1.call-done = bf16[3,256,2048]{2,1,0:T(8,128)(2,1)} async-done(((bf16[3,32,2048]{2,1,0:T(8,128)(2,1)}), bf16[3,256,2048]{2,1,0:T(8,128)(2,1)}) %all-gather.2.cloned.1.call-update) | async-done | bytes 3145744 | tf_op jit(solution)/shard_map/all_gather | solution.py:80
  45.9 3.7 %fusion.19 = f32[3,256,4,128]{3,1,2,0:T(8,128)S(1)} fusion(bf16[3,256,2048]{2,1,0:T(8,128)(2,1)} %all-gather.2.cloned.1.call-done, bf16[1,2048,128]{2,1,0:T(8,128)(2,1)S(1)} %bitcast.137, bf16[1,2048,128]{2,1,0:T(8,128)(2,1)S(1)} %bitcast.136, bf16[1,2048,128]{2,1,0:T(8,128)(2,1)S(1)} %bitcast.135, bf16[1,2048,128]{2,1,0:T(8,128)(2,1)S(1)} %bitcast.134), kind=kOutput, calls=%fused_computation.21 | convolution fusion | flops 1619001344 | bytes 6815744 | tf_op jit(solution)/shard_map/srk,jkc->srjc/dot_general | solution.py:81
  49.6 1.0 copy.39
  50.6 0.6 reshape.313
  51.3 1.3 copy.40
  52.5 6.0 %all-to-all-start = ((f32[3,32,8,512]{3,2,0,1:T(8,128)}), f32[3,32,8,512]{3,2,0,1:T(8,128)S(1)}, u32[]{:S(2)}, u32[]{:S(2)}) async-start(f32[3,32,8,512]{3,2,0,1:T(8,128)} %copy.40), calls=%async_computation | async-start | bytes 3145728 | tf_op jit(solution)/shard_map/all_to_all | solution.py:85
  59.0 1.2 scatter_custom_fusion
  60.5 0.2 reshape.353
  60.7 19.2 %all-to-all-done = f32[3,32,8,512]{3,2,0,1:T(8,128)S(1)} async-done(((f32[3,32,8,512]{3,2,0,1:T(8,128)}), f32[3,32,8,512]{3,2,0,1:T(8,128)S(1)}, u32[]{:S(2)}, u32[]{:S(2)}) %all-to-all-start) | async-done | bytes 1572896 | tf_op jit(solution)/shard_map/all_to_all | solution.py:85
  79.9 0.2 reduce_sum.59
  80.1 0.6 gather_fusion
  81.3 3.1 %gather_fusion.3 = bf16[384,32,128]{2,1,0:T(8,128)(2,1)} fusion(bf16[25,32,128]{2,1,0:T(8,128)(2,1)S(1)} %concatenate.15, s32[1024]{0:T(1024)S(1)} %pad_clamp_fusion.1), kind=kCustom, calls=%fused_computation.3 | custom fusion | bytes 6292992 | tf_op jit(solution)/shard_map/jit(_take)/gather | solution.py:127
  84.4 7.0 %all-to-all-start.3 = ((bf16[128,96,128]{2,1,0:T(8,128)(2,1)}), bf16[128,96,128]{2,1,0:T(8,128)(2,1)S(1)}, u32[]{:S(2)}, u32[]{:S(2)}) async-start(bf16[128,96,128]{2,1,0:T(8,128)(2,1)} %bitcast.123), calls=%async_computation.3 | async-start | bytes 6291456 | tf_op jit(solution)/shard_map/all_to_all | solution.py:128
  91.5 0.2 reshape.337
  91.7 3.2 %gather_fusion.1 = bf16[384,32,128]{2,1,0:T(8,128)(2,1)} fusion(bf16[25,32,128]{2,1,0:T(8,128)(2,1)S(1)} %concatenate.15, s32[1024]{0:T(1024)S(1)} %pad_clamp_fusion.3), kind=kCustom, calls=%fused_computation.1 | custom fusion | bytes 6292992 | tf_op jit(solution)/shard_map/jit(_take)/gather | solution.py:127
  94.9 38.6 %all-to-all-done.3 = bf16[128,96,128]{2,1,0:T(8,128)(2,1)S(1)} async-done(((bf16[128,96,128]{2,1,0:T(8,128)(2,1)}), bf16[128,96,128]{2,1,0:T(8,128)(2,1)S(1)}, u32[]{:S(2)}, u32[]{:S(2)}) %all-to-all-start.3) | async-done | bytes 3145760 | tf_op jit(solution)/shard_map/all_to_all | solution.py:128
  133.5 4.9 %all-to-all-start.1 = ((bf16[128,96,128]{2,1,0:T(8,128)(2,1)}), bf16[128,96,128]{2,1,0:T(8,128)(2,1)}, u32[]{:S(2)}, u32[]{:S(2)}) async-start(bf16[128,96,128]{2,1,0:T(8,128)(2,1)} %bitcast.122), calls=%async_computation.1 | async-start | bytes 6291456 | tf_op jit(solution)/shard_map/all_to_all | solution.py:128
  138.3 3.4 %reshape.322 = bf16[384,4096]{1,0:T(8,128)(2,1)} reshape(bf16[128,96,128]{2,1,0:T(8,128)(2,1)S(1)} %all-to-all-done.3) | data formatting | bytes 6291456 | tf_op jit(solution)/shard_map/reshape | solution.py:129
  141.7 7.5 %fusion.9 = f32[384,768]{1,0:T(8,128)} fusion(bf16[384,4096]{1,0:T(8,128)(2,1)} %reshape.322, bf16[1,4096,768]{2,1,0:T(8,128)(2,1)} %param.21), kind=kOutput, calls=%fused_computation.15 | convolution fusion | flops 2415919104 | bytes 10616832 | tf_op jit(solution)/shard_map/dot_general | solution.py:130
  149.2 13.3 %fusion.16 = bf16[384,4096]{1,0:T(8,128)(2,1)} fusion(bf16[1,768,4096]{2,1,0:T(8,128)(2,1)} %param.23, bf16[384,4096]{1,0:T(8,128)(2,1)S(1)} %copy-done.3, bf16[1,4096,768]{2,1,0:T(8,128)(2,1)} %param.22, f32[384,768]{1,0:T(8,128)} %fusion.9), kind=kOutput, calls=%fused_computation.20 | convolution fusion | flops 4835180544 | bytes 20054016 | tf_op jit(solution)/shard_map/dot_general | solution.py:133
  162.5 5.9 %reshape.323 = bf16[128,96,128]{2,1,0:T(8,128)(2,1)} reshape(bf16[384,4096]{1,0:T(8,128)(2,1)} %fusion.16) | data formatting | bytes 6291456 | tf_op jit(solution)/shard_map/reshape | solution.py:137
  168.4 11.7 %all-to-all-done.1 = bf16[128,96,128]{2,1,0:T(8,128)(2,1)} async-done(((bf16[128,96,128]{2,1,0:T(8,128)(2,1)}), bf16[128,96,128]{2,1,0:T(8,128)(2,1)}, u32[]{:S(2)}, u32[]{:S(2)}) %all-to-all-start.1) | async-done | bytes 3145760 | tf_op jit(solution)/shard_map/all_to_all | solution.py:128
  180.1 3.8 %all-to-all-start.4 = ((bf16[128,96,128]{2,1,0:T(8,128)(2,1)}), bf16[128,96,128]{2,1,0:T(8,128)(2,1)S(1)}, u32[]{:S(2)}, u32[]{:S(2)}) async-start(bf16[128,96,128]{2,1,0:T(8,128)(2,1)} %reshape.323), calls=%async_computation.4 | async-start | bytes 6291456 | tf_op jit(solution)/shard_map/all_to_all | solution.py:136
  184.0 5.8 %reshape.318 = bf16[384,4096]{1,0:T(8,128)(2,1)} reshape(bf16[128,96,128]{2,1,0:T(8,128)(2,1)} %all-to-all-done.1) | data formatting | bytes 6291456 | tf_op jit(solution)/shard_map/reshape | solution.py:129
  189.8 7.4 %fusion.11 = f32[384,768]{1,0:T(8,128)} fusion(bf16[384,4096]{1,0:T(8,128)(2,1)} %reshape.318, bf16[1,4096,768]{2,1,0:T(8,128)(2,1)} %param.21), kind=kOutput, calls=%fused_computation.17 | convolution fusion | flops 2415919104 | bytes 10616832 | tf_op jit(solution)/shard_map/dot_general | solution.py:130
  197.2 14.2 %fusion.13 = bf16[384,4096]{1,0:T(8,128)(2,1)} fusion(bf16[1,768,4096]{2,1,0:T(8,128)(2,1)} %param.23, bf16[384,4096]{1,0:T(8,128)(2,1)} %reshape.318, bf16[1,4096,768]{2,1,0:T(8,128)(2,1)} %param.22, f32[384,768]{1,0:T(8,128)} %fusion.11), kind=kOutput, calls=%fused_computation.19 | convolution fusion | flops 4835180544 | bytes 20054016 | tf_op jit(solution)/shard_map/dot_general | solution.py:133
  211.4 5.9 %reshape.319 = bf16[128,96,128]{2,1,0:T(8,128)(2,1)} reshape(bf16[384,4096]{1,0:T(8,128)(2,1)} %fusion.13) | data formatting | bytes 6291456 | tf_op jit(solution)/shard_map/reshape | solution.py:137
  217.3 8.8 %all-to-all-done.4 = bf16[128,96,128]{2,1,0:T(8,128)(2,1)S(1)} async-done(((bf16[128,96,128]{2,1,0:T(8,128)(2,1)}), bf16[128,96,128]{2,1,0:T(8,128)(2,1)S(1)}, u32[]{:S(2)}, u32[]{:S(2)}) %all-to-all-start.4) | async-done | bytes 3145760 | tf_op jit(solution)/shard_map/all_to_all | solution.py:136
  226.1 4.8 %all-to-all-start.2 = ((bf16[128,96,128]{2,1,0:T(8,128)(2,1)}), bf16[128,96,128]{2,1,0:T(8,128)(2,1)}, u32[]{:S(2)}, u32[]{:S(2)}) async-start(bf16[128,96,128]{2,1,0:T(8,128)(2,1)} %reshape.319), calls=%async_computation.2 | async-start | bytes 6291456 | tf_op jit(solution)/shard_map/all_to_all | solution.py:136
  231.0 0.6 pad_clamp_fusion.2
  231.7 0.2 fusion.58
  231.9 2.0 gather_fusion.4
  233.9 38.8 %all-to-all-done.2 = bf16[128,96,128]{2,1,0:T(8,128)(2,1)} async-done(((bf16[128,96,128]{2,1,0:T(8,128)(2,1)}), bf16[128,96,128]{2,1,0:T(8,128)(2,1)}, u32[]{:S(2)}, u32[]{:S(2)}) %all-to-all-start.2) | async-done | bytes 3145760 | tf_op jit(solution)/shard_map/all_to_all | solution.py:136
  272.8 2.9 %gather_fusion.2 = bf16[192,32,128]{2,1,0:T(8,128)(2,1)S(1)} fusion(bf16[384,32,128]{2,1,0:T(8,128)(2,1)} %bitcast.27, s32[1024]{0:T(1024)} %pad_clamp_fusion.2), kind=kCustom, calls=%fused_computation.2 | custom fusion | bytes 3146496 | tf_op jit(solution)/shard_map/jit(_take)/gather | solution.py:141
  275.7 1.7 multiply_reduce_fusion
  277.4 1.1 reshape.325
  278.5 1.7 add_convert_fusion
  (66 shorter events, 2.1 us)
Async XLA Ops:
  6.5 2.5 copy-start.5
  6.5 39.4 %all-gather.2.cloned.1.call-start = ((), (), s32[]{:S(2)}) async-start(), calls=%async_computation.5 | async-start | bytes 3538944 | tf_op jit(solution)/shard_map/all_gather | solution.py:80
  7.4 1.8 copy-start.8
  11.5 3.0 %copy-start.9 = (bf16[2048,128]{1,0:T(8,128)(2,1)S(1)}, bf16[2048,128]{1,0:T(8,128)(2,1)}, u32[]{:S(2)}) copy-start(bf16[2048,128]{1,0:T(8,128)(2,1)} %param.18) | copy-start | bytes 1572868
  11.5 8.7 %copy-start.6 = (s32[3,8,8]{2,1,0:T(8,128)S(1)}, s32[3,8,8]{2,1,0:T(8,128)}, u32[]{:S(2)}) copy-start(s32[3,8,8]{2,1,0:T(8,128)} %param.19) | copy-start | bytes 2308
  14.5 14.6 %collective-permute-start = (bf16[2048,128]{1,0:T(8,128)(2,1)S(1)}, bf16[2048,128]{1,0:T(8,128)(2,1)S(1)}, u32[]{:S(2)}, u32[]{:S(2)}) collective-permute-start(bf16[2048,128]{1,0:T(8,128)(2,1)S(1)} %copy-done.9), channel_id=1, source_target_pairs={{0,32},{32,64},{64,96},{96,0},{1,33},{33,65},{65,97},{97,1},{2,34}... | collective-permute-start | bytes 1572872 | tf_op jit(solution)/shard_map/ppermute | solution.py:77
  16.6 25.0 %collective-permute-start.1 = (bf16[2048,128]{1,0:T(8,128)(2,1)S(1)}, bf16[2048,128]{1,0:T(8,128)(2,1)S(1)}, u32[]{:S(2)}, u32[]{:S(2)}) collective-permute-start(bf16[2048,128]{1,0:T(8,128)(2,1)S(1)} %copy-done.9), channel_id=1, source_target_pairs={{0,64},{32,96},{64,0},{96,32},{1,65},{33,97},{65,1},{97,33},{2,66}... | collective-permute-start | bytes 1572872 | tf_op jit(solution)/shard_map/ppermute | solution.py:77
  19.0 22.6 %collective-permute-start.2 = (bf16[2048,128]{1,0:T(8,128)(2,1)S(1)}, bf16[2048,128]{1,0:T(8,128)(2,1)S(1)}, u32[]{:S(2)}, u32[]{:S(2)}) collective-permute-start(bf16[2048,128]{1,0:T(8,128)(2,1)S(1)} %copy-done.9), channel_id=1, source_target_pairs={{0,96},{32,0},{64,32},{96,64},{1,97},{33,1},{65,33},{97,65},{2,98}... | collective-permute-start | bytes 1572872 | tf_op jit(solution)/shard_map/ppermute | solution.py:77
  52.5 27.4 %all-to-all-start = ((f32[3,32,8,512]{3,2,0,1:T(8,128)}), f32[3,32,8,512]{3,2,0,1:T(8,128)S(1)}, u32[]{:S(2)}, u32[]{:S(2)}) async-start(f32[3,32,8,512]{3,2,0,1:T(8,128)} %copy.40), calls=%async_computation | async-start | bytes 3145728 | tf_op jit(solution)/shard_map/all_to_all | solution.py:85
  79.9 1.0 copy-start.4
  79.9 1.2 copy-start.7
  80.9 3.5 %copy-start.1 = (f32[3,8,4096]{2,1,0:T(8,128)}, f32[3,8,4096]{2,1,0:T(8,128)S(1)}, u32[]{:S(2)}) copy-start(f32[3,8,4096]{2,1,0:T(8,128)S(1)} %reshape.326) | copy-start | bytes 1179652
  84.4 49.0 %all-to-all-start.3 = ((bf16[128,96,128]{2,1,0:T(8,128)(2,1)}), bf16[128,96,128]{2,1,0:T(8,128)(2,1)S(1)}, u32[]{:S(2)}, u32[]{:S(2)}) async-start(bf16[128,96,128]{2,1,0:T(8,128)(2,1)} %bitcast.123), calls=%async_computation.3 | async-start | bytes 6291456 | tf_op jit(solution)/shard_map/all_to_all | solution.py:128
  133.5 46.7 %all-to-all-start.1 = ((bf16[128,96,128]{2,1,0:T(8,128)(2,1)}), bf16[128,96,128]{2,1,0:T(8,128)(2,1)}, u32[]{:S(2)}, u32[]{:S(2)}) async-start(bf16[128,96,128]{2,1,0:T(8,128)(2,1)} %bitcast.122), calls=%async_computation.1 | async-start | bytes 6291456 | tf_op jit(solution)/shard_map/all_to_all | solution.py:128
  141.7 7.5 %copy-start.3 = (bf16[384,4096]{1,0:T(8,128)(2,1)S(1)}, bf16[384,4096]{1,0:T(8,128)(2,1)}, u32[]{:S(2)}) copy-start(bf16[384,4096]{1,0:T(8,128)(2,1)} %reshape.322) | copy-start | bytes 9437188
  180.1 46.0 %all-to-all-start.4 = ((bf16[128,96,128]{2,1,0:T(8,128)(2,1)}), bf16[128,96,128]{2,1,0:T(8,128)(2,1)S(1)}, u32[]{:S(2)}, u32[]{:S(2)}) async-start(bf16[128,96,128]{2,1,0:T(8,128)(2,1)} %reshape.323), calls=%async_computation.4 | async-start | bytes 6291456 | tf_op jit(solution)/shard_map/all_to_all | solution.py:136
  217.3 14.4 %copy-start.10 = (f32[3,8,8]{2,1,0:T(8,128)S(1)}, f32[3,8,8]{2,1,0:T(8,128)}, u32[]{:S(2)}) copy-start(f32[3,8,8]{2,1,0:T(8,128)} %param.20) | copy-start | bytes 2308
  226.1 46.7 %all-to-all-start.2 = ((bf16[128,96,128]{2,1,0:T(8,128)(2,1)}), bf16[128,96,128]{2,1,0:T(8,128)(2,1)}, u32[]{:S(2)}, u32[]{:S(2)}) async-start(bf16[128,96,128]{2,1,0:T(8,128)(2,1)} %reshape.319), calls=%async_computation.2 | async-start | bytes 6291456 | tf_op jit(solution)/shard_map/all_to_all | solution.py:136
  233.9 41.8 %copy-start = (bf16[192,32,128]{2,1,0:T(8,128)(2,1)S(1)}, bf16[192,32,128]{2,1,0:T(8,128)(2,1)}, u32[]{:S(2)}) copy-start(bf16[192,32,128]{2,1,0:T(8,128)(2,1)} %gather_fusion.4) | copy-start | bytes 4718596
  275.7 2.8 copy-start.2
Sparse Core Ops, SparseCore 0:
  14.6 31.2 all-gather.1
